TPU v7x, 128 devices: a whole 4x4x4 slice. The times are simulated.
128 devices in a mesh: seq: 32 (over z, x, y_lo), tp: 4 (over y_hi, core).
Axes of the slice: x: 4, y: 4 (y_hi: 2, y_lo: 2; y = y_hi * 2 + y_lo), z: 4, core: 2. Of those that a mesh axis runs over, the one named last changes fastest.
Arguments:
- tokens: bfloat16 [16384, 1536], P('seq'), may hold values from -6 to 6
- segment_ids: int32 [16384], P('seq'), may hold values from 0 to 511, never falling along the last dimension, each value on 1 to 4096 neighbouring positions
- attn_gain: float32 [1536], replicated, may hold values from 0.25 to 1.75
- w_query: bfloat16 [1536, 1536], P(None, 'tp'), as said below
- w_kv: bfloat16 [1536, 512], replicated, as said below
- w_out: bfloat16 [1536, 1536], P('tp'), may hold values from -0.15625 to 0.15625
- ffn_gain: float32 [1536], replicated, may hold values from 0.25 to 1.75
- w_gate: bfloat16 [32, 1536, 768], P('seq', None, 'tp'), may hold values from -0.15625 to 0.15625
- w_up: bfloat16 [32, 1536, 768], P('seq', None, 'tp'), may hold values from -0.15625 to 0.15625
- w_down: bfloat16 [32, 768, 1536], P('seq', 'tp'), may hold values from -0.21875 to 0.21875
- expert_picks: int32 [16384, 4], P('seq'), may hold values from 0 to 31, all different within a row; in each aligned block of 512 rows (0 to 511, 512 to 1023, ...) at most 80 rows name the same one
- gate_weights: float32 [16384, 4], P('seq'), may hold values from 0.05 to 1
- page_table: int32 [128], P('seq'), may hold values from 0 to 127, as said below
Outputs:
- layer_out: bfloat16 [16384, 1536], P('seq', 'tp')
- kv_pages: bfloat16 [128, 128, 512], P('seq', None, 'tp')
Inputs may be any that keep to these rules, and one draw needn't show every extreme that they name: `segment_ids`: never falls along the pack; each prompt has 1 to 4096 tokens and one has exactly 4096. `expert_picks`: each row names 4 different experts; among the 512 rows of one index of seq no expert is named more than 80 times, a bound that some block reaches. `page_table`: the 4 entries of one index of seq are a permutation of that index's own physical pages, its index times 4 up to 4 more. `w_query`: A projection matrix. `w_kv`: A projection matrix.
All inputs are finite; a program needn't handle non-finite values.
Results may differ from a plain program's by a relative error of at most 0.014.
Values may be sent and summed in bfloat16 or wider, within the bound.
No kernel may reach another device: no remote copies, remote signals or barrier semaphores. Data moves between devices by JAX's collectives and lax.ppermute only.
A program may use at most 128 MiB of HBM per device.

v0:
```python
import jax
import jax.numpy as jnp
from jax import lax
from jax.sharding import PartitionSpec as P

HQ = 12
HK = 2
HD = 128


EPSILON = 1e-06
NEGATIVE = -1e30


def shifted(value, axis, steps):
    count = lax.axis_size(axis)
    leading, last = (max(0, -steps), min(count, count - steps))
    return lax.ppermute(value, axis, [(source, source + steps) for source in range(leading, last)])


def row_norm(values, gain):
    values = values.astype(jnp.float32)
    factor = lax.rsqrt(jnp.mean(values * values, axis=-1, keepdims=True) + EPSILON)
    return values * factor * gain


def attend_block(carry, queries, key_block, value_block, allowed):
    running, total, accum = carry
    scores = jnp.einsum(
        "qhd,kd->qhk", queries, key_block, preferred_element_type=jnp.float32
    ) * HD ** (-0.5)
    open_mask = allowed[:, None, :]
    highest = jnp.max(jnp.where(open_mask, scores, NEGATIVE), axis=2)
    renewed = jnp.maximum(running, highest)
    weights = jnp.where(open_mask, jnp.exp(scores - renewed[:, :, None]), 0.0)
    factor = jnp.exp(running - renewed)
    total = total * factor + jnp.sum(weights, axis=2)
    accum = accum * factor[:, :, None] + jnp.einsum(
        "qhk,kd->qhd", weights.astype(jnp.bfloat16), value_block, preferred_element_type=jnp.float32
    )
    return (renewed, total, accum)


def per_device(
    tokens,
    segment_ids,
    attn_gain,
    w_query,
    w_kv,
    w_out,
    ffn_gain,
    w_gate,
    w_up,
    w_down,
    expert_picks,
    gate_weights,
    page_table,
):
    count = tokens.shape[0]
    seq_index = lax.axis_index("seq")
    tp_index = lax.axis_index("tp")
    tp_count = lax.axis_size("tp")
    normed = row_norm(tokens, attn_gain).astype(jnp.bfloat16)
    queries = jnp.dot(normed, w_query, preferred_element_type=jnp.float32).astype(jnp.bfloat16)
    keyval = jnp.dot(normed, w_kv, preferred_element_type=jnp.float32).astype(jnp.bfloat16)
    cache_width = keyval.shape[1] // tp_count
    cache_columns = lax.dynamic_slice_in_dim(keyval, tp_index * cache_width, cache_width, 1)
    page_rows = page_table.shape[0]
    page_length = count // page_rows
    local_pages = page_table - seq_index * page_rows
    kv_pages = (
        jnp.zeros((page_rows, page_length, cache_width), jnp.bfloat16)
        .at[local_pages]
        .set(cache_columns.reshape(page_rows, page_length, cache_width))
    )
    heads = queries.shape[1] // HD
    group = tp_index * heads // (HQ // HK)
    key_head = lax.dynamic_slice_in_dim(keyval, group * HD, HD, 1)
    value_head = lax.dynamic_slice_in_dim(keyval, (HK + group) * HD, HD, 1)
    query_heads = queries.reshape(count, heads, HD)
    query_index = seq_index * count + jnp.arange(count, dtype=jnp.int32)

    def visit(carry, piece, start):
        key_piece, value_piece, segment_piece = piece
        width = key_piece.shape[0]
        key_index = start + jnp.arange(width, dtype=jnp.int32)
        allowed = (
            (segment_piece[None, :] == segment_ids[:, None])
            & (key_index[None, :] <= query_index[:, None])
            & (key_index[None, :] >= 0)
        )
        return attend_block(carry, query_heads, key_piece, value_piece, allowed)

    start_state = (
        jnp.full((count, heads), NEGATIVE, jnp.float32),
        jnp.zeros((count, heads), jnp.float32),
        jnp.zeros((count, heads, HD), jnp.float32),
    )
    own_piece = (key_head, value_head, segment_ids)
    first_state = visit(start_state, own_piece, seq_index * count)

    def backward(carry, number):
        state, piece = carry
        moved = shifted((piece[0], piece[1], piece[2]), "seq", 1)
        state = visit(state, moved, (seq_index - number) * count)
        return ((state, moved), None)

    reach_steps = lax.axis_size("seq") // 4
    (final, ignored_piece), ignored = lax.scan(
        backward, (first_state, own_piece), jnp.arange(1, reach_steps + 1, dtype=jnp.int32)
    )
    attended = (final[2] / final[1][:, :, None]).astype(jnp.bfloat16).reshape(count, heads * HD)
    projected = jnp.dot(attended, w_out, preferred_element_type=jnp.float32)
    experts = lax.axis_size("seq") * w_gate.shape[0]
    choose = expert_picks.shape[1]
    capacity = count * choose * 5 // (4 * experts)
    flat_picks = expert_picks.reshape(-1)
    matches = (flat_picks[:, None] == jnp.arange(experts, dtype=jnp.int32)[None, :]).astype(
        jnp.int32
    )
    ranks = jnp.sum((jnp.cumsum(matches, axis=0) - 1) * matches, axis=1)
    target = flat_picks * capacity + ranks
    source = jnp.arange(count * choose, dtype=jnp.int32) // choose
    part_width = tokens.shape[1] // tp_count
    summed = lax.psum(projected.astype(jnp.bfloat16), "tp").astype(jnp.float32)
    residual = tokens.astype(jnp.float32) + summed
    mixed_in = row_norm(residual, ffn_gain).astype(jnp.bfloat16)
    columns = mixed_in.shape[1]
    arrived = lax.all_to_all(
        jnp.zeros((experts * capacity, columns), jnp.bfloat16)
        .at[target]
        .set(mixed_in[source])
        .reshape(experts, capacity, columns),
        "seq",
        split_axis=0,
        concat_axis=0,
        tiled=True,
    )
    sources, slots, apply_columns = arrived.shape
    stacked = arrived.reshape(sources * slots, apply_columns)
    gate_part = jnp.dot(stacked, w_gate[0], preferred_element_type=jnp.float32)
    up_part = jnp.dot(stacked, w_up[0], preferred_element_type=jnp.float32)
    hidden = (jax.nn.relu(gate_part) * up_part).astype(jnp.bfloat16)
    partial_out = jnp.dot(hidden, w_down[0], preferred_element_type=jnp.float32).reshape(
        sources, slots, apply_columns
    )
    share = lax.psum_scatter(
        partial_out.astype(jnp.bfloat16), "tp", scatter_dimension=2, tiled=True
    )
    returned = lax.all_to_all(share, "seq", split_axis=0, concat_axis=0, tiled=True)
    residual_part = lax.dynamic_slice_in_dim(residual, tp_index * part_width, part_width, 1)
    gathered = (
        returned.reshape(experts * capacity, part_width)[target]
        .astype(jnp.float32)
        .reshape(count, choose, part_width)
    )
    mixture = jnp.sum(gathered * gate_weights[:, :, None], axis=1)
    layer_out = (residual_part + mixture).astype(jnp.bfloat16)
    return (layer_out, kv_pages)


def solution(mesh):
    placed = (
        P("seq", None),
        P("seq"),
        P(),
        P(None, "tp"),
        P(),
        P("tp", None),
        P(),
        P("seq", None, "tp"),
        P("seq", None, "tp"),
        P("seq", "tp", None),
        P("seq", None),
        P("seq", None),
        P("seq"),
    )
    return jax.shard_map(
        per_device,
        mesh=mesh,
        in_specs=placed,
        out_specs=(P("seq", "tp"), P("seq", None, "tp")),
        check_vma=False,
    )
```

profile of v0, /device:TPU:1, one launch (start us, length us, event | category | flops | bytes accessed | tf_op | source)
XLA Modules:
  0.0 546.5 jit_solution(9336817382695276845)
XLA Ops:
  9.2 3.4 convolution_convert_fusion.2
  18.7 126.3 %while.21 = (s32[]{:T(128)}, f32[512,3]{0,1:T(4,128)S(1)}, f32[512,3]{0,1:T(4,128)S(1)}, f32[512,3,128]{2,0,1:T(8,128)}, bf16[512,128]{1,0:T(8,128)(2,1)S(1)}, /...) while((s32[]{:T(128)}, f32[512,3]{0,1:T(4,128)S(1)}, ...), condition=%wide.region_6.7_spmd.clone, body=%wide.region_3.6_spmd.clone.sunk | while | flops 412750848 | bytes 20702564 | solution.py:109
  18.7 4.0 collective-permute-start
  37.0 3.6 collective-permute-start.1
  48.1 3.6 collective-permute-start
  51.7 4.4 collective-permute-start.1
  64.0 3.3 collective-permute-start
  67.4 5.0 collective-permute-start.1
  72.4 3.6 collective-permute-start.2
  81.1 4.1 collective-permute-start
  85.3 4.5 collective-permute-start.1
  97.0 4.8 collective-permute-start
  101.8 4.4 collective-permute-start.1
  127.1 3.7 collective-permute-start
  130.8 4.9 collective-permute-start.1
  135.7 4.1 collective-permute-start.2
  146.5 3.4 convolution_convert_fusion.1
  150.7 9.1 %reduce-window.6 = s32[32,16,128]{2,1,0:T(8,128)S(1)} reduce-window(s32[32,16,128]{2,1,0:T(8,128)S(1)} %fusion.43, s32[]{:T(128)} %constant.39.clone.1), window={size=1x1x128 pad=0_0x0_0x127_0}, to_apply=%region_8.9 | reduce-window | flops 8323072 | bytes 524292 | tf_op jit(solution)/shard_map/reduce-window
  161.0 52.6 %all-reduce.2.cloned.1.call-done = bf16[512,1536]{1,0:T(8,128)(2,1)} async-done(((bf16[512,1536]{1,0:T(8,128)(2,1)}), bf16[512,1536]{1,0:T(8,128)(2,1)}) %all-reduce.2.cloned.1.call-update) | async-done | bytes 1572880 | tf_op jit(solution)/shard_map/psum | solution.py:125
  213.6 3.7 convert_add_fusion
  219.2 36.0 %scatter_custom_fusion = bf16[2560,1536]{1,0:T(8,128)(2,1)} fusion(s32[2048]{0:T(1024)S(1)} %bitcast.87, bf16[512,1536]{1,0:T(8,128)(2,1)} %multiply_convert_fusion, s32[2048]{0:T(1024)S(1)} %broadcast_clamp_fusion.1, bf16[]{:T(256)} %constant.97.clone.1), kind=kCustom, calls=%fused_computation.26 | custom fusion | bytes 7864832 | tf_op jit(solution)/shard_map/scatter | solution.py:132
  255.1 97.2 %all_to_all.10 = bf16[32,80,1536]{2,1,0:T(8,128)(2,1)S(1)} all-to-all(bf16[32,80,1536]{2,1,0:T(8,128)(2,1)} %bitcast.74), channel_id=1, replica_groups=mesh['seq'=32,'tp'=4] {'seq'}, dimensions={0} | all-to-all | bytes 15728640 | tf_op jit(solution)/shard_map/all_to_all | solution.py:129
  358.4 5.2 convolution_convert_fusion
  363.7 15.6 %copy.49 = bf16[32,80,1536]{1,0,2:T(8,128)(2,1)} copy(bf16[32,80,1536]{2,1,0:T(8,128)(2,1)} %convolution_convert_fusion) | data formatting | bytes 15728640
  379.3 22.9 %reshape.332 = bf16[1536,2560]{1,0:T(8,128)(2,1)} reshape(bf16[1536,32,80]{2,1,0:T(8,128)(2,1)} %bitcast.73) | data formatting | bytes 15728640
  402.2 75.0 %reduce-scatter.4.cloned.1.call-done = bf16[384,2560]{1,0:T(8,128)(2,1)} async-done(((bf16[1536,2560]{1,0:T(8,128)(2,1)}), bf16[384,2560]{1,0:T(8,128)(2,1)}) %reduce-scatter.4.cloned.1.call-update) | async-done | bytes 1966096
  477.2 5.3 reshape.333
  485.7 7.4 %all-to-all-start.1 = ((bf16[32,80,384]{2,1,0:T(8,128)(2,1)}), bf16[32,80,384]{2,1,0:T(8,128)(2,1)S(1)}, u32[]{:S(2)}, u32[]{:S(2)}) async-start(bf16[32,80,384]{2,1,0:T(8,128)(2,1)} %copy.50), calls=%async_computation.1 | async-start | bytes 3932160 | tf_op jit(solution)/shard_map/all_to_all | solution.py:150
  494.0 25.7 %all-to-all-done.1 = bf16[32,80,384]{2,1,0:T(8,128)(2,1)S(1)} async-done(((bf16[32,80,384]{2,1,0:T(8,128)(2,1)}), bf16[32,80,384]{2,1,0:T(8,128)(2,1)S(1)}, u32[]{:S(2)}, u32[]{:S(2)}) %all-to-all-start.1) | async-done | bytes 1966112 | tf_op jit(solution)/shard_map/all_to_all | solution.py:150
  519.7 9.0 %gather_fusion = bf16[2048,384]{1,0:T(8,128)(2,1)} fusion(bf16[2560,384]{1,0:T(8,128)(2,1)S(1)} %bitcast.72, s32[2048]{0:T(1024)S(1)} %broadcast_clamp_fusion), kind=kCustom, calls=%fused_computation.1 | custom fusion | bytes 3153920 | tf_op jit(solution)/shard_map/gather | solution.py:153
  528.8 4.4 reshape.293
  533.1 4.6 multiply_reduce_fusion
  (248 shorter events, 87.8 us)
Async XLA Ops:
  7.2 206.4 %all-reduce.2.cloned.1.call-start = ((), (), s32[]{:S(2)}) async-start(), calls=%async_computation.3 | async-start | bytes 3145728 | tf_op jit(solution)/shard_map/psum | solution.py:125
  18.7 11.4 %collective-permute-start = (s32[512]{0:T(512)S(1)}, s32[512]{0:T(512)S(1)}, u32[]{:S(2)}, u32[]{:S(2)}) collective-permute-start(s32[512]{0:T(512)S(1)} %get-tuple-element.274), channel_id=1, source_target_pairs={{0,4},{4,8},{8,12},{12,16},{16,20},{20,24},{24,28},{28,32},{32,36}... | collective-permute-start | bytes 6152 | tf_op jit(solution)/shard_map/while/body/eval_jaxpr/ppermute | solution.py:18
  22.7 7.7 %collective-permute-start.1 = (bf16[512,128]{1,0:T(8,128)(2,1)S(1)}, bf16[512,128]{1,0:T(8,128)(2,1)S(1)}, u32[]{:S(2)}, u32[]{:S(2)}) collective-permute-start(bf16[512,128]{1,0:T(8,128)(2,1)S(1)} %get-tuple-element.272), channel_id=1, source_target_pairs={{0,4},{4,8},{8,12},{12,16},{16,20},{20,24},{24,28},{28,32},{32,36}... | collective-permute-start | bytes 393224 | tf_op jit(solution)/shard_map/while/body/eval_jaxpr/ppermute | solution.py:18
  25.7 6.2 %collective-permute-start.2 = (bf16[512,128]{1,0:T(8,128)(2,1)S(1)}, bf16[512,128]{1,0:T(8,128)(2,1)S(1)}, u32[]{:S(2)}, u32[]{:S(2)}) collective-permute-start(bf16[512,128]{1,0:T(8,128)(2,1)S(1)} %get-tuple-element.273), channel_id=1, source_target_pairs={{0,4},{4,8},{8,12},{12,16},{16,20},{20,24},{24,28},{28,32},{32,36}... | collective-permute-start | bytes 393224 | tf_op jit(solution)/shard_map/while/body/eval_jaxpr/ppermute | solution.py:18
  34.0 10.1 %collective-permute-start = (s32[512]{0:T(512)S(1)}, s32[512]{0:T(512)S(1)}, u32[]{:S(2)}, u32[]{:S(2)}) collective-permute-start(s32[512]{0:T(512)S(1)} %get-tuple-element.274), channel_id=1, source_target_pairs={{0,4},{4,8},{8,12},{12,16},{16,20},{20,24},{24,28},{28,32},{32,36}... | collective-permute-start | bytes 6152 | tf_op jit(solution)/shard_map/while/body/eval_jaxpr/ppermute | solution.py:18
  37.0 7.4 %collective-permute-start.1 = (bf16[512,128]{1,0:T(8,128)(2,1)S(1)}, bf16[512,128]{1,0:T(8,128)(2,1)S(1)}, u32[]{:S(2)}, u32[]{:S(2)}) collective-permute-start(bf16[512,128]{1,0:T(8,128)(2,1)S(1)} %get-tuple-element.272), channel_id=1, source_target_pairs={{0,4},{4,8},{8,12},{12,16},{16,20},{20,24},{24,28},{28,32},{32,36}... | collective-permute-start | bytes 393224 | tf_op jit(solution)/shard_map/while/body/eval_jaxpr/ppermute | solution.py:18
  40.6 5.4 collective-permute-start.2
  48.1 11.9 %collective-permute-start = (s32[512]{0:T(512)S(1)}, s32[512]{0:T(512)S(1)}, u32[]{:S(2)}, u32[]{:S(2)}) collective-permute-start(s32[512]{0:T(512)S(1)} %get-tuple-element.274), channel_id=1, source_target_pairs={{0,4},{4,8},{8,12},{12,16},{16,20},{20,24},{24,28},{28,32},{32,36}... | collective-permute-start | bytes 6152 | tf_op jit(solution)/shard_map/while/body/eval_jaxpr/ppermute | solution.py:18
  51.7 8.6 %collective-permute-start.1 = (bf16[512,128]{1,0:T(8,128)(2,1)S(1)}, bf16[512,128]{1,0:T(8,128)(2,1)S(1)}, u32[]{:S(2)}, u32[]{:S(2)}) collective-permute-start(bf16[512,128]{1,0:T(8,128)(2,1)S(1)} %get-tuple-element.272), channel_id=1, source_target_pairs={{0,4},{4,8},{8,12},{12,16},{16,20},{20,24},{24,28},{28,32},{32,36}... | collective-permute-start | bytes 393224 | tf_op jit(solution)/shard_map/while/body/eval_jaxpr/ppermute | solution.py:18
  56.1 5.8 %collective-permute-start.2 = (bf16[512,128]{1,0:T(8,128)(2,1)S(1)}, bf16[512,128]{1,0:T(8,128)(2,1)S(1)}, u32[]{:S(2)}, u32[]{:S(2)}) collective-permute-start(bf16[512,128]{1,0:T(8,128)(2,1)S(1)} %get-tuple-element.273), channel_id=1, source_target_pairs={{0,4},{4,8},{8,12},{12,16},{16,20},{20,24},{24,28},{28,32},{32,36}... | collective-permute-start | bytes 393224 | tf_op jit(solution)/shard_map/while/body/eval_jaxpr/ppermute | solution.py:18
  64.0 13.1 %collective-permute-start = (s32[512]{0:T(512)S(1)}, s32[512]{0:T(512)S(1)}, u32[]{:S(2)}, u32[]{:S(2)}) collective-permute-start(s32[512]{0:T(512)S(1)} %get-tuple-element.274), channel_id=1, source_target_pairs={{0,4},{4,8},{8,12},{12,16},{16,20},{20,24},{24,28},{28,32},{32,36}... | collective-permute-start | bytes 6152 | tf_op jit(solution)/shard_map/while/body/eval_jaxpr/ppermute | solution.py:18
  67.4 10.1 %collective-permute-start.1 = (bf16[512,128]{1,0:T(8,128)(2,1)S(1)}, bf16[512,128]{1,0:T(8,128)(2,1)S(1)}, u32[]{:S(2)}, u32[]{:S(2)}) collective-permute-start(bf16[512,128]{1,0:T(8,128)(2,1)S(1)} %get-tuple-element.272), channel_id=1, source_target_pairs={{0,4},{4,8},{8,12},{12,16},{16,20},{20,24},{24,28},{28,32},{32,36}... | collective-permute-start | bytes 393224 | tf_op jit(solution)/shard_map/while/body/eval_jaxpr/ppermute | solution.py:18
  72.4 6.6 %collective-permute-start.2 = (bf16[512,128]{1,0:T(8,128)(2,1)S(1)}, bf16[512,128]{1,0:T(8,128)(2,1)S(1)}, u32[]{:S(2)}, u32[]{:S(2)}) collective-permute-start(bf16[512,128]{1,0:T(8,128)(2,1)S(1)} %get-tuple-element.273), channel_id=1, source_target_pairs={{0,4},{4,8},{8,12},{12,16},{16,20},{20,24},{24,28},{28,32},{32,36}... | collective-permute-start | bytes 393224 | tf_op jit(solution)/shard_map/while/body/eval_jaxpr/ppermute | solution.py:18
  81.1 11.9 %collective-permute-start = (s32[512]{0:T(512)S(1)}, s32[512]{0:T(512)S(1)}, u32[]{:S(2)}, u32[]{:S(2)}) collective-permute-start(s32[512]{0:T(512)S(1)} %get-tuple-element.274), channel_id=1, source_target_pairs={{0,4},{4,8},{8,12},{12,16},{16,20},{20,24},{24,28},{28,32},{32,36}... | collective-permute-start | bytes 6152 | tf_op jit(solution)/shard_map/while/body/eval_jaxpr/ppermute | solution.py:18
  85.3 8.1 %collective-permute-start.1 = (bf16[512,128]{1,0:T(8,128)(2,1)S(1)}, bf16[512,128]{1,0:T(8,128)(2,1)S(1)}, u32[]{:S(2)}, u32[]{:S(2)}) collective-permute-start(bf16[512,128]{1,0:T(8,128)(2,1)S(1)} %get-tuple-element.272), channel_id=1, source_target_pairs={{0,4},{4,8},{8,12},{12,16},{16,20},{20,24},{24,28},{28,32},{32,36}... | collective-permute-start | bytes 393224 | tf_op jit(solution)/shard_map/while/body/eval_jaxpr/ppermute | solution.py:18
  89.7 5.1 collective-permute-start.2
  97.0 12.3 %collective-permute-start = (s32[512]{0:T(512)S(1)}, s32[512]{0:T(512)S(1)}, u32[]{:S(2)}, u32[]{:S(2)}) collective-permute-start(s32[512]{0:T(512)S(1)} %get-tuple-element.274), channel_id=1, source_target_pairs={{0,4},{4,8},{8,12},{12,16},{16,20},{20,24},{24,28},{28,32},{32,36}... | collective-permute-start | bytes 6152 | tf_op jit(solution)/shard_map/while/body/eval_jaxpr/ppermute | solution.py:18
  101.8 7.8 %collective-permute-start.1 = (bf16[512,128]{1,0:T(8,128)(2,1)S(1)}, bf16[512,128]{1,0:T(8,128)(2,1)S(1)}, u32[]{:S(2)}, u32[]{:S(2)}) collective-permute-start(bf16[512,128]{1,0:T(8,128)(2,1)S(1)} %get-tuple-element.272), channel_id=1, source_target_pairs={{0,4},{4,8},{8,12},{12,16},{16,20},{20,24},{24,28},{28,32},{32,36}... | collective-permute-start | bytes 393224 | tf_op jit(solution)/shard_map/while/body/eval_jaxpr/ppermute | solution.py:18
  106.2 4.9 collective-permute-start.2
  113.3 9.8 %collective-permute-start = (s32[512]{0:T(512)S(1)}, s32[512]{0:T(512)S(1)}, u32[]{:S(2)}, u32[]{:S(2)}) collective-permute-start(s32[512]{0:T(512)S(1)} %get-tuple-element.274), channel_id=1, source_target_pairs={{0,4},{4,8},{8,12},{12,16},{16,20},{20,24},{24,28},{28,32},{32,36}... | collective-permute-start | bytes 6152 | tf_op jit(solution)/shard_map/while/body/eval_jaxpr/ppermute | solution.py:18
  115.9 7.5 %collective-permute-start.1 = (bf16[512,128]{1,0:T(8,128)(2,1)S(1)}, bf16[512,128]{1,0:T(8,128)(2,1)S(1)}, u32[]{:S(2)}, u32[]{:S(2)}) collective-permute-start(bf16[512,128]{1,0:T(8,128)(2,1)S(1)} %get-tuple-element.272), channel_id=1, source_target_pairs={{0,4},{4,8},{8,12},{12,16},{16,20},{20,24},{24,28},{28,32},{32,36}... | collective-permute-start | bytes 393224 | tf_op jit(solution)/shard_map/while/body/eval_jaxpr/ppermute | solution.py:18
  118.8 6.2 %collective-permute-start.2 = (bf16[512,128]{1,0:T(8,128)(2,1)S(1)}, bf16[512,128]{1,0:T(8,128)(2,1)S(1)}, u32[]{:S(2)}, u32[]{:S(2)}) collective-permute-start(bf16[512,128]{1,0:T(8,128)(2,1)S(1)} %get-tuple-element.273), channel_id=1, source_target_pairs={{0,4},{4,8},{8,12},{12,16},{16,20},{20,24},{24,28},{28,32},{32,36}... | collective-permute-start | bytes 393224 | tf_op jit(solution)/shard_map/while/body/eval_jaxpr/ppermute | solution.py:18
  127.1 13.9 %collective-permute-start = (s32[512]{0:T(512)S(1)}, s32[512]{0:T(512)S(1)}, u32[]{:S(2)}, u32[]{:S(2)}) collective-permute-start(s32[512]{0:T(512)S(1)} %get-tuple-element.274), channel_id=1, source_target_pairs={{0,4},{4,8},{8,12},{12,16},{16,20},{20,24},{24,28},{28,32},{32,36}... | collective-permute-start | bytes 6152 | tf_op jit(solution)/shard_map/while/body/eval_jaxpr/ppermute | solution.py:18
  130.8 10.5 %collective-permute-start.1 = (bf16[512,128]{1,0:T(8,128)(2,1)S(1)}, bf16[512,128]{1,0:T(8,128)(2,1)S(1)}, u32[]{:S(2)}, u32[]{:S(2)}) collective-permute-start(bf16[512,128]{1,0:T(8,128)(2,1)S(1)} %get-tuple-element.272), channel_id=1, source_target_pairs={{0,4},{4,8},{8,12},{12,16},{16,20},{20,24},{24,28},{28,32},{32,36}... | collective-permute-start | bytes 393224 | tf_op jit(solution)/shard_map/while/body/eval_jaxpr/ppermute | solution.py:18
  135.7 7.1 %collective-permute-start.2 = (bf16[512,128]{1,0:T(8,128)(2,1)S(1)}, bf16[512,128]{1,0:T(8,128)(2,1)S(1)}, u32[]{:S(2)}, u32[]{:S(2)}) collective-permute-start(bf16[512,128]{1,0:T(8,128)(2,1)S(1)} %get-tuple-element.273), channel_id=1, source_target_pairs={{0,4},{4,8},{8,12},{12,16},{16,20},{20,24},{24,28},{28,32},{32,36}... | collective-permute-start | bytes 393224 | tf_op jit(solution)/shard_map/while/body/eval_jaxpr/ppermute | solution.py:18
  149.9 327.3 %reduce-scatter.4.cloned.1.call-start = ((), (), s32[]{:S(2)}) async-start(), calls=%async_computation.4 | async-start | bytes 9830400
  161.0 56.4 %copy-start.10 = (f32[1536]{0:T(1024)S(1)}, f32[1536]{0:T(1024)}, u32[]{:S(2)}) copy-start(f32[1536]{0:T(1024)} %param.21) | copy-start | bytes 18436
  255.1 97.2 %copy-start.13 = (bf16[1,1536,192]{1,2,0:T(8,128)(2,1)S(1)}, bf16[1,1536,192]{1,2,0:T(8,128)(2,1)}, u32[]{:S(2)}) copy-start(bf16[1,1536,192]{1,2,0:T(8,128)(2,1)} %param.22) | copy-start | bytes 1769476
  485.7 7.6 %copy-start.16 = (s32[4]{0:T(128)S(1)}, s32[4]{0:T(128)}, u32[]{:S(2)}) copy-start(s32[4]{0:T(128)} %param.27) | copy-start | bytes 52
  485.7 34.0 %all-to-all-start.1 = ((bf16[32,80,384]{2,1,0:T(8,128)(2,1)}), bf16[32,80,384]{2,1,0:T(8,128)(2,1)S(1)}, u32[]{:S(2)}, u32[]{:S(2)}) async-start(bf16[32,80,384]{2,1,0:T(8,128)(2,1)} %copy.50), calls=%async_computation.1 | async-start | bytes 3932160 | tf_op jit(solution)/shard_map/all_to_all | solution.py:150
  494.0 34.7 %copy-start.7 = (bf16[4,128,128]{2,1,0:T(8,128)(2,1)}, bf16[4,128,128]{2,1,0:T(8,128)(2,1)S(1)}, u32[]{:S(2)}) copy-start(bf16[4,128,128]{2,1,0:T(8,128)(2,1)S(1)} %scatter_fusion) | copy-start | bytes 393220
  528.8 10.9 %copy-start.1 = (bf16[1536,512]{1,0:T(8,128)(2,1)S(1)}, bf16[1536,512]{1,0:T(8,128)(2,1)}, u32[]{:S(2)}) copy-start(bf16[1536,512]{1,0:T(8,128)(2,1)} %param.19) | copy-start | bytes 4718596
  (26 other events, 53.9 us)
Sparse Core Ops, SparseCore 0:
  150.1 63.5 all-reduce.1
  402.3 74.8 reduce-scatter.3
where the time goes:
time: 550 us; the launch traced here: 546 us
  waiting for transfers between devices  153 us (28%)
  local copies, waits for them, and re-layouts  113 us (21%)
  blocking collectives  97.2 us (18%)
  starting transfers between devices  92.7 us (17%)
  matrix products  36.4 us (7%)
  other arithmetic  33.2 us (6%)
  between operations  14.5 us (3%)
  loops' own time  5.64 us (1%)
    all_to_all x1, blocking collectives, per_device(): lax.all_to_all(jnp.zeros((experts * capacity, columns), jnp.bfloat16).at[...  97.2 us
    ppermute x24, starting transfers between devices, shifted(): lax.ppermute(value, axis, [(source, source + steps) for source in range(l...  85.1 us
    unnamed x3, waiting for transfers between devices  75 us
    psum x1, waiting for transfers between devices, per_device(): summed = lax.psum(projected.astype(jnp.bfloat16), 'tp').astype(jnp.float32)  52.6 us
    unnamed x38, local copies, waits for them, and re-layouts  47.6 us
    scatter x1, local copies, waits for them, and re-layouts, per_device(): arrived = lax.all_to_all(jnp.zeros((experts * capacity, columns), jnp.bfl...  36 us
    all_to_all x1, waiting for transfers between devices, per_device(): lax.all_to_all(share, 'seq', split_axis=0, concat_axis=0, tiled=True)  25.7 us
    dot_general x9, matrix products, attend_block(): jnp.einsum('qhk,kd->qhd', weights.astype(jnp.bfloat16), value_block, pref...  11.5 us
  transfers between devices with their start and end apart: 27, of which 3 were waited for; matrix products, arithmetic and copies ran while one was open for 6% of the time, Pallas kernels for 0%

commit v1 on v0

--- a/solution.py
+++ b/solution.py
@@ -79,81 +79,72 @@
     value_head = lax.dynamic_slice_in_dim(keyval, (HK + group) * HD, HD, 1)
     query_heads = queries.reshape(count, heads, HD)
     query_index = seq_index * count + jnp.arange(count, dtype=jnp.int32)
+    all_segments = lax.all_gather(segment_ids, "seq", tiled=True)
+    own_piece = jnp.concatenate([key_head, value_head], axis=1)
+    reach_steps = lax.axis_size("seq") // 4
+    pieces = [own_piece] + [shifted(own_piece, "seq", number) for number in range(1, reach_steps + 1)]
 
-    def visit(carry, piece, start):
-        key_piece, value_piece, segment_piece = piece
-        width = key_piece.shape[0]
-        key_index = start + jnp.arange(width, dtype=jnp.int32)
+    def visit(carry, piece, number):
+        start = (seq_index - number) * count
+        key_index = start + jnp.arange(count, dtype=jnp.int32)
+        segment_piece = lax.dynamic_slice_in_dim(all_segments, jnp.maximum(start, 0), count)
         allowed = (
             (segment_piece[None, :] == segment_ids[:, None])
             & (key_index[None, :] <= query_index[:, None])
             & (key_index[None, :] >= 0)
         )
-        return attend_block(carry, query_heads, key_piece, value_piece, allowed)
+        return attend_block(carry, query_heads, piece[:, :HD], piece[:, HD:], allowed)
 
-    start_state = (
+    state = (
         jnp.full((count, heads), NEGATIVE, jnp.float32),
         jnp.zeros((count, heads), jnp.float32),
         jnp.zeros((count, heads, HD), jnp.float32),
     )
-    own_piece = (key_head, value_head, segment_ids)
-    first_state = visit(start_state, own_piece, seq_index * count)
-
-    def backward(carry, number):
-        state, piece = carry
-        moved = shifted((piece[0], piece[1], piece[2]), "seq", 1)
-        state = visit(state, moved, (seq_index - number) * count)
-        return ((state, moved), None)
-
-    reach_steps = lax.axis_size("seq") // 4
-    (final, ignored_piece), ignored = lax.scan(
-        backward, (first_state, own_piece), jnp.arange(1, reach_steps + 1, dtype=jnp.int32)
-    )
-    attended = (final[2] / final[1][:, :, None]).astype(jnp.bfloat16).reshape(count, heads * HD)
+    for number, piece in enumerate(pieces):
+        state = visit(state, piece, number)
+    attended = (state[2] / state[1][:, :, None]).astype(jnp.bfloat16).reshape(count, heads * HD)
     projected = jnp.dot(attended, w_out, preferred_element_type=jnp.float32)
     experts = lax.axis_size("seq") * w_gate.shape[0]
     choose = expert_picks.shape[1]
     capacity = count * choose * 5 // (4 * experts)
-    flat_picks = expert_picks.reshape(-1)
-    matches = (flat_picks[:, None] == jnp.arange(experts, dtype=jnp.int32)[None, :]).astype(
-        jnp.int32
+    share = capacity // tp_count
+    slots = experts * share
+    onehot = (expert_picks[:, :, None] == jnp.arange(experts, dtype=jnp.int32)[None, None, :]).astype(
+        jnp.float32
     )
-    ranks = jnp.sum((jnp.cumsum(matches, axis=0) - 1) * matches, axis=1)
-    target = flat_picks * capacity + ranks
-    source = jnp.arange(count * choose, dtype=jnp.int32) // choose
+    earlier = (
+        jnp.arange(count, dtype=jnp.int32)[:, None] > jnp.arange(count, dtype=jnp.int32)[None, :]
+    ).astype(jnp.bfloat16)
+    before = jnp.dot(
+        earlier, jnp.sum(onehot, axis=1).astype(jnp.bfloat16), preferred_element_type=jnp.float32
+    )
+    ranks = jnp.sum(before[:, None, :] * onehot, axis=2).astype(jnp.int32)
+    owner = ranks // share
+    slot = expert_picks * share + ranks % share
+    token_of = jnp.broadcast_to(jnp.arange(count, dtype=jnp.int32)[:, None], expert_picks.shape)
+    table = (
+        jnp.full((slots,), count, jnp.int32)
+        .at[jnp.where(owner == tp_index, slot, slots).reshape(-1)]
+        .set(token_of.reshape(-1), mode="drop")
+    )
     part_width = tokens.shape[1] // tp_count
     summed = lax.psum(projected.astype(jnp.bfloat16), "tp").astype(jnp.float32)
     residual = tokens.astype(jnp.float32) + summed
     mixed_in = row_norm(residual, ffn_gain).astype(jnp.bfloat16)
     columns = mixed_in.shape[1]
-    arrived = lax.all_to_all(
-        jnp.zeros((experts * capacity, columns), jnp.bfloat16)
-        .at[target]
-        .set(mixed_in[source])
-        .reshape(experts, capacity, columns),
-        "seq",
-        split_axis=0,
-        concat_axis=0,
-        tiled=True,
-    )
-    sources, slots, apply_columns = arrived.shape
-    stacked = arrived.reshape(sources * slots, apply_columns)
-    gate_part = jnp.dot(stacked, w_gate[0], preferred_element_type=jnp.float32)
-    up_part = jnp.dot(stacked, w_up[0], preferred_element_type=jnp.float32)
+    padded = jnp.concatenate([mixed_in, jnp.zeros((1, columns), jnp.bfloat16)], axis=0)
+    arrived = lax.all_to_all(padded[table], "seq", split_axis=0, concat_axis=0, tiled=True)
+    gate_full = lax.all_gather(w_gate[0], "tp", axis=1, tiled=True)
+    up_full = lax.all_gather(w_up[0], "tp", axis=1, tiled=True)
+    down_full = lax.all_gather(w_down[0], "tp", axis=0, tiled=True)
+    gate_part = jnp.dot(arrived, gate_full, preferred_element_type=jnp.float32)
+    up_part = jnp.dot(arrived, up_full, preferred_element_type=jnp.float32)
     hidden = (jax.nn.relu(gate_part) * up_part).astype(jnp.bfloat16)
-    partial_out = jnp.dot(hidden, w_down[0], preferred_element_type=jnp.float32).reshape(
-        sources, slots, apply_columns
-    )
-    share = lax.psum_scatter(
-        partial_out.astype(jnp.bfloat16), "tp", scatter_dimension=2, tiled=True
-    )
-    returned = lax.all_to_all(share, "seq", split_axis=0, concat_axis=0, tiled=True)
+    expert_out = jnp.dot(hidden, down_full, preferred_element_type=jnp.float32).astype(jnp.bfloat16)
+    returned = lax.all_to_all(expert_out, "seq", split_axis=0, concat_axis=0, tiled=True)
+    mine = lax.all_to_all(returned, "tp", split_axis=1, concat_axis=0, tiled=True)
     residual_part = lax.dynamic_slice_in_dim(residual, tp_index * part_width, part_width, 1)
-    gathered = (
-        returned.reshape(experts * capacity, part_width)[target]
-        .astype(jnp.float32)
-        .reshape(count, choose, part_width)
-    )
+    gathered = mine[jnp.minimum(owner * slots + slot, tp_count * slots - 1)].astype(jnp.float32)
     mixture = jnp.sum(gathered * gate_weights[:, :, None], axis=1)
     layer_out = (residual_part + mixture).astype(jnp.bfloat16)
     return (layer_out, kv_pages)

time: 550 us -> 437 us (0.79)
  local copies, waits for them, and re-layouts: 113 us -> 39.1 us
  starting transfers between devices: 92.7 us -> 31.1 us
  blocking collectives: 97.2 us -> 144 us
  waiting for transfers between devices: 153 us -> 135 us
  other arithmetic: 33.2 us -> 23.1 us
  matrix products: 36.4 us -> 43.3 us
  loops' own time: 5.64 us -> 0 us
    unnamed x3 -> x4, waiting for transfers between devices: 75 us -> 1.91 us
    all_gather x0 -> x1, blocking collectives: none -> 63.7 us  [per_device(): all_segments = lax.all_gather(segment_ids, 'seq', tiled=True)]
    ppermute x24 -> x8, starting transfers between devices: 85.1 us -> 25.7 us  [shifted(): lax.ppermute(value, axis, [(source, source + steps) for source in range(l...]
    all_gather x0 -> x3, waiting for transfers between devices: none -> 52.2 us  [the longest x1 29.1 us: per_device(): gate_full = lax.all_gather(w_gate[0], 'tp', axis=1, tiled=True)]
    unnamed x38 -> x25, local copies, waits for them, and re-layouts: 47.6 us -> 0.22 us
    scatter x1, local copies, waits for them, and re-layouts: 36 us -> 8.04 us  [per_device(): table = jnp.full((slots,), count, jnp.int32).at[jnp.where(owner == tp_ind...]
    all_to_all x1 -> x2, blocking collectives: 97.2 us -> 80.7 us  [the longest x1 42.5 us: per_device(): lax.all_to_all(padded[table], 'seq', split_axis=0, concat_axis=0, tiled=T...]
    all_to_all x0 -> x5, local copies, waits for them, and re-layouts: none -> 11.9 us  [the longest x2 5.07 us: per_device(): lax.all_to_all(padded[table], 'seq', split_axis=0, concat_axis=0, tiled=T...]
  transfers between devices with their start and end apart: 27 -> 13, of which waited for: 3 -> 4; matrix products, arithmetic and copies ran while one was open for 6% -> 9% of each run, Pallas kernels for 0% -> 0%
where the time goes in v1:
time: 437 us; the launch traced here: 431 us
  blocking collectives  144 us (33%)
  waiting for transfers between devices  135 us (31%)
  matrix products  43.3 us (10%)
  local copies, waits for them, and re-layouts  39.1 us (9%)
  starting transfers between devices  31.1 us (7%)
  other arithmetic  23.1 us (5%)
  between operations  15 us (3%)
    all_gather x1, blocking collectives, per_device(): all_segments = lax.all_gather(segment_ids, 'seq', tiled=True)  63.7 us
    psum x1, waiting for transfers between devices, per_device(): summed = lax.psum(projected.astype(jnp.bfloat16), 'tp').astype(jnp.float32)  57.6 us
    all_to_all x1, blocking collectives, per_device(): lax.all_to_all(padded[table], 'seq', split_axis=0, concat_axis=0, tiled=T...  42.5 us
    all_to_all x1, blocking collectives, per_device(): lax.all_to_all(expert_out, 'seq', split_axis=0, concat_axis=0, tiled=True)  38.2 us
    all_gather x1, waiting for transfers between devices, per_device(): gate_full = lax.all_gather(w_gate[0], 'tp', axis=1, tiled=True)  29.1 us
    ppermute x8, starting transfers between devices, shifted(): lax.ppermute(value, axis, [(source, source + steps) for source in range(l...  25.7 us
    all_to_all x1, waiting for transfers between devices, per_device(): lax.all_to_all(returned, 'tp', split_axis=1, concat_axis=0, tiled=True)  23.6 us
    all_gather x1, waiting for transfers between devices, per_device(): down_full = lax.all_gather(w_down[0], 'tp', axis=0, tiled=True)  23.2 us
  transfers between devices with their start and end apart: 13, of which 4 were waited for; matrix products, arithmetic and copies ran while one was open for 9% of the time, Pallas kernels for 0%

profile of v1, /device:TPU:1, one launch (start us, length us, event | category | flops | bytes accessed | tf_op | source)
XLA Modules:
  0.0 431.2 jit_solution(3679500511276597271)
XLA Ops:
  7.3 1.9 fusion
  9.2 2.5 convolution_convert_fusion.2
  12.6 6.9 %collective-permute-start.6 = (bf16[512,256]{1,0:T(8,128)(2,1)}, bf16[512,256]{1,0:T(8,128)(2,1)}, u32[]{:S(2)}, u32[]{:S(2)}) collective-permute-start(bf16[512,256]{1,0:T(8,128)(2,1)} %pad_maximum_fusion), channel_id=1, source_target_pairs={{0,28},{4,32},{8,36},{12,40},{16,44},{20,48},{24,52},{28,56},{32,6... | collective-permute-start | bytes 786440 | tf_op jit(solution)/shard_map/ppermute | solution.py:18
  19.5 4.5 %collective-permute-start.5 = (bf16[512,256]{1,0:T(8,128)(2,1)}, bf16[512,256]{1,0:T(8,128)(2,1)}, u32[]{:S(2)}, u32[]{:S(2)}) collective-permute-start(bf16[512,256]{1,0:T(8,128)(2,1)} %pad_maximum_fusion), channel_id=1, source_target_pairs={{0,24},{4,28},{8,32},{12,36},{16,40},{20,44},{24,48},{28,52},{32,5... | collective-permute-start | bytes 786440 | tf_op jit(solution)/shard_map/ppermute | solution.py:18
  24.0 3.4 collective-permute-start.4
  27.4 4.4 %collective-permute-start.3 = (bf16[512,256]{1,0:T(8,128)(2,1)}, bf16[512,256]{1,0:T(8,128)(2,1)}, u32[]{:S(2)}, u32[]{:S(2)}) collective-permute-start(bf16[512,256]{1,0:T(8,128)(2,1)} %pad_maximum_fusion), channel_id=1, source_target_pairs={{0,16},{4,20},{8,24},{12,28},{16,32},{20,36},{24,40},{28,44},{32,4... | collective-permute-start | bytes 786440 | tf_op jit(solution)/shard_map/ppermute | solution.py:18
  31.8 2.4 collective-permute-start.2
  34.4 63.7 %all-gather.3 = s32[32,1,512]{2,1,0:T(1,128)S(1)} all-gather(s32[1,1,512]{2,1,0:T(1,128)S(1)} %bitcast.123), channel_id=1, replica_groups=mesh['seq'=32,'tp'=4] {'seq'}, dimensions={0}, use_global_device_ids=true | all-gather | bytes 67584 | tf_op jit(solution)/shard_map/all_gather | solution.py:82
  98.2 2.2 convolution_convert_fusion.3
  100.5 1.9 and_and_fusion.8
  126.7 1.9 fusion.38
  137.6 2.2 convolution_convert_fusion.1
  142.8 8.0 %scatter_custom_fusion = s32[640]{0:T(1024)S(1)} fusion(s32[2048]{0:T(1024)S(1)} %bitcast.124, s32[2048]{0:T(1024)S(1)} %reshape.953, s32[]{:T(128)} %constant.41.clone.1), kind=kCustom, calls=%fused_computation.192 | custom fusion | bytes 2564 | tf_op jit(solution)/shard_map/scatter | solution.py:128
  150.9 57.6 %all-reduce.3.cloned.1.call-done = bf16[512,1536]{1,0:T(8,128)(2,1)} async-done(((bf16[512,1536]{1,0:T(8,128)(2,1)}), bf16[512,1536]{1,0:T(8,128)(2,1)}) %all-reduce.3.cloned.1.call-update) | async-done | bytes 1572880 | tf_op jit(solution)/shard_map/psum | solution.py:131
  208.5 3.7 convert_add_fusion
  212.9 3.7 gather_fusion
  216.6 2.5 all_to_all.28
  219.1 42.5 %all_to_all.40 = bf16[32,20,1536]{2,1,0:T(8,128)(2,1)} all-to-all(bf16[32,20,1536]{2,1,0:T(8,128)(2,1)S(1)} %all_to_all.28), channel_id=1, replica_groups=mesh['seq'=32,'tp'=4] {'seq'}, dimensions={0} | all-to-all | bytes 3932160 | tf_op jit(solution)/shard_map/all_to_all | solution.py:136
  261.6 2.6 all_to_all.30
  264.2 4.6 %fusion.22 = f32[640,768]{1,0:T(8,128)} fusion(bf16[640,1536]{1,0:T(8,128)(2,1)S(1)} %all_to_all.30, bf16[1,1536,768]{1,2,0:T(8,128)(2,1)} %all-gather.10.cloned.1.call-done), kind=kOutput, calls=%fused_computation.52 | convolution fusion | flops 1509949440 | bytes 6291456 | tf_op jit(solution)/shard_map/dot_general | solution.py:141
  268.8 23.2 %all-gather.12.cloned.1.call-done = bf16[1,768,1536]{2,1,0:T(8,128)(2,1)} async-done(((bf16[1,192,1536]{2,1,0:T(8,128)(2,1)}), bf16[1,768,1536]{2,1,0:T(8,128)(2,1)}) %all-gather.12.cloned.1.call-update) | async-done | bytes 2359312 | tf_op jit(solution)/shard_map/all_gather | solution.py:139
  292.0 29.1 %all-gather.8.cloned.1.call-done = bf16[1,1536,768]{1,2,0:T(8,128)(2,1)} async-done(((bf16[1,1536,192]{1,2,0:T(8,128)(2,1)}), bf16[1,1536,768]{1,2,0:T(8,128)(2,1)}) %all-gather.8.cloned.1.call-update) | async-done | bytes 2359312 | tf_op jit(solution)/shard_map/all_gather | solution.py:137
  321.0 8.2 %convolution_convert_fusion = bf16[640,1536]{1,0:T(8,128)(2,1)} fusion(bf16[1,768,1536]{2,1,0:T(8,128)(2,1)} %all-gather.12.cloned.1.call-done, f32[640,768]{1,0:T(8,128)} %fusion.22, bf16[640,1536]{1,0:T(8,128)(2,1)S(1)} %all_to_all.30, bf16[1,1536,768]{1,2,0:T(8,128)(2,1)} %all-gather.8.cloned.1.call-done), kind=kOutput, calls=%fused_computation.7 | convolution fusion | flops 3022356480 | bytes 10616832 | tf_op jit(solution)/shard_map/dot_general | solution.py:143
  329.2 2.5 all_to_all.31
  331.7 38.2 %all_to_all.41 = bf16[32,20,1536]{2,1,0:T(8,128)(2,1)} all-to-all(bf16[32,20,1536]{2,1,0:T(8,128)(2,1)S(1)} %all_to_all.31), channel_id=1, replica_groups=mesh['seq'=32,'tp'=4] {'seq'}, dimensions={0} | all-to-all | bytes 3932160 | tf_op jit(solution)/shard_map/all_to_all | solution.py:144
  369.9 2.8 all_to_all.33
  374.3 5.2 %all-to-all-start.2 = ((bf16[640,4,384]{2,0,1:T(8,128)(2,1)}), bf16[640,4,384]{2,0,1:T(8,128)(2,1)S(1)}, u32[]{:S(2)}, u32[]{:S(2)}) async-start(bf16[640,4,384]{2,0,1:T(8,128)(2,1)} %copy.140), calls=%async_computation.2 | async-start | bytes 3932160 | tf_op jit(solution)/shard_map/all_to_all | solution.py:145
  380.7 23.6 %all-to-all-done.2 = bf16[640,4,384]{2,0,1:T(8,128)(2,1)S(1)} async-done(((bf16[640,4,384]{2,0,1:T(8,128)(2,1)}), bf16[640,4,384]{2,0,1:T(8,128)(2,1)S(1)}, u32[]{:S(2)}, u32[]{:S(2)}) %all-to-all-start.2) | async-done | bytes 1966112 | tf_op jit(solution)/shard_map/all_to_all | solution.py:145
  404.3 9.0 %gather_fusion.1 = bf16[2048,384]{1,0:T(8,128)(2,1)} fusion(bf16[2560,384]{1,0:T(8,128)(2,1)S(1)} %bitcast.110, s32[2048]{0:T(1024)S(1)} %broadcast_clamp_fusion), kind=kCustom, calls=%fused_computation.1 | custom fusion | bytes 3153920 | tf_op jit(solution)/shard_map/gather | solution.py:147
  413.3 4.4 %reshape.972 = f32[512,4,384]{2,1,0:T(4,128)} reshape(bf16[2048,384]{1,0:T(8,128)(2,1)} %gather_fusion.1) | data formatting | bytes 4718592 | tf_op jit(solution)/shard_map/convert_element_type | solution.py:147
  417.7 4.6 %multiply_reduce_fusion = f32[512,384]{1,0:T(8,128)S(1)} fusion(f32[512,4,384]{2,1,0:T(4,128)} %reshape.972, f32[512,4]{1,0:T(8,128)S(1)} %copy.142), kind=kLoop, calls=%fused_computation.11 | loop fusion | flops 1376256 | bytes 3940352 | tf_op jit(solution)/shard_map/reduce_sum | solution.py:148
  422.3 2.0 add_convert_fusion
  (113 shorter events, 40.5 us)
Async XLA Ops:
  7.2 2.0 copy-start
  7.2 201.3 %all-reduce.3.cloned.1.call-start = ((), (), s32[]{:S(2)}) async-start(), calls=%async_computation.3 | async-start | bytes 3145728 | tf_op jit(solution)/shard_map/psum | solution.py:131
  9.2 25.3 %copy-start.7 = (s32[512]{0:T(512)S(1)}, s32[512]{0:T(512)}, u32[]{:S(2)}) copy-start(s32[512]{0:T(512)} %param.14) | copy-start | bytes 6148
  9.2 89.0 %copy-start.2 = (bf16[512,1536]{1,0:T(8,128)(2,1)S(1)}, bf16[512,1536]{1,0:T(8,128)(2,1)}, u32[]{:S(2)}) copy-start(bf16[512,1536]{1,0:T(8,128)(2,1)} %param.13) | copy-start | bytes 4718596
  9.2 89.0 %copy-start.10 = (f32[1536]{0:T(1024)S(1)}, f32[1536]{0:T(1024)}, u32[]{:S(2)}) copy-start(f32[1536]{0:T(1024)} %param.15) | copy-start | bytes 18436
  12.6 91.6 %collective-permute-start.6 = (bf16[512,256]{1,0:T(8,128)(2,1)}, bf16[512,256]{1,0:T(8,128)(2,1)}, u32[]{:S(2)}, u32[]{:S(2)}) collective-permute-start(bf16[512,256]{1,0:T(8,128)(2,1)} %pad_maximum_fusion), channel_id=1, source_target_pairs={{0,28},{4,32},{8,36},{12,40},{16,44},{20,48},{24,52},{28,56},{32,6... | collective-permute-start | bytes 786440 | tf_op jit(solution)/shard_map/ppermute | solution.py:18
  19.5 87.7 %collective-permute-start.5 = (bf16[512,256]{1,0:T(8,128)(2,1)}, bf16[512,256]{1,0:T(8,128)(2,1)}, u32[]{:S(2)}, u32[]{:S(2)}) collective-permute-start(bf16[512,256]{1,0:T(8,128)(2,1)} %pad_maximum_fusion), channel_id=1, source_target_pairs={{0,24},{4,28},{8,32},{12,36},{16,40},{20,44},{24,48},{28,52},{32,5... | collective-permute-start | bytes 786440 | tf_op jit(solution)/shard_map/ppermute | solution.py:18
  24.0 86.1 %collective-permute-start.4 = (bf16[512,256]{1,0:T(8,128)(2,1)}, bf16[512,256]{1,0:T(8,128)(2,1)}, u32[]{:S(2)}, u32[]{:S(2)}) collective-permute-start(bf16[512,256]{1,0:T(8,128)(2,1)} %pad_maximum_fusion), channel_id=1, source_target_pairs={{0,20},{4,24},{8,28},{12,32},{16,36},{20,40},{24,44},{28,48},{32,5... | collective-permute-start | bytes 786440 | tf_op jit(solution)/shard_map/ppermute | solution.py:18
  27.4 85.8 %collective-permute-start.3 = (bf16[512,256]{1,0:T(8,128)(2,1)}, bf16[512,256]{1,0:T(8,128)(2,1)}, u32[]{:S(2)}, u32[]{:S(2)}) collective-permute-start(bf16[512,256]{1,0:T(8,128)(2,1)} %pad_maximum_fusion), channel_id=1, source_target_pairs={{0,16},{4,20},{8,24},{12,28},{16,32},{20,36},{24,40},{28,44},{32,4... | collective-permute-start | bytes 786440 | tf_op jit(solution)/shard_map/ppermute | solution.py:18
  31.8 83.1 %collective-permute-start.2 = (bf16[512,256]{1,0:T(8,128)(2,1)}, bf16[512,256]{1,0:T(8,128)(2,1)}, u32[]{:S(2)}, u32[]{:S(2)}) collective-permute-start(bf16[512,256]{1,0:T(8,128)(2,1)} %pad_maximum_fusion), channel_id=1, source_target_pairs={{0,12},{4,16},{8,20},{12,24},{16,28},{20,32},{24,36},{28,40},{32,4... | collective-permute-start | bytes 786440 | tf_op jit(solution)/shard_map/ppermute | solution.py:18
  104.2 12.3 %collective-permute-start.1 = (bf16[512,256]{1,0:T(8,128)(2,1)}, bf16[512,256]{1,0:T(8,128)(2,1)S(1)}, u32[]{:S(2)}, u32[]{:S(2)}) collective-permute-start(bf16[512,256]{1,0:T(8,128)(2,1)} %pad_maximum_fusion), channel_id=1, source_target_pairs={{0,8},{4,12},{8,16},{12,20},{16,24},{20,28},{24,32},{28,36},{32,40... | collective-permute-start | bytes 786440 | tf_op jit(solution)/shard_map/ppermute | solution.py:18
  107.2 10.1 %collective-permute-start = (bf16[512,256]{1,0:T(8,128)(2,1)}, bf16[512,256]{1,0:T(8,128)(2,1)S(1)}, u32[]{:S(2)}, u32[]{:S(2)}) collective-permute-start(bf16[512,256]{1,0:T(8,128)(2,1)} %pad_maximum_fusion), channel_id=1, source_target_pairs={{0,4},{4,8},{8,12},{12,16},{16,20},{20,24},{24,28},{28,32},{32,36}... | collective-permute-start | bytes 786440 | tf_op jit(solution)/shard_map/ppermute | solution.py:18
  110.2 7.8 %collective-permute-start.7 = (bf16[512,256]{1,0:T(8,128)(2,1)}, bf16[512,256]{1,0:T(8,128)(2,1)S(1)}, u32[]{:S(2)}, u32[]{:S(2)}) collective-permute-start(bf16[512,256]{1,0:T(8,128)(2,1)} %pad_maximum_fusion), channel_id=1, source_target_pairs={{0,32},{4,36},{8,40},{12,44},{16,48},{20,52},{24,56},{28,60},{32,6... | collective-permute-start | bytes 786440 | tf_op jit(solution)/shard_map/ppermute | solution.py:18
  136.2 1.4 copy-start.4
  137.6 4.3 copy-start.6
  139.8 124.4 %all-gather.10.cloned.1.call-start = ((), (), s32[]{:S(2)}) async-start(), calls=%async_computation.5 | async-start | bytes 2949120 | tf_op jit(solution)/shard_map/all_gather | solution.py:138
  140.6 151.4 %all-gather.12.cloned.1.call-start = ((), (), s32[]{:S(2)}) async-start(), calls=%async_computation.6 | async-start | bytes 2949120 | tf_op jit(solution)/shard_map/all_gather | solution.py:139
  141.3 179.7 %all-gather.8.cloned.1.call-start = ((), (), s32[]{:S(2)}) async-start(), calls=%async_computation.4 | async-start | bytes 2949120 | tf_op jit(solution)/shard_map/all_gather | solution.py:137
  150.9 61.3 %copy-start.8 = (f32[1536]{0:T(1024)S(1)}, f32[1536]{0:T(1024)}, u32[]{:S(2)}) copy-start(f32[1536]{0:T(1024)} %param.19) | copy-start | bytes 18436
  208.5 3.7 copy-start.3
  374.3 5.5 %copy-start.9 = (f32[512,4]{0,1:T(4,128)S(1)}, f32[512,4]{0,1:T(4,128)}, u32[]{:S(2)}) copy-start(f32[512,4]{0,1:T(4,128)} %param.24) | copy-start | bytes 24580
  374.3 5.7 %copy-start.11 = (s32[4]{0:T(128)S(1)}, s32[4]{0:T(128)}, u32[]{:S(2)}) copy-start(s32[4]{0:T(128)} %param.25) | copy-start | bytes 52
  374.3 30.0 %all-to-all-start.2 = ((bf16[640,4,384]{2,0,1:T(8,128)(2,1)}), bf16[640,4,384]{2,0,1:T(8,128)(2,1)S(1)}, u32[]{:S(2)}, u32[]{:S(2)}) async-start(bf16[640,4,384]{2,0,1:T(8,128)(2,1)} %copy.140), calls=%async_computation.2 | async-start | bytes 3932160 | tf_op jit(solution)/shard_map/all_to_all | solution.py:145
  380.7 32.6 %copy-start.5 = (bf16[4,128,128]{2,1,0:T(8,128)(2,1)}, bf16[4,128,128]{2,1,0:T(8,128)(2,1)S(1)}, u32[]{:S(2)}) copy-start(bf16[4,128,128]{2,1,0:T(8,128)(2,1)S(1)} %scatter_fusion) | copy-start | bytes 393220
  413.3 10.9 %copy-start.1 = (bf16[1536,512]{1,0:T(8,128)(2,1)S(1)}, bf16[1536,512]{1,0:T(8,128)(2,1)}, u32[]{:S(2)}) copy-start(bf16[1536,512]{1,0:T(8,128)(2,1)} %param.17) | copy-start | bytes 4718596
Sparse Core Ops, SparseCore 0:
  139.9 68.5 all-reduce.2
  210.1 52.7 all-gather.9
  264.6 27.2 all-gather.11
  293.5 27.4 all-gather.7

commit v2 on v1

--- a/solution.py
+++ b/solution.py
@@ -79,21 +79,25 @@
     value_head = lax.dynamic_slice_in_dim(keyval, (HK + group) * HD, HD, 1)
     query_heads = queries.reshape(count, heads, HD)
     query_index = seq_index * count + jnp.arange(count, dtype=jnp.int32)
-    all_segments = lax.all_gather(segment_ids, "seq", tiled=True)
-    own_piece = jnp.concatenate([key_head, value_head], axis=1)
+    width = 2 * HD
+    code_rows = 2 * count // width
+    code = jnp.stack([segment_ids // 256, segment_ids % 256]).astype(jnp.bfloat16).reshape(code_rows, width)
+    code = jnp.concatenate([code, jnp.zeros((16 - code_rows % 16, width), jnp.bfloat16)], axis=0)
+    own_piece = jnp.concatenate([jnp.concatenate([key_head, value_head], axis=1), code], axis=0)
     reach_steps = lax.axis_size("seq") // 4
     pieces = [own_piece] + [shifted(own_piece, "seq", number) for number in range(1, reach_steps + 1)]
 
     def visit(carry, piece, number):
         start = (seq_index - number) * count
         key_index = start + jnp.arange(count, dtype=jnp.int32)
-        segment_piece = lax.dynamic_slice_in_dim(all_segments, jnp.maximum(start, 0), count)
+        coded = piece[count : count + code_rows].reshape(2, count).astype(jnp.int32)
+        segment_piece = coded[0] * 256 + coded[1]
         allowed = (
             (segment_piece[None, :] == segment_ids[:, None])
             & (key_index[None, :] <= query_index[:, None])
             & (key_index[None, :] >= 0)
         )
-        return attend_block(carry, query_heads, piece[:, :HD], piece[:, HD:], allowed)
+        return attend_block(carry, query_heads, piece[:count, :HD], piece[:count, HD:], allowed)
 
     state = (
         jnp.full((count, heads), NEGATIVE, jnp.float32),
@@ -103,6 +107,13 @@
     for number, piece in enumerate(pieces):
         state = visit(state, piece, number)
     attended = (state[2] / state[1][:, :, None]).astype(jnp.bfloat16).reshape(count, heads * HD)
+    hidden_part = w_gate.shape[2]
+    packed = jnp.concatenate([w_gate[0], w_up[0], w_down[0].T], axis=1)
+    weight_parts = [packed] + [
+        lax.ppermute(packed, "tp", [(source, (source + number) % tp_count) for source in range(tp_count)])
+        for number in range(1, tp_count)
+    ]
+    attended, weight_parts = lax.optimization_barrier((attended, weight_parts))
     projected = jnp.dot(attended, w_out, preferred_element_type=jnp.float32)
     experts = lax.axis_size("seq") * w_gate.shape[0]
     choose = expert_picks.shape[1]
@@ -134,9 +145,9 @@
     columns = mixed_in.shape[1]
     padded = jnp.concatenate([mixed_in, jnp.zeros((1, columns), jnp.bfloat16)], axis=0)
     arrived = lax.all_to_all(padded[table], "seq", split_axis=0, concat_axis=0, tiled=True)
-    gate_full = lax.all_gather(w_gate[0], "tp", axis=1, tiled=True)
-    up_full = lax.all_gather(w_up[0], "tp", axis=1, tiled=True)
-    down_full = lax.all_gather(w_down[0], "tp", axis=0, tiled=True)
+    gate_full = jnp.concatenate([part[:, :hidden_part] for part in weight_parts], axis=1)
+    up_full = jnp.concatenate([part[:, hidden_part : 2 * hidden_part] for part in weight_parts], axis=1)
+    down_full = jnp.concatenate([part[:, 2 * hidden_part :] for part in weight_parts], axis=1).T
     gate_part = jnp.dot(arrived, gate_full, preferred_element_type=jnp.float32)
     up_part = jnp.dot(arrived, up_full, preferred_element_type=jnp.float32)
     hidden = (jax.nn.relu(gate_part) * up_part).astype(jnp.bfloat16)

time: 437 us -> 365 us (0.84)
  blocking collectives: 144 us -> 36.4 us
  starting transfers between devices: 31.1 us -> 48.9 us
  local copies, waits for them, and re-layouts: 39.1 us -> 49.2 us
  other arithmetic: 23.1 us -> 28.3 us
    all_gather x1 -> x0, blocking collectives: 63.7 us -> none  [per_device(): all_segments = lax.all_gather(segment_ids, 'seq', tiled=True)]
    all_gather x3 -> x0, waiting for transfers between devices: 52.2 us -> none  [the longest x1 29.1 us: per_device(): gate_full = lax.all_gather(w_gate[0], 'tp', axis=1, tiled=True)]
    all_to_all x1 -> x0, blocking collectives: 42.5 us -> none  [per_device(): lax.all_to_all(padded[table], 'seq', split_axis=0, concat_axis=0, tiled=T...]
    ppermute x0 -> x3, waiting for transfers between devices: none -> 29.3 us  [per_device(): lax.ppermute(packed, 'tp', [(source, (source + number) % tp_count) for so...]
    all_to_all x0 -> x1, waiting for transfers between devices: none -> 23.1 us  [per_device(): lax.all_to_all(padded[table], 'seq', split_axis=0, concat_axis=0, tiled=T...]
    ppermute x8, waiting for transfers between devices: 0.02 us -> 11.1 us  [shifted(): lax.ppermute(value, axis, [(source, source + steps) for source in range(l...]
    psum x1, waiting for transfers between devices: 57.6 us -> 47 us  [per_device(): summed = lax.psum(projected.astype(jnp.bfloat16), 'tp').astype(jnp.float32)]
    slice x0 -> x4, local copies, waits for them, and re-layouts: none -> 9.27 us  [per_device(): part[:, hidden_part:2 * hidden_part]]
  transfers between devices with their start and end apart: 13 -> 14, of which waited for: 4 -> 5; matrix products, arithmetic and copies ran while one was open for 9% -> 17% of each run, Pallas kernels for 0% -> 0%
where the time goes in v2:
time: 365 us; the launch traced here: 359 us
  waiting for transfers between devices  134 us (37%)
  local copies, waits for them, and re-layouts  49.2 us (13%)
  starting transfers between devices  48.9 us (13%)
  matrix products  46.5 us (13%)
  blocking collectives  36.4 us (10%)
  other arithmetic  28.3 us (8%)
  between operations  15.4 us (4%)
    psum x1, waiting for transfers between devices, per_device(): summed = lax.psum(projected.astype(jnp.bfloat16), 'tp').astype(jnp.float32)  47 us
    all_to_all x1, blocking collectives, per_device(): lax.all_to_all(expert_out, 'seq', split_axis=0, concat_axis=0, tiled=True)  36.4 us
    ppermute x8, starting transfers between devices, shifted(): lax.ppermute(value, axis, [(source, source + steps) for source in range(l...  29.5 us
    ppermute x3, waiting for transfers between devices, per_device(): lax.ppermute(packed, 'tp', [(source, (source + number) % tp_count) for so...  29.3 us
    all_to_all x1, waiting for transfers between devices, per_device(): lax.all_to_all(returned, 'tp', split_axis=1, concat_axis=0, tiled=True)  23.6 us
    all_to_all x1, waiting for transfers between devices, per_device(): lax.all_to_all(padded[table], 'seq', split_axis=0, concat_axis=0, tiled=T...  23.1 us
    dot_general x9, matrix products, attend_block(): jnp.einsum('qhk,kd->qhd', weights.astype(jnp.bfloat16), value_block, pref...  15.2 us
    ppermute x8, waiting for transfers between devices, shifted(): lax.ppermute(value, axis, [(source, source + steps) for source in range(l...  11.1 us
  transfers between devices with their start and end apart: 14, of which 5 were waited for; matrix products, arithmetic and copies ran while one was open for 17% of the time, Pallas kernels for 0%

profile of v2, /device:TPU:1, one launch (start us, length us, event | category | flops | bytes accessed | tf_op | source)
XLA Modules:
  0.0 358.7 jit_solution(6473571595825198180)
XLA Ops:
  10.0 2.6 convolution_convert_fusion.2
  12.8 5.7 %collective-permute-start.2 = (bf16[528,256]{1,0:T(8,128)(2,1)S(1)}, bf16[528,256]{1,0:T(8,128)(2,1)}, u32[]{:S(2)}, u32[]{:S(2)}) collective-permute-start(bf16[528,256]{1,0:T(8,128)(2,1)S(1)} %maximum_maximum_fusion), channel_id=1, source_target_pairs={{0,12},{4,16},{8,20},{12,24},{16,28},{20,32},{24,36},{28,40},{32,4... | collective-permute-start | bytes 811016 | tf_op jit(solution)/shard_map/ppermute | solution.py:18
  18.5 4.4 %collective-permute-start.3 = (bf16[528,256]{1,0:T(8,128)(2,1)S(1)}, bf16[528,256]{1,0:T(8,128)(2,1)}, u32[]{:S(2)}, u32[]{:S(2)}) collective-permute-start(bf16[528,256]{1,0:T(8,128)(2,1)S(1)} %maximum_maximum_fusion), channel_id=1, source_target_pairs={{0,16},{4,20},{8,24},{12,28},{16,32},{20,36},{24,40},{28,44},{32,4... | collective-permute-start | bytes 811016 | tf_op jit(solution)/shard_map/ppermute | solution.py:18
  22.8 5.2 %collective-permute-start.4 = (bf16[528,256]{1,0:T(8,128)(2,1)S(1)}, bf16[528,256]{1,0:T(8,128)(2,1)}, u32[]{:S(2)}, u32[]{:S(2)}) collective-permute-start(bf16[528,256]{1,0:T(8,128)(2,1)S(1)} %maximum_maximum_fusion), channel_id=1, source_target_pairs={{0,20},{4,24},{8,28},{12,32},{16,36},{20,40},{24,44},{28,48},{32,5... | collective-permute-start | bytes 811016 | tf_op jit(solution)/shard_map/ppermute | solution.py:18
  28.0 4.1 %collective-permute-start.5 = (bf16[528,256]{1,0:T(8,128)(2,1)S(1)}, bf16[528,256]{1,0:T(8,128)(2,1)}, u32[]{:S(2)}, u32[]{:S(2)}) collective-permute-start(bf16[528,256]{1,0:T(8,128)(2,1)S(1)} %maximum_maximum_fusion), channel_id=1, source_target_pairs={{0,24},{4,28},{8,32},{12,36},{16,40},{20,44},{24,48},{28,52},{32,5... | collective-permute-start | bytes 811016 | tf_op jit(solution)/shard_map/ppermute | solution.py:18
  32.2 2.7 collective-permute-start.6
  38.8 3.6 %collective-permute-start = (bf16[528,256]{1,0:T(8,128)(2,1)S(1)}, bf16[528,256]{1,0:T(8,128)(2,1)S(1)}, u32[]{:S(2)}, u32[]{:S(2)}) collective-permute-start(bf16[528,256]{1,0:T(8,128)(2,1)S(1)} %maximum_maximum_fusion), channel_id=1, source_target_pairs={{0,4},{4,8},{8,12},{12,16},{16,20},{20,24},{24,28},{28,32},{32,36}... | collective-permute-start | bytes 811016 | tf_op jit(solution)/shard_map/ppermute | solution.py:18
  43.1 2.5 collective-permute-start.1
  48.3 2.7 collective-permute-start.10
  51.7 2.8 collective-permute-start.8
  56.1 11.1 %collective-permute-done.7 = bf16[528,256]{1,0:T(8,128)(2,1)S(1)} collective-permute-done((bf16[528,256]{1,0:T(8,128)(2,1)S(1)}, bf16[528,256]{1,0:T(8,128)(2,1)S(1)}, u32[]{:S(2)}, u32[]{:S(2)}) %collective-permute-start.7) | collective-permute-done | bytes 270368 | tf_op jit(solution)/shard_map/ppermute | solution.py:18
  103.2 29.3 %collective-permute-done.9 = bf16[1536,576]{0,1:T(8,128)(2,1)} collective-permute-done((bf16[1536,576]{0,1:T(8,128)(2,1)S(1)}, bf16[1536,576]{0,1:T(8,128)(2,1)}, u32[]{:S(2)}, u32[]{:S(2)}) %collective-permute-start.9) | collective-permute-done | bytes 1769504 | tf_op jit(solution)/shard_map/ppermute | solution.py:113
  135.6 8.0 %scatter_custom_fusion = s32[640]{0:T(1024)S(1)} fusion(s32[2048]{0:T(1024)S(1)} %bitcast.153, s32[2048]{0:T(1024)S(1)} %reshape.1029, s32[]{:T(128)} %constant.63.clone.1), kind=kCustom, calls=%fused_computation.251 | custom fusion | bytes 2564 | tf_op jit(solution)/shard_map/scatter | solution.py:139
  143.7 47.0 %all-reduce.3.cloned.1.call-done = bf16[512,1536]{1,0:T(8,128)(2,1)} async-done(((bf16[512,1536]{1,0:T(8,128)(2,1)}), bf16[512,1536]{1,0:T(8,128)(2,1)}) %all-reduce.3.cloned.1.call-update) | async-done | bytes 1572880 | tf_op jit(solution)/shard_map/psum | solution.py:142
  190.7 3.7 %convert_add_fusion = (f32[512,1536]{1,0:T(8,128)}, f32[512]{0:T(512)S(1)}) fusion(bf16[512,1536]{1,0:T(8,128)(2,1)S(1)} %copy-done.2, bf16[512,1536]{1,0:T(8,128)(2,1)} %all-reduce.3.cloned.1.call-done), kind=kLoop, calls=%fused_computation.4 | loop fusion | flops 3931648 | bytes 6293504 | tf_op jit(solution)/shard_map/add | solution.py:143
  195.1 3.7 %gather_fusion = bf16[640,1536]{1,0:T(8,128)(2,1)} fusion(bf16[513,1536]{1,0:T(8,128)(2,1)S(1)} %concatenate.24, s32[1024]{0:T(1024)S(1)} %pad_clamp_fusion), kind=kCustom, calls=%fused_computation | custom fusion | bytes 3934720 | tf_op jit(solution)/shard_map/gather | solution.py:147
  198.8 3.9 %all_to_all.28 = bf16[32,20,1536]{2,1,0:T(8,128)(2,1)} reshape(bf16[640,1536]{1,0:T(8,128)(2,1)} %gather_fusion) | data formatting | bytes 3932160 | tf_op jit(solution)/shard_map/all_to_all | solution.py:147
  202.8 7.2 %all-to-all-start = ((bf16[32,20,1536]{2,1,0:T(8,128)(2,1)}), bf16[32,20,1536]{2,1,0:T(8,128)(2,1)S(1)}, u32[]{:S(2)}, u32[]{:S(2)}) async-start(bf16[32,20,1536]{2,1,0:T(8,128)(2,1)} %all_to_all.28), calls=%async_computation | async-start | bytes 4718592 | tf_op jit(solution)/shard_map/all_to_all | solution.py:147
  210.0 2.6 fusion.214
  212.6 2.8 fusion.215
  215.3 2.7 fusion.216
  219.3 23.1 %all-to-all-done = bf16[32,20,1536]{2,1,0:T(8,128)(2,1)S(1)} async-done(((bf16[32,20,1536]{2,1,0:T(8,128)(2,1)}), bf16[32,20,1536]{2,1,0:T(8,128)(2,1)S(1)}, u32[]{:S(2)}, u32[]{:S(2)}) %all-to-all-start) | async-done | bytes 1966112 | tf_op jit(solution)/shard_map/all_to_all | solution.py:147
  244.4 5.3 %fusion.21 = f32[640,768]{1,0:T(8,128)} fusion(bf16[640,1536]{1,0:T(8,128)(2,1)} %all_to_all.30, bf16[1536,192]{0,1:T(8,128)(2,1)} %get-tuple-element.44, bf16[1536,192]{0,1:T(8,128)(2,1)} %get-tuple-element.41, bf16[1536,192]{0,1:T(8,128)(2,1)} %get-tuple-element.38, bf16[1536,192]{0,1:T(8,128)(2,1)} %get-tuple-element.35), kind=kOutput, calls=%fused_computation.51 | convolution fusion | flops 1519386624 | bytes 6291456 | tf_op jit(solution)/shard_map/dot_general | solution.py:151
  249.7 7.9 %convolution_convert_fusion = bf16[640,1536]{1,0:T(8,128)(2,1)} fusion(bf16[1536,192]{0,1:T(8,128)(2,1)} %get-tuple-element.43, bf16[1536,192]{0,1:T(8,128)(2,1)} %get-tuple-element.40, bf16[1536,192]{0,1:T(8,128)(2,1)} %get-tuple-element.37, bf16[1536,192]{0,1:T(8,128)(2,1)} %get-tuple-element.34, f32[640,768]{1,0:T(8,128)} %fusion.21, ...), kind=kOutput, calls=%fused_computation.7 | convolution fusion | flops 3041230848 | bytes 10616832 | tf_op jit(solution)/shard_map/dot_general | solution.py:154
  257.6 2.5 all_to_all.31
  260.1 36.4 %all_to_all.40 = bf16[32,20,1536]{2,1,0:T(8,128)(2,1)} all-to-all(bf16[32,20,1536]{2,1,0:T(8,128)(2,1)S(1)} %all_to_all.31), channel_id=1, replica_groups=mesh['seq'=32,'tp'=4] {'seq'}, dimensions={0} | all-to-all | bytes 3932160 | tf_op jit(solution)/shard_map/all_to_all | solution.py:155
  296.5 2.8 all_to_all.33
  300.8 5.8 %all-to-all-start.2 = ((bf16[640,4,384]{2,0,1:T(8,128)(2,1)}), bf16[640,4,384]{2,0,1:T(8,128)(2,1)S(1)}, u32[]{:S(2)}, u32[]{:S(2)}) async-start(bf16[640,4,384]{2,0,1:T(8,128)(2,1)} %copy.140), calls=%async_computation.2 | async-start | bytes 3932160 | tf_op jit(solution)/shard_map/all_to_all | solution.py:156
  307.9 23.6 %all-to-all-done.2 = bf16[640,4,384]{2,0,1:T(8,128)(2,1)S(1)} async-done(((bf16[640,4,384]{2,0,1:T(8,128)(2,1)}), bf16[640,4,384]{2,0,1:T(8,128)(2,1)S(1)}, u32[]{:S(2)}, u32[]{:S(2)}) %all-to-all-start.2) | async-done | bytes 1966112 | tf_op jit(solution)/shard_map/all_to_all | solution.py:156
  331.5 9.0 %gather_fusion.1 = bf16[2048,384]{1,0:T(8,128)(2,1)} fusion(bf16[2560,384]{1,0:T(8,128)(2,1)S(1)} %bitcast.127, s32[2048]{0:T(1024)S(1)} %broadcast_clamp_fusion), kind=kCustom, calls=%fused_computation.1 | custom fusion | bytes 3153920 | tf_op jit(solution)/shard_map/gather | solution.py:158
  340.5 4.4 %reshape.1045 = f32[512,4,384]{2,1,0:T(4,128)} reshape(bf16[2048,384]{1,0:T(8,128)(2,1)} %gather_fusion.1) | data formatting | bytes 4718592 | tf_op jit(solution)/shard_map/convert_element_type | solution.py:158
  344.9 4.6 %multiply_reduce_fusion = f32[512,384]{1,0:T(8,128)S(1)} fusion(f32[512,4,384]{2,1,0:T(4,128)} %reshape.1045, f32[512,4]{1,0:T(8,128)S(1)} %copy.142), kind=kLoop, calls=%fused_computation.11 | loop fusion | flops 1376256 | bytes 3940352 | tf_op jit(solution)/shard_map/reduce_sum | solution.py:159
  (160 shorter events, 59.7 us)
Async XLA Ops:
  7.2 183.5 %all-reduce.3.cloned.1.call-start = ((), (), s32[]{:S(2)}) async-start(), calls=%async_computation.3 | async-start | bytes 3145728 | tf_op jit(solution)/shard_map/psum | solution.py:142
  10.0 25.2 %copy-start.2 = (bf16[512,1536]{1,0:T(8,128)(2,1)S(1)}, bf16[512,1536]{1,0:T(8,128)(2,1)}, u32[]{:S(2)}) copy-start(bf16[512,1536]{1,0:T(8,128)(2,1)} %param.13) | copy-start | bytes 4718596
  10.0 25.2 %copy-start.18 = (f32[1536]{0:T(1024)S(1)}, f32[1536]{0:T(1024)}, u32[]{:S(2)}) copy-start(f32[1536]{0:T(1024)} %param.15) | copy-start | bytes 18436
  12.5 24.8 %copy-start.9 = (bf16[1,192,1536]{2,1,0:T(8,128)(2,1)S(1)}, bf16[1,192,1536]{2,1,0:T(8,128)(2,1)}, u32[]{:S(2)}) copy-start(bf16[1,192,1536]{2,1,0:T(8,128)(2,1)} %param.22) | copy-start | bytes 1769476
  12.8 26.0 %collective-permute-start.2 = (bf16[528,256]{1,0:T(8,128)(2,1)S(1)}, bf16[528,256]{1,0:T(8,128)(2,1)}, u32[]{:S(2)}, u32[]{:S(2)}) collective-permute-start(bf16[528,256]{1,0:T(8,128)(2,1)S(1)} %maximum_maximum_fusion), channel_id=1, source_target_pairs={{0,12},{4,16},{8,20},{12,24},{16,28},{20,32},{24,36},{28,40},{32,4... | collective-permute-start | bytes 811016 | tf_op jit(solution)/shard_map/ppermute | solution.py:18
  18.5 24.6 %collective-permute-start.3 = (bf16[528,256]{1,0:T(8,128)(2,1)S(1)}, bf16[528,256]{1,0:T(8,128)(2,1)}, u32[]{:S(2)}, u32[]{:S(2)}) collective-permute-start(bf16[528,256]{1,0:T(8,128)(2,1)S(1)} %maximum_maximum_fusion), channel_id=1, source_target_pairs={{0,16},{4,20},{8,24},{12,28},{16,32},{20,36},{24,40},{28,44},{32,4... | collective-permute-start | bytes 811016 | tf_op jit(solution)/shard_map/ppermute | solution.py:18
  22.8 23.5 %collective-permute-start.4 = (bf16[528,256]{1,0:T(8,128)(2,1)S(1)}, bf16[528,256]{1,0:T(8,128)(2,1)}, u32[]{:S(2)}, u32[]{:S(2)}) collective-permute-start(bf16[528,256]{1,0:T(8,128)(2,1)S(1)} %maximum_maximum_fusion), channel_id=1, source_target_pairs={{0,20},{4,24},{8,28},{12,32},{16,36},{20,40},{24,44},{28,48},{32,5... | collective-permute-start | bytes 811016 | tf_op jit(solution)/shard_map/ppermute | solution.py:18
  28.0 20.3 %collective-permute-start.5 = (bf16[528,256]{1,0:T(8,128)(2,1)S(1)}, bf16[528,256]{1,0:T(8,128)(2,1)}, u32[]{:S(2)}, u32[]{:S(2)}) collective-permute-start(bf16[528,256]{1,0:T(8,128)(2,1)S(1)} %maximum_maximum_fusion), channel_id=1, source_target_pairs={{0,24},{4,28},{8,32},{12,36},{16,40},{20,44},{24,48},{28,52},{32,5... | collective-permute-start | bytes 811016 | tf_op jit(solution)/shard_map/ppermute | solution.py:18
  32.2 19.5 %collective-permute-start.6 = (bf16[528,256]{1,0:T(8,128)(2,1)S(1)}, bf16[528,256]{1,0:T(8,128)(2,1)}, u32[]{:S(2)}, u32[]{:S(2)}) collective-permute-start(bf16[528,256]{1,0:T(8,128)(2,1)S(1)} %maximum_maximum_fusion), channel_id=1, source_target_pairs={{0,28},{4,32},{8,36},{12,40},{16,44},{20,48},{24,52},{28,56},{32,6... | collective-permute-start | bytes 811016 | tf_op jit(solution)/shard_map/ppermute | solution.py:18
  35.2 32.1 %copy-start.15 = (s32[512]{0:T(512)S(1)}, s32[512]{0:T(512)}, u32[]{:S(2)}) copy-start(s32[512]{0:T(512)} %param.14) | copy-start | bytes 6148
  38.8 32.4 %copy-start.3 = (bf16[1536,576]{0,1:T(8,128)(2,1)}, bf16[1536,576]{0,1:T(8,128)(2,1)S(1)}, u32[]{:S(2)}) copy-start(bf16[1536,576]{0,1:T(8,128)(2,1)S(1)} %pad_maximum_fusion) | copy-start | bytes 5308420
  38.8 16.4 %collective-permute-start = (bf16[528,256]{1,0:T(8,128)(2,1)S(1)}, bf16[528,256]{1,0:T(8,128)(2,1)S(1)}, u32[]{:S(2)}, u32[]{:S(2)}) collective-permute-start(bf16[528,256]{1,0:T(8,128)(2,1)S(1)} %maximum_maximum_fusion), channel_id=1, source_target_pairs={{0,4},{4,8},{8,12},{12,16},{16,20},{20,24},{24,28},{28,32},{32,36}... | collective-permute-start | bytes 811016 | tf_op jit(solution)/shard_map/ppermute | solution.py:18
  43.1 12.9 %collective-permute-start.1 = (bf16[528,256]{1,0:T(8,128)(2,1)S(1)}, bf16[528,256]{1,0:T(8,128)(2,1)S(1)}, u32[]{:S(2)}, u32[]{:S(2)}) collective-permute-start(bf16[528,256]{1,0:T(8,128)(2,1)S(1)} %maximum_maximum_fusion), channel_id=1, source_target_pairs={{0,8},{4,12},{8,16},{12,20},{16,24},{20,28},{24,32},{28,36},{32,40... | collective-permute-start | bytes 811016 | tf_op jit(solution)/shard_map/ppermute | solution.py:18
  46.3 20.9 %collective-permute-start.7 = (bf16[528,256]{1,0:T(8,128)(2,1)S(1)}, bf16[528,256]{1,0:T(8,128)(2,1)S(1)}, u32[]{:S(2)}, u32[]{:S(2)}) collective-permute-start(bf16[528,256]{1,0:T(8,128)(2,1)S(1)} %maximum_maximum_fusion), channel_id=1, source_target_pairs={{0,32},{4,36},{8,40},{12,44},{16,48},{20,52},{24,56},{28,60},{32,6... | collective-permute-start | bytes 811016 | tf_op jit(solution)/shard_map/ppermute | solution.py:18
  48.3 54.8 %collective-permute-start.10 = (bf16[1536,576]{0,1:T(8,128)(2,1)S(1)}, bf16[1536,576]{0,1:T(8,128)(2,1)S(1)}, u32[]{:S(2)}, u32[]{:S(2)}) collective-permute-start(bf16[1536,576]{0,1:T(8,128)(2,1)S(1)} %pad_maximum_fusion), channel_id=1, source_target_pairs={{0,3},{1,0},{2,1},{3,2},{4,7},{5,4},{6,5},{7,6},{8,11},{9,8},{10,9... | collective-permute-start | bytes 5308424 | tf_op jit(solution)/shard_map/ppermute | solution.py:113
  51.7 51.5 %collective-permute-start.8 = (bf16[1536,576]{0,1:T(8,128)(2,1)S(1)}, bf16[1536,576]{0,1:T(8,128)(2,1)}, u32[]{:S(2)}, u32[]{:S(2)}) collective-permute-start(bf16[1536,576]{0,1:T(8,128)(2,1)S(1)} %pad_maximum_fusion), channel_id=1, source_target_pairs={{0,1},{1,2},{2,3},{3,0},{4,5},{5,6},{6,7},{7,4},{8,9},{9,10},{10,1... | collective-permute-start | bytes 5308424 | tf_op jit(solution)/shard_map/ppermute | solution.py:113
  55.2 24.8 %copy-start.12 = (bf16[528,256]{1,0:T(8,128)(2,1)}, bf16[528,256]{1,0:T(8,128)(2,1)S(1)}, u32[]{:S(2)}) copy-start(bf16[528,256]{1,0:T(8,128)(2,1)S(1)} %collective-permute-done) | copy-start | bytes 811012
  55.2 77.2 %collective-permute-start.9 = (bf16[1536,576]{0,1:T(8,128)(2,1)S(1)}, bf16[1536,576]{0,1:T(8,128)(2,1)}, u32[]{:S(2)}, u32[]{:S(2)}) collective-permute-start(bf16[1536,576]{0,1:T(8,128)(2,1)S(1)} %pad_maximum_fusion), channel_id=1, source_target_pairs={{0,2},{1,3},{2,0},{3,1},{4,6},{5,7},{6,4},{7,5},{8,10},{9,11},{10,... | collective-permute-start | bytes 5308424 | tf_op jit(solution)/shard_map/ppermute | solution.py:113
  56.0 23.2 %copy-start.14 = (bf16[528,256]{1,0:T(8,128)(2,1)}, bf16[528,256]{1,0:T(8,128)(2,1)S(1)}, u32[]{:S(2)}) copy-start(bf16[528,256]{1,0:T(8,128)(2,1)S(1)} %collective-permute-done.1) | copy-start | bytes 811012
  67.2 13.5 %copy-start.13 = (bf16[528,256]{1,0:T(8,128)(2,1)}, bf16[528,256]{1,0:T(8,128)(2,1)S(1)}, u32[]{:S(2)}) copy-start(bf16[528,256]{1,0:T(8,128)(2,1)S(1)} %collective-permute-done.7) | copy-start | bytes 811012
  100.8 31.7 %copy-start.8 = (bf16[384,1536]{1,0:T(8,128)(2,1)S(1)}, bf16[384,1536]{1,0:T(8,128)(2,1)}, u32[]{:S(2)}) copy-start(bf16[384,1536]{1,0:T(8,128)(2,1)} %param.18) | copy-start | bytes 3538948
  103.1 31.5 %copy-start.11 = (s32[512,4]{0,1:T(4,128)S(1)}, s32[512,4]{0,1:T(4,128)}, u32[]{:S(2)}) copy-start(s32[512,4]{0,1:T(4,128)} %param.23) | copy-start | bytes 24580
  103.1 29.3 %copy-start.6 = (bf16[1536,576]{0,1:T(8,128)(2,1)}, bf16[1536,576]{0,1:T(8,128)(2,1)S(1)}, u32[]{:S(2)}) copy-start(bf16[1536,576]{0,1:T(8,128)(2,1)S(1)} %collective-permute-done.10) | copy-start | bytes 5308420
  143.6 50.8 %copy-start.16 = (f32[1536]{0:T(1024)S(1)}, f32[1536]{0:T(1024)}, u32[]{:S(2)}) copy-start(f32[1536]{0:T(1024)} %param.19) | copy-start | bytes 18436
  202.8 39.6 %all-to-all-start = ((bf16[32,20,1536]{2,1,0:T(8,128)(2,1)}), bf16[32,20,1536]{2,1,0:T(8,128)(2,1)S(1)}, u32[]{:S(2)}, u32[]{:S(2)}) async-start(bf16[32,20,1536]{2,1,0:T(8,128)(2,1)} %all_to_all.28), calls=%async_computation | async-start | bytes 4718592 | tf_op jit(solution)/shard_map/all_to_all | solution.py:147
  212.6 5.5 %copy-start.7 = (bf16[1536,576]{0,1:T(8,128)(2,1)S(1)}, bf16[1536,576]{0,1:T(8,128)(2,1)}, u32[]{:S(2)}) copy-start(bf16[1536,576]{0,1:T(8,128)(2,1)} %copy-done.6) | copy-start | bytes 5308420
  244.4 5.3 %copy-start.5 = (bf16[640,1536]{1,0:T(8,128)(2,1)S(1)}, bf16[640,1536]{1,0:T(8,128)(2,1)}, u32[]{:S(2)}) copy-start(bf16[640,1536]{1,0:T(8,128)(2,1)} %all_to_all.30) | copy-start | bytes 5898244
  300.8 6.2 %copy-start.17 = (f32[512,4]{0,1:T(4,128)S(1)}, f32[512,4]{0,1:T(4,128)}, u32[]{:S(2)}) copy-start(f32[512,4]{0,1:T(4,128)} %param.24) | copy-start | bytes 24580
  300.8 6.3 %copy-start.19 = (s32[4]{0:T(128)S(1)}, s32[4]{0:T(128)}, u32[]{:S(2)}) copy-start(s32[4]{0:T(128)} %param.25) | copy-start | bytes 52
  300.8 30.6 %all-to-all-start.2 = ((bf16[640,4,384]{2,0,1:T(8,128)(2,1)}), bf16[640,4,384]{2,0,1:T(8,128)(2,1)S(1)}, u32[]{:S(2)}, u32[]{:S(2)}) async-start(bf16[640,4,384]{2,0,1:T(8,128)(2,1)} %copy.140), calls=%async_computation.2 | async-start | bytes 3932160 | tf_op jit(solution)/shard_map/all_to_all | solution.py:156
  307.9 32.6 %copy-start.10 = (bf16[4,128,128]{2,1,0:T(8,128)(2,1)}, bf16[4,128,128]{2,1,0:T(8,128)(2,1)S(1)}, u32[]{:S(2)}) copy-start(bf16[4,128,128]{2,1,0:T(8,128)(2,1)S(1)} %scatter_fusion) | copy-start | bytes 393220
  340.5 10.9 %copy-start.1 = (bf16[1536,512]{1,0:T(8,128)(2,1)S(1)}, bf16[1536,512]{1,0:T(8,128)(2,1)}, u32[]{:S(2)}) copy-start(bf16[1536,512]{1,0:T(8,128)(2,1)} %param.17) | copy-start | bytes 4718596
  (2 other events, 6.5 us)
Sparse Core Ops, SparseCore 0:
  134.7 55.9 all-reduce.2

commit v3 on v2

--- a/solution.py
+++ b/solution.py
@@ -113,7 +113,6 @@
         lax.ppermute(packed, "tp", [(source, (source + number) % tp_count) for source in range(tp_count)])
         for number in range(1, tp_count)
     ]
-    attended, weight_parts = lax.optimization_barrier((attended, weight_parts))
     projected = jnp.dot(attended, w_out, preferred_element_type=jnp.float32)
     experts = lax.axis_size("seq") * w_gate.shape[0]
     choose = expert_picks.shape[1]
@@ -132,19 +131,20 @@
     ranks = jnp.sum(before[:, None, :] * onehot, axis=2).astype(jnp.int32)
     owner = ranks // share
     slot = expert_picks * share + ranks % share
-    token_of = jnp.broadcast_to(jnp.arange(count, dtype=jnp.int32)[:, None], expert_picks.shape)
-    table = (
-        jnp.full((slots,), count, jnp.int32)
-        .at[jnp.where(owner == tp_index, slot, slots).reshape(-1)]
-        .set(token_of.reshape(-1), mode="drop")
-    )
+    mine_slot = jnp.where(owner == tp_index, slot, slots)
+    slot_range = jnp.arange(slots, dtype=jnp.int32)
+    placing = jnp.sum(
+        (mine_slot[:, :, None] == slot_range[None, None, :]).astype(jnp.bfloat16), axis=1
+    ).T
     part_width = tokens.shape[1] // tp_count
-    summed = lax.psum(projected.astype(jnp.bfloat16), "tp").astype(jnp.float32)
+    summed = lax.psum(projected.astype(jnp.bfloat16), "tp")
+    summed, weight_parts = lax.optimization_barrier((summed, weight_parts))
+    summed = summed.astype(jnp.float32)
     residual = tokens.astype(jnp.float32) + summed
     mixed_in = row_norm(residual, ffn_gain).astype(jnp.bfloat16)
     columns = mixed_in.shape[1]
-    padded = jnp.concatenate([mixed_in, jnp.zeros((1, columns), jnp.bfloat16)], axis=0)
-    arrived = lax.all_to_all(padded[table], "seq", split_axis=0, concat_axis=0, tiled=True)
+    rows = jnp.dot(placing, mixed_in, preferred_element_type=jnp.float32).astype(jnp.bfloat16)
+    arrived = lax.all_to_all(rows, "seq", split_axis=0, concat_axis=0, tiled=True)
     gate_full = jnp.concatenate([part[:, :hidden_part] for part in weight_parts], axis=1)
     up_full = jnp.concatenate([part[:, hidden_part : 2 * hidden_part] for part in weight_parts], axis=1)
     down_full = jnp.concatenate([part[:, 2 * hidden_part :] for part in weight_parts], axis=1).T
@@ -155,8 +155,14 @@
     returned = lax.all_to_all(expert_out, "seq", split_axis=0, concat_axis=0, tiled=True)
     mine = lax.all_to_all(returned, "tp", split_axis=1, concat_axis=0, tiled=True)
     residual_part = lax.dynamic_slice_in_dim(residual, tp_index * part_width, part_width, 1)
-    gathered = mine[jnp.minimum(owner * slots + slot, tp_count * slots - 1)].astype(jnp.float32)
-    mixture = jnp.sum(gathered * gate_weights[:, :, None], axis=1)
+    every_slot = jnp.arange(tp_count * slots, dtype=jnp.int32)
+    picked = (owner * slots + slot)[:, :, None] == every_slot[None, None, :]
+    scales = jnp.sum(jnp.where(picked, gate_weights[:, :, None], 0.0), axis=1)
+    high = scales.astype(jnp.bfloat16)
+    low = (scales - high.astype(jnp.float32)).astype(jnp.bfloat16)
+    mixture = jnp.dot(high, mine, preferred_element_type=jnp.float32) + jnp.dot(
+        low, mine, preferred_element_type=jnp.float32
+    )
     layer_out = (residual_part + mixture).astype(jnp.bfloat16)
     return (layer_out, kv_pages)
 

time: 365 us -> 330 us (0.904)
  local copies, waits for them, and re-layouts: 49.2 us -> 25.6 us
  waiting for transfers between devices: 134 us -> 115 us
  matrix products: 46.5 us -> 54.8 us
    psum x1, waiting for transfers between devices: 47 us -> 21.4 us  [per_device(): summed = lax.psum(projected.astype(jnp.bfloat16), 'tp')]
    gather x2 -> x0, local copies, waits for them, and re-layouts: 12.8 us -> none  [the longest x1 9.04 us: per_device(): mine[jnp.minimum(owner * slots + slot, tp_count * slots - 1)]]
    dot_general x0 -> x3, matrix products: none -> 12.1 us  [the longest x1 5.71 us: per_device(): jnp.dot(low, mine, preferred_element_type=jnp.float32)]
    ppermute x3, waiting for transfers between devices: 29.3 us -> 40.5 us  [per_device(): lax.ppermute(packed, 'tp', [(source, (source + number) % tp_count) for so...]
    scatter x1 -> x0, local copies, waits for them, and re-layouts: 8.04 us -> none  [per_device(): table = jnp.full((slots,), count, jnp.int32).at[jnp.where(owner == tp_ind...]
    all_to_all x1, waiting for transfers between devices: 23.6 us -> 18.6 us  [per_device(): lax.all_to_all(returned, 'tp', split_axis=1, concat_axis=0, tiled=True)]
    convert_element_type x1 -> x0, local copies, waits for them, and re-layouts: 4.4 us -> none  [per_device(): mine[jnp.minimum(owner * slots + slot, tp_count * slots - 1)]]
  transfers between devices with their start and end apart: 14 -> 14, of which waited for: 5 -> 5; matrix products, arithmetic and copies ran while one was open for 17% -> 18% of each run, Pallas kernels for 0% -> 0%
where the time goes in v3:
time: 330 us; the launch traced here: 324 us
  waiting for transfers between devices  115 us (35%)
  matrix products  54.8 us (17%)
  starting transfers between devices  49 us (15%)
  blocking collectives  36.6 us (11%)
  other arithmetic  28.3 us (9%)
  local copies, waits for them, and re-layouts  25.6 us (8%)
  between operations  15.2 us (5%)
    ppermute x3, waiting for transfers between devices, per_device(): lax.ppermute(packed, 'tp', [(source, (source + number) % tp_count) for so...  40.5 us
    all_to_all x1, blocking collectives, per_device(): lax.all_to_all(expert_out, 'seq', split_axis=0, concat_axis=0, tiled=True)  36.6 us
    ppermute x8, starting transfers between devices, shifted(): lax.ppermute(value, axis, [(source, source + steps) for source in range(l...  29.5 us
    all_to_all x1, waiting for transfers between devices, per_device(): lax.all_to_all(rows, 'seq', split_axis=0, concat_axis=0, tiled=True)  23.2 us
    psum x1, waiting for transfers between devices, per_device(): summed = lax.psum(projected.astype(jnp.bfloat16), 'tp')  21.4 us
    all_to_all x1, waiting for transfers between devices, per_device(): lax.all_to_all(returned, 'tp', split_axis=1, concat_axis=0, tiled=True)  18.6 us
    dot_general x9, matrix products, attend_block(): jnp.einsum('qhk,kd->qhd', weights.astype(jnp.bfloat16), value_block, pref...  12.4 us
    ppermute x8, waiting for transfers between devices, shifted(): lax.ppermute(value, axis, [(source, source + steps) for source in range(l...  11.1 us
  transfers between devices with their start and end apart: 14, of which 5 were waited for; matrix products, arithmetic and copies ran while one was open for 18% of the time, Pallas kernels for 0%

profile of v3, /device:TPU:1, one launch (start us, length us, event | category | flops | bytes accessed | tf_op | source)
XLA Modules:
  0.0 324.4 jit_solution(10472491499269796797)
XLA Ops:
  10.0 2.6 convolution_convert_fusion.3
  13.4 5.7 %collective-permute-start.2 = (bf16[528,256]{1,0:T(8,128)(2,1)S(1)}, bf16[528,256]{1,0:T(8,128)(2,1)}, u32[]{:S(2)}, u32[]{:S(2)}) collective-permute-start(bf16[528,256]{1,0:T(8,128)(2,1)S(1)} %maximum_maximum_fusion), channel_id=1, source_target_pairs={{0,12},{4,16},{8,20},{12,24},{16,28},{20,32},{24,36},{28,40},{32,4... | collective-permute-start | bytes 811016 | tf_op jit(solution)/shard_map/ppermute | solution.py:18
  19.1 4.4 %collective-permute-start.3 = (bf16[528,256]{1,0:T(8,128)(2,1)S(1)}, bf16[528,256]{1,0:T(8,128)(2,1)}, u32[]{:S(2)}, u32[]{:S(2)}) collective-permute-start(bf16[528,256]{1,0:T(8,128)(2,1)S(1)} %maximum_maximum_fusion), channel_id=1, source_target_pairs={{0,16},{4,20},{8,24},{12,28},{16,32},{20,36},{24,40},{28,44},{32,4... | collective-permute-start | bytes 811016 | tf_op jit(solution)/shard_map/ppermute | solution.py:18
  23.5 5.2 %collective-permute-start.4 = (bf16[528,256]{1,0:T(8,128)(2,1)S(1)}, bf16[528,256]{1,0:T(8,128)(2,1)}, u32[]{:S(2)}, u32[]{:S(2)}) collective-permute-start(bf16[528,256]{1,0:T(8,128)(2,1)S(1)} %maximum_maximum_fusion), channel_id=1, source_target_pairs={{0,20},{4,24},{8,28},{12,32},{16,36},{20,40},{24,44},{28,48},{32,5... | collective-permute-start | bytes 811016 | tf_op jit(solution)/shard_map/ppermute | solution.py:18
  28.7 4.1 %collective-permute-start.5 = (bf16[528,256]{1,0:T(8,128)(2,1)S(1)}, bf16[528,256]{1,0:T(8,128)(2,1)}, u32[]{:S(2)}, u32[]{:S(2)}) collective-permute-start(bf16[528,256]{1,0:T(8,128)(2,1)S(1)} %maximum_maximum_fusion), channel_id=1, source_target_pairs={{0,24},{4,28},{8,32},{12,36},{16,40},{20,44},{24,48},{28,52},{32,5... | collective-permute-start | bytes 811016 | tf_op jit(solution)/shard_map/ppermute | solution.py:18
  32.8 2.7 collective-permute-start.6
  39.4 3.6 %collective-permute-start = (bf16[528,256]{1,0:T(8,128)(2,1)S(1)}, bf16[528,256]{1,0:T(8,128)(2,1)S(1)}, u32[]{:S(2)}, u32[]{:S(2)}) collective-permute-start(bf16[528,256]{1,0:T(8,128)(2,1)S(1)} %maximum_maximum_fusion), channel_id=1, source_target_pairs={{0,4},{4,8},{8,12},{12,16},{16,20},{20,24},{24,28},{28,32},{32,36}... | collective-permute-start | bytes 811016 | tf_op jit(solution)/shard_map/ppermute | solution.py:18
  43.7 2.5 collective-permute-start.1
  48.9 2.7 collective-permute-start.10
  52.3 2.8 collective-permute-start.8
  56.8 11.1 %collective-permute-done.7 = bf16[528,256]{1,0:T(8,128)(2,1)S(1)} collective-permute-done((bf16[528,256]{1,0:T(8,128)(2,1)S(1)}, bf16[528,256]{1,0:T(8,128)(2,1)S(1)}, u32[]{:S(2)}, u32[]{:S(2)}) %collective-permute-start.7) | collective-permute-done | bytes 270368 | tf_op jit(solution)/shard_map/ppermute | solution.py:18
  105.2 40.5 %collective-permute-done.9 = bf16[1536,576]{0,1:T(8,128)(2,1)} collective-permute-done((bf16[1536,576]{0,1:T(8,128)(2,1)S(1)}, bf16[1536,576]{0,1:T(8,128)(2,1)}, u32[]{:S(2)}, u32[]{:S(2)}) %collective-permute-start.9) | collective-permute-done | bytes 1769504 | tf_op jit(solution)/shard_map/ppermute | solution.py:113
  145.7 21.4 %all-reduce.2.cloned.1.call-done = bf16[512,1536]{1,0:T(8,128)(2,1)} async-done(((bf16[512,1536]{1,0:T(8,128)(2,1)}), bf16[512,1536]{1,0:T(8,128)(2,1)}) %all-reduce.2.cloned.1.call-update) | async-done | bytes 1572880 | tf_op jit(solution)/shard_map/psum | solution.py:140
  167.1 3.7 %convert_add_fusion = (f32[512,1536]{1,0:T(8,128)}, f32[512]{0:T(512)S(1)}) fusion(bf16[512,1536]{1,0:T(8,128)(2,1)S(1)} %copy-done.4, bf16[512,1536]{1,0:T(8,128)(2,1)} %all-reduce.2.cloned.1.call-done), kind=kLoop, calls=%fused_computation.6 | loop fusion | flops 3931648 | bytes 6293504 | tf_op jit(solution)/shard_map/add | solution.py:143
  170.8 2.8 convolution_convert_fusion.1
  173.6 3.9 %all_to_all.28 = bf16[32,20,1536]{2,1,0:T(8,128)(2,1)} reshape(bf16[640,1536]{1,0:T(8,128)(2,1)} %convolution_convert_fusion.1) | data formatting | bytes 3932160 | tf_op jit(solution)/shard_map/all_to_all | solution.py:147
  177.5 7.3 %all-to-all-start = ((bf16[32,20,1536]{2,1,0:T(8,128)(2,1)}), bf16[32,20,1536]{2,1,0:T(8,128)(2,1)}, u32[]{:S(2)}, u32[]{:S(2)}) async-start(bf16[32,20,1536]{2,1,0:T(8,128)(2,1)} %all_to_all.28), calls=%async_computation | async-start | bytes 4718592 | tf_op jit(solution)/shard_map/all_to_all | solution.py:147
  185.8 2.8 fusion.224
  188.6 2.7 fusion.225
  191.2 2.8 fusion.226
  194.0 23.2 %all-to-all-done = bf16[32,20,1536]{2,1,0:T(8,128)(2,1)} async-done(((bf16[32,20,1536]{2,1,0:T(8,128)(2,1)}), bf16[32,20,1536]{2,1,0:T(8,128)(2,1)}, u32[]{:S(2)}, u32[]{:S(2)}) %all-to-all-start) | async-done | bytes 1966112 | tf_op jit(solution)/shard_map/all_to_all | solution.py:147
  217.2 2.6 all_to_all.30
  219.8 4.6 %fusion.24 = f32[640,768]{1,0:T(8,128)} fusion(bf16[640,1536]{1,0:T(8,128)(2,1)S(1)} %all_to_all.30, bf16[1536,192]{0,1:T(8,128)(2,1)} %get-tuple-element.44, bf16[1536,192]{0,1:T(8,128)(2,1)} %get-tuple-element.41, bf16[1536,192]{0,1:T(8,128)(2,1)} %get-tuple-element.38, bf16[1536,192]{0,1:T(8,128)(2,1)} %get-tuple-element.35), kind=kOutput, calls=%fused_computation.55 | convolution fusion | flops 1519386624 | bytes 6291456 | tf_op jit(solution)/shard_map/dot_general | solution.py:151
  224.4 7.8 %convolution_convert_fusion = bf16[640,1536]{1,0:T(8,128)(2,1)} fusion(bf16[1536,192]{0,1:T(8,128)(2,1)} %get-tuple-element.43, bf16[1536,192]{0,1:T(8,128)(2,1)} %get-tuple-element.40, bf16[1536,192]{0,1:T(8,128)(2,1)} %get-tuple-element.37, bf16[1536,192]{0,1:T(8,128)(2,1)S(1)} %get-tuple-element.34, f32[640,768]{1,0:T(8,128)} %fusion.24, ...), kind=kOutput, calls=%fused_computation.9 | convolution fusion | flops 3041230848 | bytes 10616832 | tf_op jit(solution)/shard_map/dot_general | solution.py:154
  232.2 3.9 %all_to_all.31 = bf16[32,20,1536]{2,1,0:T(8,128)(2,1)} reshape(bf16[640,1536]{1,0:T(8,128)(2,1)} %convolution_convert_fusion) | data formatting | bytes 3932160 | tf_op jit(solution)/shard_map/all_to_all | solution.py:155
  236.1 36.6 %all_to_all.40 = bf16[32,20,1536]{2,1,0:T(8,128)(2,1)} all-to-all(bf16[32,20,1536]{2,1,0:T(8,128)(2,1)} %all_to_all.31), channel_id=1, replica_groups=mesh['seq'=32,'tp'=4] {'seq'}, dimensions={0} | all-to-all | bytes 3932160 | tf_op jit(solution)/shard_map/all_to_all | solution.py:155
  272.7 2.8 all_to_all.33
  277.2 5.8 %all-to-all-start.2 = ((bf16[640,4,384]{2,0,1:T(8,128)(2,1)}), bf16[640,4,384]{2,0,1:T(8,128)(2,1)S(1)}, u32[]{:S(2)}, u32[]{:S(2)}) async-start(bf16[640,4,384]{2,0,1:T(8,128)(2,1)} %copy.140), calls=%async_computation.2 | async-start | bytes 3932160 | tf_op jit(solution)/shard_map/all_to_all | solution.py:156
  283.7 5.4 %select_reduce_fusion = f32[512,2560]{1,0:T(8,128)} fusion(f32[512,4]{0,1:T(4,128)S(1)} %copy-done.13, s32[512,4]{0,1:T(4,128)S(1)} %get-tuple-element.48), kind=kLoop, calls=%fused_computation.1 | loop fusion | flops 14417920 | bytes 5259264 | tf_op jit(solution)/shard_map/reduce_sum | solution.py:160
  289.1 18.6 %all-to-all-done.2 = bf16[640,4,384]{2,0,1:T(8,128)(2,1)S(1)} async-done(((bf16[640,4,384]{2,0,1:T(8,128)(2,1)}), bf16[640,4,384]{2,0,1:T(8,128)(2,1)S(1)}, u32[]{:S(2)}, u32[]{:S(2)}) %all-to-all-start.2) | async-done | bytes 1966112 | tf_op jit(solution)/shard_map/all_to_all | solution.py:156
  307.7 5.7 %fusion.5 = f32[512,384]{1,0:T(8,128)S(1)} fusion(bf16[2560,384]{1,0:T(8,128)(2,1)S(1)} %bitcast.138, f32[512,2560]{1,0:T(8,128)} %select_reduce_fusion), kind=kOutput, calls=%fused_computation.36 | convolution fusion | flops 1011875840 | bytes 7995392 | tf_op jit(solution)/shard_map/dot_general | solution.py:163
  313.5 3.6 %add_convert_fusion = bf16[512,384]{1,0:T(8,128)(2,1)} fusion(f32[512,1536]{1,0:T(8,128)} %get-tuple-element.31, s32[]{:T(128)S(6)} %select_n.128, f32[512,384]{1,0:T(8,128)S(1)} %fusion.5, bf16[2560,384]{1,0:T(8,128)(2,1)S(1)} %bitcast.139, f32[512,2560]{1,0:T(8,128)S(1)} %copy-done.2), kind=kOutput, calls=%fused_computation.163 | convolution fusion | flops 1008533504 | bytes 9175044 | tf_op jit(solution)/shard_map/dot_general | solution.py:163
  (140 shorter events, 53.3 us)
Async XLA Ops:
  7.2 2.8 copy-start
  7.2 159.9 %all-reduce.2.cloned.1.call-start = ((), (), s32[]{:S(2)}) async-start(), calls=%async_computation.3 | async-start | bytes 3145728 | tf_op jit(solution)/shard_map/psum | solution.py:140
  10.0 25.8 %copy-start.3 = (bf16[512,1536]{1,0:T(8,128)(2,1)S(1)}, bf16[512,1536]{1,0:T(8,128)(2,1)}, u32[]{:S(2)}) copy-start(bf16[512,1536]{1,0:T(8,128)(2,1)} %param.13) | copy-start | bytes 4718596
  10.0 25.8 %copy-start.14 = (f32[1536]{0:T(1024)S(1)}, f32[1536]{0:T(1024)}, u32[]{:S(2)}) copy-start(f32[1536]{0:T(1024)} %param.15) | copy-start | bytes 18436
  12.5 25.5 %copy-start.8 = (bf16[1,192,1536]{2,1,0:T(8,128)(2,1)S(1)}, bf16[1,192,1536]{2,1,0:T(8,128)(2,1)}, u32[]{:S(2)}) copy-start(bf16[1,192,1536]{2,1,0:T(8,128)(2,1)} %param.22) | copy-start | bytes 1769476
  13.4 26.0 %collective-permute-start.2 = (bf16[528,256]{1,0:T(8,128)(2,1)S(1)}, bf16[528,256]{1,0:T(8,128)(2,1)}, u32[]{:S(2)}, u32[]{:S(2)}) collective-permute-start(bf16[528,256]{1,0:T(8,128)(2,1)S(1)} %maximum_maximum_fusion), channel_id=1, source_target_pairs={{0,12},{4,16},{8,20},{12,24},{16,28},{20,32},{24,36},{28,40},{32,4... | collective-permute-start | bytes 811016 | tf_op jit(solution)/shard_map/ppermute | solution.py:18
  19.1 24.6 %collective-permute-start.3 = (bf16[528,256]{1,0:T(8,128)(2,1)S(1)}, bf16[528,256]{1,0:T(8,128)(2,1)}, u32[]{:S(2)}, u32[]{:S(2)}) collective-permute-start(bf16[528,256]{1,0:T(8,128)(2,1)S(1)} %maximum_maximum_fusion), channel_id=1, source_target_pairs={{0,16},{4,20},{8,24},{12,28},{16,32},{20,36},{24,40},{28,44},{32,4... | collective-permute-start | bytes 811016 | tf_op jit(solution)/shard_map/ppermute | solution.py:18
  23.5 23.5 %collective-permute-start.4 = (bf16[528,256]{1,0:T(8,128)(2,1)S(1)}, bf16[528,256]{1,0:T(8,128)(2,1)}, u32[]{:S(2)}, u32[]{:S(2)}) collective-permute-start(bf16[528,256]{1,0:T(8,128)(2,1)S(1)} %maximum_maximum_fusion), channel_id=1, source_target_pairs={{0,20},{4,24},{8,28},{12,32},{16,36},{20,40},{24,44},{28,48},{32,5... | collective-permute-start | bytes 811016 | tf_op jit(solution)/shard_map/ppermute | solution.py:18
  28.7 20.3 %collective-permute-start.5 = (bf16[528,256]{1,0:T(8,128)(2,1)S(1)}, bf16[528,256]{1,0:T(8,128)(2,1)}, u32[]{:S(2)}, u32[]{:S(2)}) collective-permute-start(bf16[528,256]{1,0:T(8,128)(2,1)S(1)} %maximum_maximum_fusion), channel_id=1, source_target_pairs={{0,24},{4,28},{8,32},{12,36},{16,40},{20,44},{24,48},{28,52},{32,5... | collective-permute-start | bytes 811016 | tf_op jit(solution)/shard_map/ppermute | solution.py:18
  32.8 19.5 %collective-permute-start.6 = (bf16[528,256]{1,0:T(8,128)(2,1)S(1)}, bf16[528,256]{1,0:T(8,128)(2,1)}, u32[]{:S(2)}, u32[]{:S(2)}) collective-permute-start(bf16[528,256]{1,0:T(8,128)(2,1)S(1)} %maximum_maximum_fusion), channel_id=1, source_target_pairs={{0,28},{4,32},{8,36},{12,40},{16,44},{20,48},{24,52},{28,56},{32,6... | collective-permute-start | bytes 811016 | tf_op jit(solution)/shard_map/ppermute | solution.py:18
  35.8 32.1 %copy-start.12 = (s32[512]{0:T(512)S(1)}, s32[512]{0:T(512)}, u32[]{:S(2)}) copy-start(s32[512]{0:T(512)} %param.14) | copy-start | bytes 6148
  39.4 16.4 %collective-permute-start = (bf16[528,256]{1,0:T(8,128)(2,1)S(1)}, bf16[528,256]{1,0:T(8,128)(2,1)S(1)}, u32[]{:S(2)}, u32[]{:S(2)}) collective-permute-start(bf16[528,256]{1,0:T(8,128)(2,1)S(1)} %maximum_maximum_fusion), channel_id=1, source_target_pairs={{0,4},{4,8},{8,12},{12,16},{16,20},{20,24},{24,28},{28,32},{32,36}... | collective-permute-start | bytes 811016 | tf_op jit(solution)/shard_map/ppermute | solution.py:18
  43.7 12.9 %collective-permute-start.1 = (bf16[528,256]{1,0:T(8,128)(2,1)S(1)}, bf16[528,256]{1,0:T(8,128)(2,1)S(1)}, u32[]{:S(2)}, u32[]{:S(2)}) collective-permute-start(bf16[528,256]{1,0:T(8,128)(2,1)S(1)} %maximum_maximum_fusion), channel_id=1, source_target_pairs={{0,8},{4,12},{8,16},{12,20},{16,24},{20,28},{24,32},{28,36},{32,40... | collective-permute-start | bytes 811016 | tf_op jit(solution)/shard_map/ppermute | solution.py:18
  46.9 20.9 %collective-permute-start.7 = (bf16[528,256]{1,0:T(8,128)(2,1)S(1)}, bf16[528,256]{1,0:T(8,128)(2,1)S(1)}, u32[]{:S(2)}, u32[]{:S(2)}) collective-permute-start(bf16[528,256]{1,0:T(8,128)(2,1)S(1)} %maximum_maximum_fusion), channel_id=1, source_target_pairs={{0,32},{4,36},{8,40},{12,44},{16,48},{20,52},{24,56},{28,60},{32,6... | collective-permute-start | bytes 811016 | tf_op jit(solution)/shard_map/ppermute | solution.py:18
  48.9 56.3 %collective-permute-start.10 = (bf16[1536,576]{0,1:T(8,128)(2,1)S(1)}, bf16[1536,576]{0,1:T(8,128)(2,1)}, u32[]{:S(2)}, u32[]{:S(2)}) collective-permute-start(bf16[1536,576]{0,1:T(8,128)(2,1)S(1)} %pad_maximum_fusion), channel_id=1, source_target_pairs={{0,3},{1,0},{2,1},{3,2},{4,7},{5,4},{6,5},{7,6},{8,11},{9,8},{10,9... | collective-permute-start | bytes 5308424 | tf_op jit(solution)/shard_map/ppermute | solution.py:113
  52.3 52.9 %collective-permute-start.8 = (bf16[1536,576]{0,1:T(8,128)(2,1)S(1)}, bf16[1536,576]{0,1:T(8,128)(2,1)}, u32[]{:S(2)}, u32[]{:S(2)}) collective-permute-start(bf16[1536,576]{0,1:T(8,128)(2,1)S(1)} %pad_maximum_fusion), channel_id=1, source_target_pairs={{0,1},{1,2},{2,3},{3,0},{4,5},{5,6},{6,7},{7,4},{8,9},{9,10},{10,1... | collective-permute-start | bytes 5308424 | tf_op jit(solution)/shard_map/ppermute | solution.py:113
  55.8 89.8 %collective-permute-start.9 = (bf16[1536,576]{0,1:T(8,128)(2,1)S(1)}, bf16[1536,576]{0,1:T(8,128)(2,1)}, u32[]{:S(2)}, u32[]{:S(2)}) collective-permute-start(bf16[1536,576]{0,1:T(8,128)(2,1)S(1)} %pad_maximum_fusion), channel_id=1, source_target_pairs={{0,2},{1,3},{2,0},{3,1},{4,6},{5,7},{6,4},{7,5},{8,10},{9,11},{10,... | collective-permute-start | bytes 5308424 | tf_op jit(solution)/shard_map/ppermute | solution.py:113
  99.6 1.4 copy-start.6
  100.9 2.2 copy-start.11
  100.9 66.2 %copy-start.4 = (bf16[512,1536]{1,0:T(8,128)(2,1)S(1)}, bf16[512,1536]{1,0:T(8,128)(2,1)}, u32[]{:S(2)}) copy-start(bf16[512,1536]{1,0:T(8,128)(2,1)} %param.13) | copy-start | bytes 4718596
  105.2 65.6 %copy-start.15 = (f32[1536]{0:T(1024)S(1)}, f32[1536]{0:T(1024)}, u32[]{:S(2)}) copy-start(f32[1536]{0:T(1024)} %param.19) | copy-start | bytes 18436
  167.1 3.7 %copy-start.5 = (bf16[512,1536]{1,0:T(8,128)(2,1)S(1)}, bf16[512,1536]{1,0:T(8,128)(2,1)}, u32[]{:S(2)}) copy-start(bf16[512,1536]{1,0:T(8,128)(2,1)} %all-reduce.2.cloned.1.call-done) | copy-start | bytes 4718596
  167.1 3.7 %copy-start.7 = (bf16[512,640]{1,0:T(8,128)(2,1)S(1)}, bf16[512,640]{1,0:T(8,128)(2,1)}, u32[]{:S(2)}) copy-start(bf16[512,640]{1,0:T(8,128)(2,1)} %fusion.4) | copy-start | bytes 1966084
  177.5 39.7 %all-to-all-start = ((bf16[32,20,1536]{2,1,0:T(8,128)(2,1)}), bf16[32,20,1536]{2,1,0:T(8,128)(2,1)}, u32[]{:S(2)}, u32[]{:S(2)}) async-start(bf16[32,20,1536]{2,1,0:T(8,128)(2,1)} %all_to_all.28), calls=%async_computation | async-start | bytes 4718592 | tf_op jit(solution)/shard_map/all_to_all | solution.py:147
  275.5 7.4 %copy-start.16 = (s32[4]{0:T(128)S(1)}, s32[4]{0:T(128)}, u32[]{:S(2)}) copy-start(s32[4]{0:T(128)} %param.25) | copy-start | bytes 52
  275.5 7.4 %copy-start.10 = (bf16[512,128]{1,0:T(8,128)(2,1)S(1)}, bf16[512,128]{1,0:T(8,128)(2,1)}, u32[]{:S(2)}) copy-start(bf16[512,128]{1,0:T(8,128)(2,1)} %get-tuple-element.45) | copy-start | bytes 393220
  277.1 6.5 %copy-start.13 = (f32[512,4]{0,1:T(4,128)S(1)}, f32[512,4]{0,1:T(4,128)}, u32[]{:S(2)}) copy-start(f32[512,4]{0,1:T(4,128)} %param.24) | copy-start | bytes 24580
  277.2 30.6 %all-to-all-start.2 = ((bf16[640,4,384]{2,0,1:T(8,128)(2,1)}), bf16[640,4,384]{2,0,1:T(8,128)(2,1)S(1)}, u32[]{:S(2)}, u32[]{:S(2)}) async-start(bf16[640,4,384]{2,0,1:T(8,128)(2,1)} %copy.140), calls=%async_computation.2 | async-start | bytes 3932160 | tf_op jit(solution)/shard_map/all_to_all | solution.py:156
  283.6 24.1 %copy-start.9 = (bf16[4,128,128]{2,1,0:T(8,128)(2,1)}, bf16[4,128,128]{2,1,0:T(8,128)(2,1)S(1)}, u32[]{:S(2)}) copy-start(bf16[4,128,128]{2,1,0:T(8,128)(2,1)S(1)} %scatter_fusion) | copy-start | bytes 393220
  307.7 5.7 %copy-start.2 = (f32[512,2560]{1,0:T(8,128)S(1)}, f32[512,2560]{1,0:T(8,128)}, u32[]{:S(2)}) copy-start(f32[512,2560]{1,0:T(8,128)} %select_reduce_fusion) | copy-start | bytes 15728644
  313.5 3.6 %copy-start.1 = (bf16[1536,512]{1,0:T(8,128)(2,1)S(1)}, bf16[1536,512]{1,0:T(8,128)(2,1)}, u32[]{:S(2)}) copy-start(bf16[1536,512]{1,0:T(8,128)(2,1)} %param.17) | copy-start | bytes 4718596
Sparse Core Ops, SparseCore 0:
  103.2 63.7 all-reduce.1

commit v4 on v3

--- a/solution.py
+++ b/solution.py
@@ -152,11 +152,16 @@
     up_part = jnp.dot(arrived, up_full, preferred_element_type=jnp.float32)
     hidden = (jax.nn.relu(gate_part) * up_part).astype(jnp.bfloat16)
     expert_out = jnp.dot(hidden, down_full, preferred_element_type=jnp.float32).astype(jnp.bfloat16)
-    returned = lax.all_to_all(expert_out, "seq", split_axis=0, concat_axis=0, tiled=True)
-    mine = lax.all_to_all(returned, "tp", split_axis=1, concat_axis=0, tiled=True)
+    sources = lax.axis_size("seq")
+    outgoing = (
+        expert_out.reshape(sources, share, tp_count, part_width)
+        .transpose(0, 2, 1, 3)
+        .reshape(sources * tp_count * share, part_width)
+    )
+    mine = lax.all_to_all(outgoing, ("seq", "tp"), split_axis=0, concat_axis=0, tiled=True)
     residual_part = lax.dynamic_slice_in_dim(residual, tp_index * part_width, part_width, 1)
-    every_slot = jnp.arange(tp_count * slots, dtype=jnp.int32)
-    picked = (owner * slots + slot)[:, :, None] == every_slot[None, None, :]
+    every_slot = jnp.arange(experts * capacity, dtype=jnp.int32)
+    picked = (expert_picks * capacity + ranks)[:, :, None] == every_slot[None, None, :]
     scales = jnp.sum(jnp.where(picked, gate_weights[:, :, None], 0.0), axis=1)
     high = scales.astype(jnp.bfloat16)
     low = (scales - high.astype(jnp.float32)).astype(jnp.bfloat16)

time: 330 us -> 305 us (0.924)
  blocking collectives: 36.6 us -> 0 us
  waiting for transfers between devices: 115 us -> 122 us
    all_to_all x1 -> x0, blocking collectives: 36.6 us -> none  [per_device(): lax.all_to_all(expert_out, 'seq', split_axis=0, concat_axis=0, tiled=True)]
    all_to_all x1, waiting for transfers between devices: 18.6 us -> 26.2 us  [per_device(): lax.all_to_all(outgoing, ('seq', 'tp'), split_axis=0, concat_axis=0, tile...]
    reshape x0 -> x1, local copies, waits for them, and re-layouts: none -> 3.34 us  [per_device(): expert_out.reshape(sources, share, tp_count, part_width)]
    all_to_all x3 -> x2, local copies, waits for them, and re-layouts: 8.3 us -> 5.84 us  [per_device(): lax.all_to_all(outgoing, ('seq', 'tp'), split_axis=0, concat_axis=0, tile...]
  transfers between devices with their start and end apart: 14 -> 14, of which waited for: 5 -> 5; matrix products, arithmetic and copies ran while one was open for 18% -> 20% of each run, Pallas kernels for 0% -> 0%
where the time goes in v4:
time: 305 us; the launch traced here: 299 us
  waiting for transfers between devices  122 us (40%)
  matrix products  55.3 us (18%)
  starting transfers between devices  51.5 us (17%)
  other arithmetic  28.6 us (9%)
  local copies, waits for them, and re-layouts  26.6 us (9%)
  between operations  15.1 us (5%)
    ppermute x3, waiting for transfers between devices, per_device(): lax.ppermute(packed, 'tp', [(source, (source + number) % tp_count) for so...  40.2 us
    ppermute x8, starting transfers between devices, shifted(): lax.ppermute(value, axis, [(source, source + steps) for source in range(l...  29.5 us
    all_to_all x1, waiting for transfers between devices, per_device(): lax.all_to_all(outgoing, ('seq', 'tp'), split_axis=0, concat_axis=0, tile...  26.2 us
    all_to_all x1, waiting for transfers between devices, per_device(): lax.all_to_all(rows, 'seq', split_axis=0, concat_axis=0, tiled=True)  23.2 us
    psum x1, waiting for transfers between devices, per_device(): summed = lax.psum(projected.astype(jnp.bfloat16), 'tp')  21.7 us
    dot_general x9, matrix products, attend_block(): jnp.einsum('qhk,kd->qhd', weights.astype(jnp.bfloat16), value_block, pref...  12.3 us
    ppermute x8, waiting for transfers between devices, shifted(): lax.ppermute(value, axis, [(source, source + steps) for source in range(l...  11.1 us
    dot_general x9, matrix products, attend_block(): jnp.einsum('qhd,kd->qhk', queries, key_block, preferred_element_type=jnp....  10.9 us
  transfers between devices with their start and end apart: 14, of which 5 were waited for; matrix products, arithmetic and copies ran while one was open for 20% of the time, Pallas kernels for 0%

profile of v4, /device:TPU:1, one launch (start us, length us, event | category | flops | bytes accessed | tf_op | source)
XLA Modules:
  0.0 299.5 jit_solution(15462558322759858668)
XLA Ops:
  10.0 2.6 convolution_convert_fusion.3
  13.4 5.7 %collective-permute-start.2 = (bf16[528,256]{1,0:T(8,128)(2,1)S(1)}, bf16[528,256]{1,0:T(8,128)(2,1)}, u32[]{:S(2)}, u32[]{:S(2)}) collective-permute-start(bf16[528,256]{1,0:T(8,128)(2,1)S(1)} %maximum_maximum_fusion), channel_id=1, source_target_pairs={{0,12},{4,16},{8,20},{12,24},{16,28},{20,32},{24,36},{28,40},{32,4... | collective-permute-start | bytes 811016 | tf_op jit(solution)/shard_map/ppermute | solution.py:18
  19.1 4.4 %collective-permute-start.3 = (bf16[528,256]{1,0:T(8,128)(2,1)S(1)}, bf16[528,256]{1,0:T(8,128)(2,1)}, u32[]{:S(2)}, u32[]{:S(2)}) collective-permute-start(bf16[528,256]{1,0:T(8,128)(2,1)S(1)} %maximum_maximum_fusion), channel_id=1, source_target_pairs={{0,16},{4,20},{8,24},{12,28},{16,32},{20,36},{24,40},{28,44},{32,4... | collective-permute-start | bytes 811016 | tf_op jit(solution)/shard_map/ppermute | solution.py:18
  23.5 5.2 %collective-permute-start.4 = (bf16[528,256]{1,0:T(8,128)(2,1)S(1)}, bf16[528,256]{1,0:T(8,128)(2,1)}, u32[]{:S(2)}, u32[]{:S(2)}) collective-permute-start(bf16[528,256]{1,0:T(8,128)(2,1)S(1)} %maximum_maximum_fusion), channel_id=1, source_target_pairs={{0,20},{4,24},{8,28},{12,32},{16,36},{20,40},{24,44},{28,48},{32,5... | collective-permute-start | bytes 811016 | tf_op jit(solution)/shard_map/ppermute | solution.py:18
  28.7 4.1 %collective-permute-start.5 = (bf16[528,256]{1,0:T(8,128)(2,1)S(1)}, bf16[528,256]{1,0:T(8,128)(2,1)}, u32[]{:S(2)}, u32[]{:S(2)}) collective-permute-start(bf16[528,256]{1,0:T(8,128)(2,1)S(1)} %maximum_maximum_fusion), channel_id=1, source_target_pairs={{0,24},{4,28},{8,32},{12,36},{16,40},{20,44},{24,48},{28,52},{32,5... | collective-permute-start | bytes 811016 | tf_op jit(solution)/shard_map/ppermute | solution.py:18
  32.8 2.7 collective-permute-start.6
  35.8 2.2 convolution_convert_fusion.4
  39.4 3.6 %collective-permute-start = (bf16[528,256]{1,0:T(8,128)(2,1)S(1)}, bf16[528,256]{1,0:T(8,128)(2,1)S(1)}, u32[]{:S(2)}, u32[]{:S(2)}) collective-permute-start(bf16[528,256]{1,0:T(8,128)(2,1)S(1)} %maximum_maximum_fusion), channel_id=1, source_target_pairs={{0,4},{4,8},{8,12},{12,16},{16,20},{20,24},{24,28},{28,32},{32,36}... | collective-permute-start | bytes 811016 | tf_op jit(solution)/shard_map/ppermute | solution.py:18
  43.7 2.5 collective-permute-start.1
  48.9 2.7 collective-permute-start.10
  52.3 2.8 collective-permute-start.8
  56.8 11.1 %collective-permute-done.7 = bf16[528,256]{1,0:T(8,128)(2,1)S(1)} collective-permute-done((bf16[528,256]{1,0:T(8,128)(2,1)S(1)}, bf16[528,256]{1,0:T(8,128)(2,1)S(1)}, u32[]{:S(2)}, u32[]{:S(2)}) %collective-permute-start.7) | collective-permute-done | bytes 270368 | tf_op jit(solution)/shard_map/ppermute | solution.py:18
  105.5 40.2 %collective-permute-done.9 = bf16[1536,576]{0,1:T(8,128)(2,1)} collective-permute-done((bf16[1536,576]{0,1:T(8,128)(2,1)S(1)}, bf16[1536,576]{0,1:T(8,128)(2,1)}, u32[]{:S(2)}, u32[]{:S(2)}) %collective-permute-start.9) | collective-permute-done | bytes 1769504 | tf_op jit(solution)/shard_map/ppermute | solution.py:113
  145.7 21.7 %all-reduce.2.cloned.1.call-done = bf16[512,1536]{1,0:T(8,128)(2,1)} async-done(((bf16[512,1536]{1,0:T(8,128)(2,1)}), bf16[512,1536]{1,0:T(8,128)(2,1)}) %all-reduce.2.cloned.1.call-update) | async-done | bytes 1572880 | tf_op jit(solution)/shard_map/psum | solution.py:140
  167.4 3.7 %convert_add_fusion = (f32[512,1536]{1,0:T(8,128)}, f32[512]{0:T(512)S(1)}) fusion(bf16[512,1536]{1,0:T(8,128)(2,1)S(1)} %copy-done.4, bf16[512,1536]{1,0:T(8,128)(2,1)} %all-reduce.2.cloned.1.call-done), kind=kLoop, calls=%fused_computation.6 | loop fusion | flops 3931648 | bytes 6293504 | tf_op jit(solution)/shard_map/add | solution.py:143
  171.1 2.8 convolution_convert_fusion.1
  173.9 3.9 %all_to_all.16 = bf16[32,20,1536]{2,1,0:T(8,128)(2,1)} reshape(bf16[640,1536]{1,0:T(8,128)(2,1)} %convolution_convert_fusion.1) | data formatting | bytes 3932160 | tf_op jit(solution)/shard_map/all_to_all | solution.py:147
  177.8 7.3 %all-to-all-start = ((bf16[32,20,1536]{2,1,0:T(8,128)(2,1)}), bf16[32,20,1536]{2,1,0:T(8,128)(2,1)}, u32[]{:S(2)}, u32[]{:S(2)}) async-start(bf16[32,20,1536]{2,1,0:T(8,128)(2,1)} %all_to_all.16), calls=%async_computation | async-start | bytes 4718592 | tf_op jit(solution)/shard_map/all_to_all | solution.py:147
  186.1 2.8 fusion.226
  188.8 2.7 fusion.227
  191.5 2.8 fusion.228
  194.3 23.2 %all-to-all-done = bf16[32,20,1536]{2,1,0:T(8,128)(2,1)} async-done(((bf16[32,20,1536]{2,1,0:T(8,128)(2,1)}), bf16[32,20,1536]{2,1,0:T(8,128)(2,1)}, u32[]{:S(2)}, u32[]{:S(2)}) %all-to-all-start) | async-done | bytes 1966112 | tf_op jit(solution)/shard_map/all_to_all | solution.py:147
  217.5 2.6 all_to_all.18
  220.1 4.6 %fusion.24 = f32[640,768]{1,0:T(8,128)} fusion(bf16[640,1536]{1,0:T(8,128)(2,1)S(1)} %all_to_all.18, bf16[1536,192]{0,1:T(8,128)(2,1)} %get-tuple-element.44, bf16[1536,192]{0,1:T(8,128)(2,1)} %get-tuple-element.41, bf16[1536,192]{0,1:T(8,128)(2,1)} %get-tuple-element.38, bf16[1536,192]{0,1:T(8,128)(2,1)} %get-tuple-element.35), kind=kOutput, calls=%fused_computation.55 | convolution fusion | flops 1519386624 | bytes 6291456 | tf_op jit(solution)/shard_map/dot_general | solution.py:151
  224.7 7.8 %convolution_convert_fusion = bf16[640,1536]{1,0:T(8,128)(2,1)} fusion(bf16[1536,192]{0,1:T(8,128)(2,1)} %get-tuple-element.43, bf16[1536,192]{0,1:T(8,128)(2,1)} %get-tuple-element.40, bf16[1536,192]{0,1:T(8,128)(2,1)} %get-tuple-element.37, bf16[1536,192]{0,1:T(8,128)(2,1)S(1)} %get-tuple-element.34, f32[640,768]{1,0:T(8,128)} %fusion.24, ...), kind=kOutput, calls=%fused_computation.9 | convolution fusion | flops 3041230848 | bytes 10616832 | tf_op jit(solution)/shard_map/dot_general | solution.py:154
  232.5 3.3 %reshape.975 = bf16[32,20,4,384]{3,2,1,0:T(4,128)(2,1)S(1)} reshape(bf16[640,1536]{1,0:T(8,128)(2,1)} %convolution_convert_fusion) | data formatting | bytes 3932160 | tf_op jit(solution)/shard_map/reshape | solution.py:157
  237.6 8.3 %all-to-all-start.1 = ((bf16[128,20,384]{2,1,0:T(8,128)(2,1)}), bf16[128,20,384]{2,1,0:T(8,128)(2,1)}, u32[]{:S(2)}, u32[]{:S(2)}) async-start(bf16[128,20,384]{2,1,0:T(8,128)(2,1)} %bitcast.140), calls=%async_computation.1 | async-start | bytes 4718592 | tf_op jit(solution)/shard_map/all_to_all | solution.py:161
  246.7 5.4 %select_reduce_fusion = f32[512,2560]{1,0:T(8,128)} fusion(f32[512,4]{0,1:T(4,128)S(1)} %copy-done.13, s32[512,4]{0,1:T(4,128)S(1)} %get-tuple-element.48), kind=kLoop, calls=%fused_computation.1 | loop fusion | flops 14417920 | bytes 5259264 | tf_op jit(solution)/shard_map/reduce_sum | solution.py:165
  252.1 26.2 %all-to-all-done.1 = bf16[128,20,384]{2,1,0:T(8,128)(2,1)} async-done(((bf16[128,20,384]{2,1,0:T(8,128)(2,1)}), bf16[128,20,384]{2,1,0:T(8,128)(2,1)}, u32[]{:S(2)}, u32[]{:S(2)}) %all-to-all-start.1) | async-done | bytes 1966112 | tf_op jit(solution)/shard_map/all_to_all | solution.py:161
  278.3 4.0 %all_to_all.21 = bf16[2560,384]{1,0:T(8,128)(2,1)} reshape(bf16[128,20,384]{2,1,0:T(8,128)(2,1)} %all-to-all-done.1) | data formatting | bytes 3932160 | tf_op jit(solution)/shard_map/all_to_all | solution.py:161
  282.4 6.3 %fusion.5 = f32[512,384]{1,0:T(8,128)S(1)} fusion(bf16[2560,384]{1,0:T(8,128)(2,1)} %all_to_all.21, f32[512,2560]{1,0:T(8,128)} %select_reduce_fusion), kind=kOutput, calls=%fused_computation.36 | convolution fusion | flops 1011875840 | bytes 7995392 | tf_op jit(solution)/shard_map/dot_general | solution.py:168
  288.8 3.6 %add_convert_fusion = bf16[512,384]{1,0:T(8,128)(2,1)} fusion(f32[512,1536]{1,0:T(8,128)} %get-tuple-element.31, s32[]{:T(128)S(6)} %select_n.128, f32[512,384]{1,0:T(8,128)S(1)} %fusion.5, bf16[2560,384]{1,0:T(8,128)(2,1)S(1)} %copy-done.2, f32[512,2560]{1,0:T(8,128)S(1)} %bitcast.130), kind=kOutput, calls=%fused_computation.163 | convolution fusion | flops 1008533504 | bytes 9175044 | tf_op jit(solution)/shard_map/dot_general | solution.py:168
  (144 shorter events, 51.7 us)
Async XLA Ops:
  7.2 2.8 copy-start
  7.2 160.2 %all-reduce.2.cloned.1.call-start = ((), (), s32[]{:S(2)}) async-start(), calls=%async_computation.2 | async-start | bytes 3145728 | tf_op jit(solution)/shard_map/psum | solution.py:140
  10.0 25.8 %copy-start.3 = (bf16[512,1536]{1,0:T(8,128)(2,1)S(1)}, bf16[512,1536]{1,0:T(8,128)(2,1)}, u32[]{:S(2)}) copy-start(bf16[512,1536]{1,0:T(8,128)(2,1)} %param.13) | copy-start | bytes 4718596
  10.0 25.8 %copy-start.14 = (f32[1536]{0:T(1024)S(1)}, f32[1536]{0:T(1024)}, u32[]{:S(2)}) copy-start(f32[1536]{0:T(1024)} %param.15) | copy-start | bytes 18436
  12.5 25.5 %copy-start.8 = (bf16[1,192,1536]{2,1,0:T(8,128)(2,1)S(1)}, bf16[1,192,1536]{2,1,0:T(8,128)(2,1)}, u32[]{:S(2)}) copy-start(bf16[1,192,1536]{2,1,0:T(8,128)(2,1)} %param.22) | copy-start | bytes 1769476
  13.4 26.0 %collective-permute-start.2 = (bf16[528,256]{1,0:T(8,128)(2,1)S(1)}, bf16[528,256]{1,0:T(8,128)(2,1)}, u32[]{:S(2)}, u32[]{:S(2)}) collective-permute-start(bf16[528,256]{1,0:T(8,128)(2,1)S(1)} %maximum_maximum_fusion), channel_id=1, source_target_pairs={{0,12},{4,16},{8,20},{12,24},{16,28},{20,32},{24,36},{28,40},{32,4... | collective-permute-start | bytes 811016 | tf_op jit(solution)/shard_map/ppermute | solution.py:18
  19.1 24.6 %collective-permute-start.3 = (bf16[528,256]{1,0:T(8,128)(2,1)S(1)}, bf16[528,256]{1,0:T(8,128)(2,1)}, u32[]{:S(2)}, u32[]{:S(2)}) collective-permute-start(bf16[528,256]{1,0:T(8,128)(2,1)S(1)} %maximum_maximum_fusion), channel_id=1, source_target_pairs={{0,16},{4,20},{8,24},{12,28},{16,32},{20,36},{24,40},{28,44},{32,4... | collective-permute-start | bytes 811016 | tf_op jit(solution)/shard_map/ppermute | solution.py:18
  23.5 23.5 %collective-permute-start.4 = (bf16[528,256]{1,0:T(8,128)(2,1)S(1)}, bf16[528,256]{1,0:T(8,128)(2,1)}, u32[]{:S(2)}, u32[]{:S(2)}) collective-permute-start(bf16[528,256]{1,0:T(8,128)(2,1)S(1)} %maximum_maximum_fusion), channel_id=1, source_target_pairs={{0,20},{4,24},{8,28},{12,32},{16,36},{20,40},{24,44},{28,48},{32,5... | collective-permute-start | bytes 811016 | tf_op jit(solution)/shard_map/ppermute | solution.py:18
  28.7 20.3 %collective-permute-start.5 = (bf16[528,256]{1,0:T(8,128)(2,1)S(1)}, bf16[528,256]{1,0:T(8,128)(2,1)}, u32[]{:S(2)}, u32[]{:S(2)}) collective-permute-start(bf16[528,256]{1,0:T(8,128)(2,1)S(1)} %maximum_maximum_fusion), channel_id=1, source_target_pairs={{0,24},{4,28},{8,32},{12,36},{16,40},{20,44},{24,48},{28,52},{32,5... | collective-permute-start | bytes 811016 | tf_op jit(solution)/shard_map/ppermute | solution.py:18
  32.8 19.5 %collective-permute-start.6 = (bf16[528,256]{1,0:T(8,128)(2,1)S(1)}, bf16[528,256]{1,0:T(8,128)(2,1)}, u32[]{:S(2)}, u32[]{:S(2)}) collective-permute-start(bf16[528,256]{1,0:T(8,128)(2,1)S(1)} %maximum_maximum_fusion), channel_id=1, source_target_pairs={{0,28},{4,32},{8,36},{12,40},{16,44},{20,48},{24,52},{28,56},{32,6... | collective-permute-start | bytes 811016 | tf_op jit(solution)/shard_map/ppermute | solution.py:18
  35.8 32.1 %copy-start.12 = (s32[512]{0:T(512)S(1)}, s32[512]{0:T(512)}, u32[]{:S(2)}) copy-start(s32[512]{0:T(512)} %param.14) | copy-start | bytes 6148
  39.4 16.4 %collective-permute-start = (bf16[528,256]{1,0:T(8,128)(2,1)S(1)}, bf16[528,256]{1,0:T(8,128)(2,1)S(1)}, u32[]{:S(2)}, u32[]{:S(2)}) collective-permute-start(bf16[528,256]{1,0:T(8,128)(2,1)S(1)} %maximum_maximum_fusion), channel_id=1, source_target_pairs={{0,4},{4,8},{8,12},{12,16},{16,20},{20,24},{24,28},{28,32},{32,36}... | collective-permute-start | bytes 811016 | tf_op jit(solution)/shard_map/ppermute | solution.py:18
  43.7 12.9 %collective-permute-start.1 = (bf16[528,256]{1,0:T(8,128)(2,1)S(1)}, bf16[528,256]{1,0:T(8,128)(2,1)S(1)}, u32[]{:S(2)}, u32[]{:S(2)}) collective-permute-start(bf16[528,256]{1,0:T(8,128)(2,1)S(1)} %maximum_maximum_fusion), channel_id=1, source_target_pairs={{0,8},{4,12},{8,16},{12,20},{16,24},{20,28},{24,32},{28,36},{32,40... | collective-permute-start | bytes 811016 | tf_op jit(solution)/shard_map/ppermute | solution.py:18
  46.9 20.9 %collective-permute-start.7 = (bf16[528,256]{1,0:T(8,128)(2,1)S(1)}, bf16[528,256]{1,0:T(8,128)(2,1)S(1)}, u32[]{:S(2)}, u32[]{:S(2)}) collective-permute-start(bf16[528,256]{1,0:T(8,128)(2,1)S(1)} %maximum_maximum_fusion), channel_id=1, source_target_pairs={{0,32},{4,36},{8,40},{12,44},{16,48},{20,52},{24,56},{28,60},{32,6... | collective-permute-start | bytes 811016 | tf_op jit(solution)/shard_map/ppermute | solution.py:18
  48.9 56.6 %collective-permute-start.10 = (bf16[1536,576]{0,1:T(8,128)(2,1)S(1)}, bf16[1536,576]{0,1:T(8,128)(2,1)}, u32[]{:S(2)}, u32[]{:S(2)}) collective-permute-start(bf16[1536,576]{0,1:T(8,128)(2,1)S(1)} %pad_maximum_fusion), channel_id=1, source_target_pairs={{0,3},{1,0},{2,1},{3,2},{4,7},{5,4},{6,5},{7,6},{8,11},{9,8},{10,9... | collective-permute-start | bytes 5308424 | tf_op jit(solution)/shard_map/ppermute | solution.py:113
  52.3 53.2 %collective-permute-start.8 = (bf16[1536,576]{0,1:T(8,128)(2,1)S(1)}, bf16[1536,576]{0,1:T(8,128)(2,1)}, u32[]{:S(2)}, u32[]{:S(2)}) collective-permute-start(bf16[1536,576]{0,1:T(8,128)(2,1)S(1)} %pad_maximum_fusion), channel_id=1, source_target_pairs={{0,1},{1,2},{2,3},{3,0},{4,5},{5,6},{6,7},{7,4},{8,9},{9,10},{10,1... | collective-permute-start | bytes 5308424 | tf_op jit(solution)/shard_map/ppermute | solution.py:113
  55.8 89.8 %collective-permute-start.9 = (bf16[1536,576]{0,1:T(8,128)(2,1)S(1)}, bf16[1536,576]{0,1:T(8,128)(2,1)}, u32[]{:S(2)}, u32[]{:S(2)}) collective-permute-start(bf16[1536,576]{0,1:T(8,128)(2,1)S(1)} %pad_maximum_fusion), channel_id=1, source_target_pairs={{0,2},{1,3},{2,0},{3,1},{4,6},{5,7},{6,4},{7,5},{8,10},{9,11},{10,... | collective-permute-start | bytes 5308424 | tf_op jit(solution)/shard_map/ppermute | solution.py:113
  101.2 2.2 copy-start.11
  101.2 66.2 %copy-start.4 = (bf16[512,1536]{1,0:T(8,128)(2,1)S(1)}, bf16[512,1536]{1,0:T(8,128)(2,1)}, u32[]{:S(2)}) copy-start(bf16[512,1536]{1,0:T(8,128)(2,1)} %param.13) | copy-start | bytes 4718596
  105.5 65.6 %copy-start.15 = (f32[1536]{0:T(1024)S(1)}, f32[1536]{0:T(1024)}, u32[]{:S(2)}) copy-start(f32[1536]{0:T(1024)} %param.19) | copy-start | bytes 18436
  167.4 3.7 %copy-start.5 = (bf16[512,1536]{1,0:T(8,128)(2,1)S(1)}, bf16[512,1536]{1,0:T(8,128)(2,1)}, u32[]{:S(2)}) copy-start(bf16[512,1536]{1,0:T(8,128)(2,1)} %all-reduce.2.cloned.1.call-done) | copy-start | bytes 4718596
  167.4 3.7 %copy-start.7 = (bf16[512,640]{1,0:T(8,128)(2,1)S(1)}, bf16[512,640]{1,0:T(8,128)(2,1)}, u32[]{:S(2)}) copy-start(bf16[512,640]{1,0:T(8,128)(2,1)} %fusion.4) | copy-start | bytes 1966084
  177.8 39.7 %all-to-all-start = ((bf16[32,20,1536]{2,1,0:T(8,128)(2,1)}), bf16[32,20,1536]{2,1,0:T(8,128)(2,1)}, u32[]{:S(2)}, u32[]{:S(2)}) async-start(bf16[32,20,1536]{2,1,0:T(8,128)(2,1)} %all_to_all.16), calls=%async_computation | async-start | bytes 4718592 | tf_op jit(solution)/shard_map/all_to_all | solution.py:147
  237.6 8.3 %copy-start.16 = (s32[4]{0:T(128)S(1)}, s32[4]{0:T(128)}, u32[]{:S(2)}) copy-start(s32[4]{0:T(128)} %param.25) | copy-start | bytes 52
  237.6 8.3 %copy-start.10 = (bf16[512,128]{1,0:T(8,128)(2,1)S(1)}, bf16[512,128]{1,0:T(8,128)(2,1)}, u32[]{:S(2)}) copy-start(bf16[512,128]{1,0:T(8,128)(2,1)} %get-tuple-element.45) | copy-start | bytes 393220
  237.6 9.0 %copy-start.13 = (f32[512,4]{0,1:T(4,128)S(1)}, f32[512,4]{0,1:T(4,128)}, u32[]{:S(2)}) copy-start(f32[512,4]{0,1:T(4,128)} %param.24) | copy-start | bytes 24580
  237.6 40.7 %all-to-all-start.1 = ((bf16[128,20,384]{2,1,0:T(8,128)(2,1)}), bf16[128,20,384]{2,1,0:T(8,128)(2,1)}, u32[]{:S(2)}, u32[]{:S(2)}) async-start(bf16[128,20,384]{2,1,0:T(8,128)(2,1)} %bitcast.140), calls=%async_computation.1 | async-start | bytes 4718592 | tf_op jit(solution)/shard_map/all_to_all | solution.py:161
  246.6 35.7 %copy-start.9 = (bf16[4,128,128]{2,1,0:T(8,128)(2,1)}, bf16[4,128,128]{2,1,0:T(8,128)(2,1)S(1)}, u32[]{:S(2)}) copy-start(bf16[4,128,128]{2,1,0:T(8,128)(2,1)S(1)} %scatter_fusion) | copy-start | bytes 393220
  278.3 10.3 %slice-start = ((s8[5242880]{0:T(1024)(128)(4,1)}), s8[1048576]{0:T(1024)(128)(4,1)S(1)}, s32[]{:S(2)}) async-start(s8[5242880]{0:T(1024)(128)(4,1)} %bitcast.129), calls=%async_computation.3 | async-start | bytes 2097152
  282.4 6.3 %slice-start.1 = ((s8[5242880]{0:T(1024)(128)(4,1)}), s8[4194304]{0:T(1024)(128)(4,1)S(1)}, s32[]{:S(2)}) async-start(s8[5242880]{0:T(1024)(128)(4,1)} %bitcast.129), calls=%async_computation.4 | async-start | bytes 8388608
  282.4 6.4 %copy-start.2 = (bf16[2560,384]{1,0:T(8,128)(2,1)S(1)}, bf16[2560,384]{1,0:T(8,128)(2,1)}, u32[]{:S(2)}) copy-start(bf16[2560,384]{1,0:T(8,128)(2,1)} %all_to_all.21) | copy-start | bytes 5898244
  288.6 3.7 %copy-start.1 = (bf16[1536,512]{1,0:T(8,128)(2,1)S(1)}, bf16[1536,512]{1,0:T(8,128)(2,1)}, u32[]{:S(2)}) copy-start(bf16[1536,512]{1,0:T(8,128)(2,1)} %param.17) | copy-start | bytes 4718596
  (1 other events, 1.4 us)
Sparse Core Ops, SparseCore 0:
  103.6 63.7 all-reduce.1

commit v5 on v4

--- a/solution.py
+++ b/solution.py
@@ -109,10 +109,9 @@
     attended = (state[2] / state[1][:, :, None]).astype(jnp.bfloat16).reshape(count, heads * HD)
     hidden_part = w_gate.shape[2]
     packed = jnp.concatenate([w_gate[0], w_up[0], w_down[0].T], axis=1)
-    weight_parts = [packed] + [
-        lax.ppermute(packed, "tp", [(source, (source + number) % tp_count) for source in range(tp_count)])
-        for number in range(1, tp_count)
-    ]
+    across = lax.ppermute(packed, "tp", [(source, source ^ 2) for source in range(tp_count)])
+    sibling = [(source, source ^ 1) for source in range(tp_count)]
+    weight_parts = [packed, across, lax.ppermute(packed, "tp", sibling), lax.ppermute(across, "tp", sibling)]
     projected = jnp.dot(attended, w_out, preferred_element_type=jnp.float32)
     experts = lax.axis_size("seq") * w_gate.shape[0]
     choose = expert_picks.shape[1]

time: 305 us -> 294 us (0.964)
  waiting for transfers between devices: 122 us -> 111 us
    ppermute x3, waiting for transfers between devices: 40.2 us -> 0.01 us  [the longest x1 0.01 us: per_device(): lax.ppermute(packed, 'tp', [(source, source ^ 2) for source in range(tp_c...]
    psum x1, waiting for transfers between devices: 21.7 us -> 49.7 us  [per_device(): summed = lax.psum(projected.astype(jnp.bfloat16), 'tp')]
  transfers between devices with their start and end apart: 14 -> 14, of which waited for: 5 -> 4; matrix products, arithmetic and copies ran while one was open for 20% -> 21% of each run, Pallas kernels for 0% -> 0%
where the time goes in v5:
time: 294 us; the launch traced here: 288 us
  waiting for transfers between devices  111 us (38%)
  matrix products  55.2 us (19%)
  starting transfers between devices  51.7 us (18%)
  other arithmetic  28.7 us (10%)
  local copies, waits for them, and re-layouts  26.4 us (9%)
  between operations  15.1 us (5%)
    psum x1, waiting for transfers between devices, per_device(): summed = lax.psum(projected.astype(jnp.bfloat16), 'tp')  49.7 us
    ppermute x8, starting transfers between devices, shifted(): lax.ppermute(value, axis, [(source, source + steps) for source in range(l...  29.6 us
    all_to_all x1, waiting for transfers between devices, per_device(): lax.all_to_all(outgoing, ('seq', 'tp'), split_axis=0, concat_axis=0, tile...  26.2 us
    all_to_all x1, waiting for transfers between devices, per_device(): lax.all_to_all(rows, 'seq', split_axis=0, concat_axis=0, tiled=True)  23.4 us
    dot_general x9, matrix products, attend_block(): jnp.einsum('qhk,kd->qhd', weights.astype(jnp.bfloat16), value_block, pref...  12.3 us
    ppermute x8, waiting for transfers between devices, shifted(): lax.ppermute(value, axis, [(source, source + steps) for source in range(l...  11.5 us
    dot_general x9, matrix products, attend_block(): jnp.einsum('qhd,kd->qhk', queries, key_block, preferred_element_type=jnp....  10.9 us
    slice x4, local copies, waits for them, and re-layouts, per_device(): part[:, hidden_part:2 * hidden_part]  9.01 us
  transfers between devices with their start and end apart: 14, of which 4 were waited for; matrix products, arithmetic and copies ran while one was open for 21% of the time, Pallas kernels for 0%

profile of v5, /device:TPU:1, one launch (start us, length us, event | category | flops | bytes accessed | tf_op | source)
XLA Modules:
  0.0 287.9 jit_solution(1107882306562472569)
XLA Ops:
  10.0 2.6 convolution_convert_fusion.3
  13.4 5.7 %collective-permute-start.2 = (bf16[528,256]{1,0:T(8,128)(2,1)S(1)}, bf16[528,256]{1,0:T(8,128)(2,1)}, u32[]{:S(2)}, u32[]{:S(2)}) collective-permute-start(bf16[528,256]{1,0:T(8,128)(2,1)S(1)} %maximum_maximum_fusion), channel_id=1, source_target_pairs={{0,12},{4,16},{8,20},{12,24},{16,28},{20,32},{24,36},{28,40},{32,4... | collective-permute-start | bytes 811016 | tf_op jit(solution)/shard_map/ppermute | solution.py:18
  19.1 4.4 %collective-permute-start.3 = (bf16[528,256]{1,0:T(8,128)(2,1)S(1)}, bf16[528,256]{1,0:T(8,128)(2,1)}, u32[]{:S(2)}, u32[]{:S(2)}) collective-permute-start(bf16[528,256]{1,0:T(8,128)(2,1)S(1)} %maximum_maximum_fusion), channel_id=1, source_target_pairs={{0,16},{4,20},{8,24},{12,28},{16,32},{20,36},{24,40},{28,44},{32,4... | collective-permute-start | bytes 811016 | tf_op jit(solution)/shard_map/ppermute | solution.py:18
  23.5 5.2 %collective-permute-start.4 = (bf16[528,256]{1,0:T(8,128)(2,1)S(1)}, bf16[528,256]{1,0:T(8,128)(2,1)}, u32[]{:S(2)}, u32[]{:S(2)}) collective-permute-start(bf16[528,256]{1,0:T(8,128)(2,1)S(1)} %maximum_maximum_fusion), channel_id=1, source_target_pairs={{0,20},{4,24},{8,28},{12,32},{16,36},{20,40},{24,44},{28,48},{32,5... | collective-permute-start | bytes 811016 | tf_op jit(solution)/shard_map/ppermute | solution.py:18
  28.7 4.1 %collective-permute-start.5 = (bf16[528,256]{1,0:T(8,128)(2,1)S(1)}, bf16[528,256]{1,0:T(8,128)(2,1)}, u32[]{:S(2)}, u32[]{:S(2)}) collective-permute-start(bf16[528,256]{1,0:T(8,128)(2,1)S(1)} %maximum_maximum_fusion), channel_id=1, source_target_pairs={{0,24},{4,28},{8,32},{12,36},{16,40},{20,44},{24,48},{28,52},{32,5... | collective-permute-start | bytes 811016 | tf_op jit(solution)/shard_map/ppermute | solution.py:18
  32.8 2.8 collective-permute-start.6
  35.9 2.2 convolution_convert_fusion.4
  39.4 3.6 %collective-permute-start = (bf16[528,256]{1,0:T(8,128)(2,1)S(1)}, bf16[528,256]{1,0:T(8,128)(2,1)S(1)}, u32[]{:S(2)}, u32[]{:S(2)}) collective-permute-start(bf16[528,256]{1,0:T(8,128)(2,1)S(1)} %maximum_maximum_fusion), channel_id=1, source_target_pairs={{0,4},{4,8},{8,12},{12,16},{16,20},{20,24},{24,28},{28,32},{32,36}... | collective-permute-start | bytes 811016 | tf_op jit(solution)/shard_map/ppermute | solution.py:18
  43.8 2.5 collective-permute-start.1
  49.0 3.0 %collective-permute-start.8 = (bf16[1536,576]{0,1:T(8,128)(2,1)S(1)}, bf16[1536,576]{0,1:T(8,128)(2,1)}, u32[]{:S(2)}, u32[]{:S(2)}) collective-permute-start(bf16[1536,576]{0,1:T(8,128)(2,1)S(1)} %pad_maximum_fusion), channel_id=1, source_target_pairs={{0,2},{1,3},{2,0},{3,1},{4,6},{5,7},{6,4},{7,5},{8,10},{9,11},{10,... | collective-permute-start | bytes 5308424 | tf_op jit(solution)/shard_map/ppermute | solution.py:112
  52.7 2.9 %collective-permute-start.9 = (bf16[1536,576]{0,1:T(8,128)(2,1)S(1)}, bf16[1536,576]{0,1:T(8,128)(2,1)}, u32[]{:S(2)}, u32[]{:S(2)}) collective-permute-start(bf16[1536,576]{0,1:T(8,128)(2,1)S(1)} %pad_maximum_fusion), channel_id=1, source_target_pairs={{0,1},{1,0},{2,3},{3,2},{4,5},{5,4},{6,7},{7,6},{8,9},{9,8},{10,11... | collective-permute-start | bytes 5308424 | tf_op jit(solution)/shard_map/ppermute | solution.py:114
  56.4 11.4 %collective-permute-done.7 = bf16[528,256]{1,0:T(8,128)(2,1)S(1)} collective-permute-done((bf16[528,256]{1,0:T(8,128)(2,1)S(1)}, bf16[528,256]{1,0:T(8,128)(2,1)S(1)}, u32[]{:S(2)}, u32[]{:S(2)}) %collective-permute-start.7) | collective-permute-done | bytes 270368 | tf_op jit(solution)/shard_map/ppermute | solution.py:18
  101.8 2.2 convolution_convert_fusion.2
  106.1 49.7 %all-reduce.2.cloned.1.call-done = bf16[512,1536]{1,0:T(8,128)(2,1)} async-done(((bf16[512,1536]{1,0:T(8,128)(2,1)}), bf16[512,1536]{1,0:T(8,128)(2,1)}) %all-reduce.2.cloned.1.call-update) | async-done | bytes 1572880 | tf_op jit(solution)/shard_map/psum | solution.py:139
  155.8 3.7 %convert_add_fusion = (f32[512,1536]{1,0:T(8,128)}, f32[512]{0:T(512)S(1)}) fusion(bf16[512,1536]{1,0:T(8,128)(2,1)S(1)} %copy-done.4, bf16[512,1536]{1,0:T(8,128)(2,1)} %all-reduce.2.cloned.1.call-done), kind=kLoop, calls=%fused_computation.6 | loop fusion | flops 3931648 | bytes 6293504 | tf_op jit(solution)/shard_map/add | solution.py:142
  159.6 2.8 convolution_convert_fusion.1
  162.3 3.9 %all_to_all.16 = bf16[32,20,1536]{2,1,0:T(8,128)(2,1)} reshape(bf16[640,1536]{1,0:T(8,128)(2,1)} %convolution_convert_fusion.1) | data formatting | bytes 3932160 | tf_op jit(solution)/shard_map/all_to_all | solution.py:146
  166.3 7.3 %all-to-all-start = ((bf16[32,20,1536]{2,1,0:T(8,128)(2,1)}), bf16[32,20,1536]{2,1,0:T(8,128)(2,1)}, u32[]{:S(2)}, u32[]{:S(2)}) async-start(bf16[32,20,1536]{2,1,0:T(8,128)(2,1)} %all_to_all.16), calls=%async_computation | async-start | bytes 4718592 | tf_op jit(solution)/shard_map/all_to_all | solution.py:146
  174.5 2.8 fusion.226
  177.3 2.7 fusion.227
  180.0 2.6 fusion.228
  182.6 23.4 %all-to-all-done = bf16[32,20,1536]{2,1,0:T(8,128)(2,1)} async-done(((bf16[32,20,1536]{2,1,0:T(8,128)(2,1)}), bf16[32,20,1536]{2,1,0:T(8,128)(2,1)}, u32[]{:S(2)}, u32[]{:S(2)}) %all-to-all-start) | async-done | bytes 1966112 | tf_op jit(solution)/shard_map/all_to_all | solution.py:146
  206.0 2.6 all_to_all.18
  208.5 4.6 %fusion.24 = f32[640,768]{1,0:T(8,128)} fusion(bf16[640,1536]{1,0:T(8,128)(2,1)S(1)} %all_to_all.18, bf16[1536,192]{0,1:T(8,128)(2,1)} %get-tuple-element.44, bf16[1536,192]{0,1:T(8,128)(2,1)} %get-tuple-element.41, bf16[1536,192]{0,1:T(8,128)(2,1)} %get-tuple-element.38, bf16[1536,192]{0,1:T(8,128)(2,1)} %get-tuple-element.35), kind=kOutput, calls=%fused_computation.55 | convolution fusion | flops 1519386624 | bytes 6291456 | tf_op jit(solution)/shard_map/dot_general | solution.py:150
  213.1 7.7 %convolution_convert_fusion = bf16[640,1536]{1,0:T(8,128)(2,1)} fusion(bf16[1536,192]{0,1:T(8,128)(2,1)} %get-tuple-element.43, bf16[1536,192]{0,1:T(8,128)(2,1)} %get-tuple-element.40, bf16[1536,192]{0,1:T(8,128)(2,1)} %get-tuple-element.37, bf16[1536,192]{0,1:T(8,128)(2,1)S(1)} %get-tuple-element.34, f32[640,768]{1,0:T(8,128)} %fusion.24, ...), kind=kOutput, calls=%fused_computation.9 | convolution fusion | flops 3041230848 | bytes 10616832 | tf_op jit(solution)/shard_map/dot_general | solution.py:153
  220.9 3.3 %reshape.975 = bf16[32,20,4,384]{3,2,1,0:T(4,128)(2,1)S(1)} reshape(bf16[640,1536]{1,0:T(8,128)(2,1)} %convolution_convert_fusion) | data formatting | bytes 3932160 | tf_op jit(solution)/shard_map/reshape | solution.py:156
  226.0 8.3 %all-to-all-start.1 = ((bf16[128,20,384]{2,1,0:T(8,128)(2,1)}), bf16[128,20,384]{2,1,0:T(8,128)(2,1)}, u32[]{:S(2)}, u32[]{:S(2)}) async-start(bf16[128,20,384]{2,1,0:T(8,128)(2,1)} %bitcast.140), calls=%async_computation.1 | async-start | bytes 4718592 | tf_op jit(solution)/shard_map/all_to_all | solution.py:160
  235.1 5.4 %select_reduce_fusion = f32[512,2560]{1,0:T(8,128)} fusion(f32[512,4]{0,1:T(4,128)S(1)} %copy-done.13, s32[512,4]{0,1:T(4,128)S(1)} %get-tuple-element.48), kind=kLoop, calls=%fused_computation.1 | loop fusion | flops 14417920 | bytes 5259264 | tf_op jit(solution)/shard_map/reduce_sum | solution.py:164
  240.5 26.2 %all-to-all-done.1 = bf16[128,20,384]{2,1,0:T(8,128)(2,1)} async-done(((bf16[128,20,384]{2,1,0:T(8,128)(2,1)}), bf16[128,20,384]{2,1,0:T(8,128)(2,1)}, u32[]{:S(2)}, u32[]{:S(2)}) %all-to-all-start.1) | async-done | bytes 1966112 | tf_op jit(solution)/shard_map/all_to_all | solution.py:160
  266.7 4.0 %all_to_all.21 = bf16[2560,384]{1,0:T(8,128)(2,1)} reshape(bf16[128,20,384]{2,1,0:T(8,128)(2,1)} %all-to-all-done.1) | data formatting | bytes 3932160 | tf_op jit(solution)/shard_map/all_to_all | solution.py:160
  270.8 6.3 %fusion.5 = f32[512,384]{1,0:T(8,128)S(1)} fusion(bf16[2560,384]{1,0:T(8,128)(2,1)} %all_to_all.21, f32[512,2560]{1,0:T(8,128)} %select_reduce_fusion), kind=kOutput, calls=%fused_computation.36 | convolution fusion | flops 1011875840 | bytes 7995392 | tf_op jit(solution)/shard_map/dot_general | solution.py:167
  277.2 3.6 %add_convert_fusion = bf16[512,384]{1,0:T(8,128)(2,1)} fusion(f32[512,1536]{1,0:T(8,128)} %get-tuple-element.31, s32[]{:T(128)S(6)} %select_n.128, f32[512,384]{1,0:T(8,128)S(1)} %fusion.5, bf16[2560,384]{1,0:T(8,128)(2,1)S(1)} %copy-done.2, f32[512,2560]{1,0:T(8,128)S(1)} %bitcast.130), kind=kOutput, calls=%fused_computation.163 | convolution fusion | flops 1008533504 | bytes 9175044 | tf_op jit(solution)/shard_map/dot_general | solution.py:167
  (144 shorter events, 49.4 us)
Async XLA Ops:
  7.2 2.8 copy-start
  7.2 148.6 %all-reduce.2.cloned.1.call-start = ((), (), s32[]{:S(2)}) async-start(), calls=%async_computation.2 | async-start | bytes 3145728 | tf_op jit(solution)/shard_map/psum | solution.py:139
  10.0 25.8 %copy-start.3 = (bf16[512,1536]{1,0:T(8,128)(2,1)S(1)}, bf16[512,1536]{1,0:T(8,128)(2,1)}, u32[]{:S(2)}) copy-start(bf16[512,1536]{1,0:T(8,128)(2,1)} %param.13) | copy-start | bytes 4718596
  10.0 25.8 %copy-start.14 = (f32[1536]{0:T(1024)S(1)}, f32[1536]{0:T(1024)}, u32[]{:S(2)}) copy-start(f32[1536]{0:T(1024)} %param.15) | copy-start | bytes 18436
  12.5 25.5 %copy-start.8 = (bf16[1,192,1536]{2,1,0:T(8,128)(2,1)S(1)}, bf16[1,192,1536]{2,1,0:T(8,128)(2,1)}, u32[]{:S(2)}) copy-start(bf16[1,192,1536]{2,1,0:T(8,128)(2,1)} %param.22) | copy-start | bytes 1769476
  13.4 26.0 %collective-permute-start.2 = (bf16[528,256]{1,0:T(8,128)(2,1)S(1)}, bf16[528,256]{1,0:T(8,128)(2,1)}, u32[]{:S(2)}, u32[]{:S(2)}) collective-permute-start(bf16[528,256]{1,0:T(8,128)(2,1)S(1)} %maximum_maximum_fusion), channel_id=1, source_target_pairs={{0,12},{4,16},{8,20},{12,24},{16,28},{20,32},{24,36},{28,40},{32,4... | collective-permute-start | bytes 811016 | tf_op jit(solution)/shard_map/ppermute | solution.py:18
  19.1 24.6 %collective-permute-start.3 = (bf16[528,256]{1,0:T(8,128)(2,1)S(1)}, bf16[528,256]{1,0:T(8,128)(2,1)}, u32[]{:S(2)}, u32[]{:S(2)}) collective-permute-start(bf16[528,256]{1,0:T(8,128)(2,1)S(1)} %maximum_maximum_fusion), channel_id=1, source_target_pairs={{0,16},{4,20},{8,24},{12,28},{16,32},{20,36},{24,40},{28,44},{32,4... | collective-permute-start | bytes 811016 | tf_op jit(solution)/shard_map/ppermute | solution.py:18
  23.5 23.5 %collective-permute-start.4 = (bf16[528,256]{1,0:T(8,128)(2,1)S(1)}, bf16[528,256]{1,0:T(8,128)(2,1)}, u32[]{:S(2)}, u32[]{:S(2)}) collective-permute-start(bf16[528,256]{1,0:T(8,128)(2,1)S(1)} %maximum_maximum_fusion), channel_id=1, source_target_pairs={{0,20},{4,24},{8,28},{12,32},{16,36},{20,40},{24,44},{28,48},{32,5... | collective-permute-start | bytes 811016 | tf_op jit(solution)/shard_map/ppermute | solution.py:18
  28.7 20.3 %collective-permute-start.5 = (bf16[528,256]{1,0:T(8,128)(2,1)S(1)}, bf16[528,256]{1,0:T(8,128)(2,1)}, u32[]{:S(2)}, u32[]{:S(2)}) collective-permute-start(bf16[528,256]{1,0:T(8,128)(2,1)S(1)} %maximum_maximum_fusion), channel_id=1, source_target_pairs={{0,24},{4,28},{8,32},{12,36},{16,40},{20,44},{24,48},{28,52},{32,5... | collective-permute-start | bytes 811016 | tf_op jit(solution)/shard_map/ppermute | solution.py:18
  32.8 19.8 %collective-permute-start.6 = (bf16[528,256]{1,0:T(8,128)(2,1)S(1)}, bf16[528,256]{1,0:T(8,128)(2,1)}, u32[]{:S(2)}, u32[]{:S(2)}) collective-permute-start(bf16[528,256]{1,0:T(8,128)(2,1)S(1)} %maximum_maximum_fusion), channel_id=1, source_target_pairs={{0,28},{4,32},{8,36},{12,40},{16,44},{20,48},{24,52},{28,56},{32,6... | collective-permute-start | bytes 811016 | tf_op jit(solution)/shard_map/ppermute | solution.py:18
  35.8 32.0 %copy-start.12 = (s32[512]{0:T(512)S(1)}, s32[512]{0:T(512)}, u32[]{:S(2)}) copy-start(s32[512]{0:T(512)} %param.14) | copy-start | bytes 6148
  39.4 16.8 %collective-permute-start = (bf16[528,256]{1,0:T(8,128)(2,1)S(1)}, bf16[528,256]{1,0:T(8,128)(2,1)S(1)}, u32[]{:S(2)}, u32[]{:S(2)}) collective-permute-start(bf16[528,256]{1,0:T(8,128)(2,1)S(1)} %maximum_maximum_fusion), channel_id=1, source_target_pairs={{0,4},{4,8},{8,12},{12,16},{16,20},{20,24},{24,28},{28,32},{32,36}... | collective-permute-start | bytes 811016 | tf_op jit(solution)/shard_map/ppermute | solution.py:18
  43.8 12.5 %collective-permute-start.1 = (bf16[528,256]{1,0:T(8,128)(2,1)S(1)}, bf16[528,256]{1,0:T(8,128)(2,1)S(1)}, u32[]{:S(2)}, u32[]{:S(2)}) collective-permute-start(bf16[528,256]{1,0:T(8,128)(2,1)S(1)} %maximum_maximum_fusion), channel_id=1, source_target_pairs={{0,8},{4,12},{8,16},{12,20},{16,24},{20,28},{24,32},{28,36},{32,40... | collective-permute-start | bytes 811016 | tf_op jit(solution)/shard_map/ppermute | solution.py:18
  47.0 20.9 %collective-permute-start.7 = (bf16[528,256]{1,0:T(8,128)(2,1)S(1)}, bf16[528,256]{1,0:T(8,128)(2,1)S(1)}, u32[]{:S(2)}, u32[]{:S(2)}) collective-permute-start(bf16[528,256]{1,0:T(8,128)(2,1)S(1)} %maximum_maximum_fusion), channel_id=1, source_target_pairs={{0,32},{4,36},{8,40},{12,44},{16,48},{20,52},{24,56},{28,60},{32,6... | collective-permute-start | bytes 811016 | tf_op jit(solution)/shard_map/ppermute | solution.py:18
  49.0 52.3 %collective-permute-start.8 = (bf16[1536,576]{0,1:T(8,128)(2,1)S(1)}, bf16[1536,576]{0,1:T(8,128)(2,1)}, u32[]{:S(2)}, u32[]{:S(2)}) collective-permute-start(bf16[1536,576]{0,1:T(8,128)(2,1)S(1)} %pad_maximum_fusion), channel_id=1, source_target_pairs={{0,2},{1,3},{2,0},{3,1},{4,6},{5,7},{6,4},{7,5},{8,10},{9,11},{10,... | collective-permute-start | bytes 5308424 | tf_op jit(solution)/shard_map/ppermute | solution.py:112
  52.7 53.5 %collective-permute-start.9 = (bf16[1536,576]{0,1:T(8,128)(2,1)S(1)}, bf16[1536,576]{0,1:T(8,128)(2,1)}, u32[]{:S(2)}, u32[]{:S(2)}) collective-permute-start(bf16[1536,576]{0,1:T(8,128)(2,1)S(1)} %pad_maximum_fusion), channel_id=1, source_target_pairs={{0,1},{1,0},{2,3},{3,2},{4,5},{5,4},{6,7},{7,6},{8,9},{9,8},{10,11... | collective-permute-start | bytes 5308424 | tf_op jit(solution)/shard_map/ppermute | solution.py:114
  101.2 2.8 copy-start.11
  101.2 54.6 %copy-start.4 = (bf16[512,1536]{1,0:T(8,128)(2,1)S(1)}, bf16[512,1536]{1,0:T(8,128)(2,1)}, u32[]{:S(2)}) copy-start(bf16[512,1536]{1,0:T(8,128)(2,1)} %param.13) | copy-start | bytes 4718596
  101.3 54.6 %collective-permute-start.10 = (bf16[1536,576]{0,1:T(8,128)(2,1)}, bf16[1536,576]{0,1:T(8,128)(2,1)}, u32[]{:S(2)}, u32[]{:S(2)}) collective-permute-start(bf16[1536,576]{0,1:T(8,128)(2,1)} %collective-permute-done.8), channel_id=1, source_target_pairs={{0,1},{1,0},{2,3},{3,2},{4,5},{5,4},{6,7},{7,6},{8,9},{9,8},{10,11... | collective-permute-start | bytes 5308424 | tf_op jit(solution)/shard_map/ppermute | solution.py:114
  106.1 53.5 %copy-start.15 = (f32[1536]{0:T(1024)S(1)}, f32[1536]{0:T(1024)}, u32[]{:S(2)}) copy-start(f32[1536]{0:T(1024)} %param.19) | copy-start | bytes 18436
  155.8 3.8 %copy-start.5 = (bf16[512,1536]{1,0:T(8,128)(2,1)S(1)}, bf16[512,1536]{1,0:T(8,128)(2,1)}, u32[]{:S(2)}) copy-start(bf16[512,1536]{1,0:T(8,128)(2,1)} %all-reduce.2.cloned.1.call-done) | copy-start | bytes 4718596
  155.8 3.8 %copy-start.7 = (bf16[512,640]{1,0:T(8,128)(2,1)S(1)}, bf16[512,640]{1,0:T(8,128)(2,1)}, u32[]{:S(2)}) copy-start(bf16[512,640]{1,0:T(8,128)(2,1)} %fusion.4) | copy-start | bytes 1966084
  166.3 39.7 %all-to-all-start = ((bf16[32,20,1536]{2,1,0:T(8,128)(2,1)}), bf16[32,20,1536]{2,1,0:T(8,128)(2,1)}, u32[]{:S(2)}, u32[]{:S(2)}) async-start(bf16[32,20,1536]{2,1,0:T(8,128)(2,1)} %all_to_all.16), calls=%async_computation | async-start | bytes 4718592 | tf_op jit(solution)/shard_map/all_to_all | solution.py:146
  226.0 8.3 %copy-start.16 = (s32[4]{0:T(128)S(1)}, s32[4]{0:T(128)}, u32[]{:S(2)}) copy-start(s32[4]{0:T(128)} %param.25) | copy-start | bytes 52
  226.0 8.4 %copy-start.10 = (bf16[512,128]{1,0:T(8,128)(2,1)S(1)}, bf16[512,128]{1,0:T(8,128)(2,1)}, u32[]{:S(2)}) copy-start(bf16[512,128]{1,0:T(8,128)(2,1)} %get-tuple-element.45) | copy-start | bytes 393220
  226.0 9.0 %copy-start.13 = (f32[512,4]{0,1:T(4,128)S(1)}, f32[512,4]{0,1:T(4,128)}, u32[]{:S(2)}) copy-start(f32[512,4]{0,1:T(4,128)} %param.24) | copy-start | bytes 24580
  226.0 40.7 %all-to-all-start.1 = ((bf16[128,20,384]{2,1,0:T(8,128)(2,1)}), bf16[128,20,384]{2,1,0:T(8,128)(2,1)}, u32[]{:S(2)}, u32[]{:S(2)}) async-start(bf16[128,20,384]{2,1,0:T(8,128)(2,1)} %bitcast.140), calls=%async_computation.1 | async-start | bytes 4718592 | tf_op jit(solution)/shard_map/all_to_all | solution.py:160
  235.0 35.7 %copy-start.9 = (bf16[4,128,128]{2,1,0:T(8,128)(2,1)}, bf16[4,128,128]{2,1,0:T(8,128)(2,1)S(1)}, u32[]{:S(2)}) copy-start(bf16[4,128,128]{2,1,0:T(8,128)(2,1)S(1)} %scatter_fusion) | copy-start | bytes 393220
  266.7 10.3 %slice-start = ((s8[5242880]{0:T(1024)(128)(4,1)}), s8[1048576]{0:T(1024)(128)(4,1)S(1)}, s32[]{:S(2)}) async-start(s8[5242880]{0:T(1024)(128)(4,1)} %bitcast.129), calls=%async_computation.3 | async-start | bytes 2097152
  270.8 6.3 %slice-start.1 = ((s8[5242880]{0:T(1024)(128)(4,1)}), s8[4194304]{0:T(1024)(128)(4,1)S(1)}, s32[]{:S(2)}) async-start(s8[5242880]{0:T(1024)(128)(4,1)} %bitcast.129), calls=%async_computation.4 | async-start | bytes 8388608
  270.8 6.4 %copy-start.2 = (bf16[2560,384]{1,0:T(8,128)(2,1)S(1)}, bf16[2560,384]{1,0:T(8,128)(2,1)}, u32[]{:S(2)}) copy-start(bf16[2560,384]{1,0:T(8,128)(2,1)} %all_to_all.21) | copy-start | bytes 5898244
  277.0 3.7 %copy-start.1 = (bf16[1536,512]{1,0:T(8,128)(2,1)S(1)}, bf16[1536,512]{1,0:T(8,128)(2,1)}, u32[]{:S(2)}) copy-start(bf16[1536,512]{1,0:T(8,128)(2,1)} %param.17) | copy-start | bytes 4718596
  (1 other events, 2.0 us)
Sparse Core Ops, SparseCore 0:
  104.1 51.6 all-reduce.1

commit v6 on v5

--- a/solution.py
+++ b/solution.py
@@ -87,32 +87,41 @@
     reach_steps = lax.axis_size("seq") // 4
     pieces = [own_piece] + [shifted(own_piece, "seq", number) for number in range(1, reach_steps + 1)]
 
-    def visit(carry, piece, number):
+    halves = 2
+    half = count // halves
+
+    def visit(carry, piece, number, rows):
         start = (seq_index - number) * count
         key_index = start + jnp.arange(count, dtype=jnp.int32)
         coded = piece[count : count + code_rows].reshape(2, count).astype(jnp.int32)
         segment_piece = coded[0] * 256 + coded[1]
         allowed = (
-            (segment_piece[None, :] == segment_ids[:, None])
-            & (key_index[None, :] <= query_index[:, None])
+            (segment_piece[None, :] == segment_ids[rows, None])
+            & (key_index[None, :] <= query_index[rows, None])
             & (key_index[None, :] >= 0)
         )
-        return attend_block(carry, query_heads, piece[:count, :HD], piece[:count, HD:], allowed)
-
-    state = (
-        jnp.full((count, heads), NEGATIVE, jnp.float32),
-        jnp.zeros((count, heads), jnp.float32),
-        jnp.zeros((count, heads, HD), jnp.float32),
-    )
-    for number, piece in enumerate(pieces):
-        state = visit(state, piece, number)
-    attended = (state[2] / state[1][:, :, None]).astype(jnp.bfloat16).reshape(count, heads * HD)
+        return attend_block(carry, query_heads[rows], piece[:count, :HD], piece[:count, HD:], allowed)
+
+    summed_parts = []
+    for part in range(halves):
+        rows = slice(part * half, (part + 1) * half)
+        state = (
+            jnp.full((half, heads), NEGATIVE, jnp.float32),
+            jnp.zeros((half, heads), jnp.float32),
+            jnp.zeros((half, heads, HD), jnp.float32),
+        )
+        for number, piece in enumerate(pieces):
+            state = visit(state, piece, number, rows)
+        attended = (state[2] / state[1][:, :, None]).astype(jnp.bfloat16).reshape(half, heads * HD)
+        projected = jnp.dot(attended, w_out, preferred_element_type=jnp.float32).astype(jnp.bfloat16)
+        if summed_parts:
+            summed_parts[-1], projected = lax.optimization_barrier((summed_parts[-1], projected))
+        summed_parts.append(lax.psum(projected, "tp"))
     hidden_part = w_gate.shape[2]
     packed = jnp.concatenate([w_gate[0], w_up[0], w_down[0].T], axis=1)
     across = lax.ppermute(packed, "tp", [(source, source ^ 2) for source in range(tp_count)])
     sibling = [(source, source ^ 1) for source in range(tp_count)]
     weight_parts = [packed, across, lax.ppermute(packed, "tp", sibling), lax.ppermute(across, "tp", sibling)]
-    projected = jnp.dot(attended, w_out, preferred_element_type=jnp.float32)
     experts = lax.axis_size("seq") * w_gate.shape[0]
     choose = expert_picks.shape[1]
     capacity = count * choose * 5 // (4 * experts)
@@ -136,7 +145,7 @@
         (mine_slot[:, :, None] == slot_range[None, None, :]).astype(jnp.bfloat16), axis=1
     ).T
     part_width = tokens.shape[1] // tp_count
-    summed = lax.psum(projected.astype(jnp.bfloat16), "tp")
+    summed = jnp.concatenate(summed_parts, axis=0)
     summed, weight_parts = lax.optimization_barrier((summed, weight_parts))
     summed = summed.astype(jnp.float32)
     residual = tokens.astype(jnp.float32) + summed

time: 294 us -> 332 us (1.13)
  matrix products: 55.2 us -> 68.1 us
  starting transfers between devices: 51.7 us -> 63.7 us
  waiting for transfers between devices: 111 us -> 117 us
  other arithmetic: 28.7 us -> 34.2 us
    psum x1 -> x2, waiting for transfers between devices: 49.7 us -> 68.5 us  [per_device(): summed_parts.append(lax.psum(projected, 'tp'))]
    ppermute x8, waiting for transfers between devices: 11.5 us -> 0.02 us  [shifted(): lax.ppermute(value, axis, [(source, source + steps) for source in range(l...]
    dot_general x9 -> x18, matrix products: 10.9 us -> 19.1 us  [attend_block(): jnp.einsum('qhd,kd->qhk', queries, key_block, preferred_element_type=jnp....]
    reduce_sum x5 -> x9, other arithmetic: 6.32 us -> 12.9 us  [attend_block(): total = total * factor + jnp.sum(weights, axis=2)]
    dot_general x9 -> x18, matrix products: 12.3 us -> 18.9 us  [attend_block(): jnp.einsum('qhk,kd->qhd', weights.astype(jnp.bfloat16), value_block, pref...]
    ppermute x1, starting transfers between devices: 2.92 us -> 9.4 us  [per_device(): lax.ppermute(packed, 'tp', sibling)]
    ppermute x1, starting transfers between devices: 0.58 us -> 6.49 us  [per_device(): lax.ppermute(across, 'tp', sibling)]
  transfers between devices with their start and end apart: 14 -> 15, of which waited for: 4 -> 4; matrix products, arithmetic and copies ran while one was open for 21% -> 26% of each run, Pallas kernels for 0% -> 0%
where the time goes in v6:
time: 332 us; the launch traced here: 326 us
  waiting for transfers between devices  117 us (35%)
  matrix products  68.1 us (21%)
  starting transfers between devices  63.7 us (19%)
  other arithmetic  34.2 us (10%)
  local copies, waits for them, and re-layouts  27.9 us (8%)
  between operations  15.8 us (5%)
    psum x2, waiting for transfers between devices, per_device(): summed_parts.append(lax.psum(projected, 'tp'))  68.5 us
    ppermute x8, starting transfers between devices, shifted(): lax.ppermute(value, axis, [(source, source + steps) for source in range(l...  29.3 us
    all_to_all x1, waiting for transfers between devices, per_device(): lax.all_to_all(outgoing, ('seq', 'tp'), split_axis=0, concat_axis=0, tile...  26.2 us
    all_to_all x1, waiting for transfers between devices, per_device(): lax.all_to_all(rows, 'seq', split_axis=0, concat_axis=0, tiled=True)  22 us
    dot_general x18, matrix products, attend_block(): jnp.einsum('qhd,kd->qhk', queries, key_block, preferred_element_type=jnp....  19.1 us
    dot_general x18, matrix products, attend_block(): jnp.einsum('qhk,kd->qhd', weights.astype(jnp.bfloat16), value_block, pref...  18.9 us
    reduce_sum x9, other arithmetic, attend_block(): total = total * factor + jnp.sum(weights, axis=2)  12.9 us
    slice x4, local copies, waits for them, and re-layouts, per_device(): part[:, hidden_part:2 * hidden_part]  10.4 us
  transfers between devices with their start and end apart: 15, of which 4 were waited for; matrix products, arithmetic and copies ran while one was open for 26% of the time, Pallas kernels for 0%

profile of v6, /device:TPU:1, one launch (start us, length us, event | category | flops | bytes accessed | tf_op | source)
XLA Modules:
  0.0 326.4 jit_solution(8011691452077508569)
XLA Ops:
  12.2 5.1 %collective-permute-start.7 = (bf16[528,256]{1,0:T(8,128)(2,1)}, bf16[528,256]{1,0:T(8,128)(2,1)}, u32[]{:S(2)}, u32[]{:S(2)}) collective-permute-start(bf16[528,256]{1,0:T(8,128)(2,1)} %maximum_maximum_fusion), channel_id=1, source_target_pairs={{0,32},{4,36},{8,40},{12,44},{16,48},{20,52},{24,56},{28,60},{32,6... | collective-permute-start | bytes 811016 | tf_op jit(solution)/shard_map/ppermute | solution.py:18
  17.2 5.4 %collective-permute-start.6 = (bf16[528,256]{1,0:T(8,128)(2,1)}, bf16[528,256]{1,0:T(8,128)(2,1)S(1)}, u32[]{:S(2)}, u32[]{:S(2)}) collective-permute-start(bf16[528,256]{1,0:T(8,128)(2,1)} %maximum_maximum_fusion), channel_id=1, source_target_pairs={{0,28},{4,32},{8,36},{12,40},{16,44},{20,48},{24,52},{28,56},{32,6... | collective-permute-start | bytes 811016 | tf_op jit(solution)/shard_map/ppermute | solution.py:18
  22.6 3.1 collective-permute-start.5
  25.8 3.1 collective-permute-start.4
  28.9 4.4 %collective-permute-start.3 = (bf16[528,256]{1,0:T(8,128)(2,1)}, bf16[528,256]{1,0:T(8,128)(2,1)S(1)}, u32[]{:S(2)}, u32[]{:S(2)}) collective-permute-start(bf16[528,256]{1,0:T(8,128)(2,1)} %maximum_maximum_fusion), channel_id=1, source_target_pairs={{0,16},{4,20},{8,24},{12,28},{16,32},{20,36},{24,40},{28,44},{32,4... | collective-permute-start | bytes 811016 | tf_op jit(solution)/shard_map/ppermute | solution.py:18
  35.6 2.3 convolution_convert_fusion.5
  41.3 3.5 %collective-permute-start.1 = (bf16[528,256]{1,0:T(8,128)(2,1)}, bf16[528,256]{1,0:T(8,128)(2,1)S(1)}, u32[]{:S(2)}, u32[]{:S(2)}) collective-permute-start(bf16[528,256]{1,0:T(8,128)(2,1)} %maximum_maximum_fusion), channel_id=1, source_target_pairs={{0,8},{4,12},{8,16},{12,20},{16,24},{20,28},{24,32},{28,36},{32,40... | collective-permute-start | bytes 811016 | tf_op jit(solution)/shard_map/ppermute | solution.py:18
  44.8 3.4 %collective-permute-start = (bf16[528,256]{1,0:T(8,128)(2,1)}, bf16[528,256]{1,0:T(8,128)(2,1)S(1)}, u32[]{:S(2)}, u32[]{:S(2)}) collective-permute-start(bf16[528,256]{1,0:T(8,128)(2,1)} %maximum_maximum_fusion), channel_id=1, source_target_pairs={{0,4},{4,8},{8,12},{12,16},{16,20},{20,24},{24,28},{28,32},{32,36}... | collective-permute-start | bytes 811016 | tf_op jit(solution)/shard_map/ppermute | solution.py:18
  48.3 9.4 %collective-permute-start.9 = (bf16[1536,576]{0,1:T(8,128)(2,1)}, bf16[1536,576]{0,1:T(8,128)(2,1)}, u32[]{:S(2)}, u32[]{:S(2)}) collective-permute-start(bf16[1536,576]{0,1:T(8,128)(2,1)} %pad_maximum_fusion), channel_id=1, source_target_pairs={{0,1},{1,0},{2,3},{3,2},{4,5},{5,4},{6,7},{7,6},{8,9},{9,8},{10,11... | collective-permute-start | bytes 5308424 | tf_op jit(solution)/shard_map/ppermute | solution.py:124
  57.7 2.7 collective-permute-start.8
  75.0 2.5 select_reduce_fusion.1
  99.1 2.6 fusion.60
  117.8 6.5 %collective-permute-start.10 = (bf16[1536,576]{0,1:T(8,128)(2,1)}, bf16[1536,576]{0,1:T(8,128)(2,1)}, u32[]{:S(2)}, u32[]{:S(2)}) collective-permute-start(bf16[1536,576]{0,1:T(8,128)(2,1)} %collective-permute-done.8), channel_id=1, source_target_pairs={{0,1},{1,0},{2,3},{3,2},{4,5},{5,4},{6,7},{7,6},{8,9},{9,8},{10,11... | collective-permute-start | bytes 5308424 | tf_op jit(solution)/shard_map/ppermute | solution.py:124
  127.5 24.8 %all-reduce.3.cloned.1.call-done = bf16[256,1536]{1,0:T(8,128)(2,1)} async-done(((bf16[256,1536]{1,0:T(8,128)(2,1)}), bf16[256,1536]{1,0:T(8,128)(2,1)}) %all-reduce.3.cloned.1.call-update) | async-done | bytes 786448 | tf_op jit(solution)/shard_map/psum | solution.py:119
  154.5 43.7 %all-reduce.5.cloned.1.call-done = bf16[256,1536]{1,0:T(8,128)(2,1)} async-done(((bf16[256,1536]{1,0:T(8,128)(2,1)}), bf16[256,1536]{1,0:T(8,128)(2,1)}) %all-reduce.5.cloned.1.call-update) | async-done | bytes 786448 | tf_op jit(solution)/shard_map/psum | solution.py:119
  199.5 2.2 convert_add_fusion
  205.1 7.1 %all-to-all-start = ((bf16[32,20,1536]{2,1,0:T(8,128)(2,1)}), bf16[32,20,1536]{2,1,0:T(8,128)(2,1)}, u32[]{:S(2)}, u32[]{:S(2)}) async-start(bf16[32,20,1536]{2,1,0:T(8,128)(2,1)} %all_to_all.16), calls=%async_computation | async-start | bytes 4718592 | tf_op jit(solution)/shard_map/all_to_all | solution.py:155
  212.2 2.4 fusion.248
  214.6 2.7 fusion.249
  217.3 2.7 fusion.250
  219.9 2.7 fusion.251
  222.6 22.0 %all-to-all-done = bf16[32,20,1536]{2,1,0:T(8,128)(2,1)} async-done(((bf16[32,20,1536]{2,1,0:T(8,128)(2,1)}), bf16[32,20,1536]{2,1,0:T(8,128)(2,1)}, u32[]{:S(2)}, u32[]{:S(2)}) %all-to-all-start) | async-done | bytes 1966112 | tf_op jit(solution)/shard_map/all_to_all | solution.py:155
  244.6 2.6 all_to_all.18
  247.2 4.6 %fusion.6 = f32[640,768]{1,0:T(8,128)} fusion(bf16[640,1536]{1,0:T(8,128)(2,1)S(1)} %all_to_all.18, bf16[1536,192]{0,1:T(8,128)(2,1)} %get-tuple-element.65, bf16[1536,192]{0,1:T(8,128)(2,1)} %get-tuple-element.62, bf16[1536,192]{0,1:T(8,128)(2,1)} %get-tuple-element.59, bf16[1536,192]{0,1:T(8,128)(2,1)} %get-tuple-element.56), kind=kOutput, calls=%fused_computation.20 | convolution fusion | flops 1519386624 | bytes 6291456 | tf_op jit(solution)/shard_map/dot_general | solution.py:159
  251.9 7.7 %convolution_convert_fusion = bf16[640,1536]{1,0:T(8,128)(2,1)} fusion(bf16[1536,192]{0,1:T(8,128)(2,1)} %get-tuple-element.64, bf16[1536,192]{0,1:T(8,128)(2,1)} %get-tuple-element.61, bf16[1536,192]{0,1:T(8,128)(2,1)} %get-tuple-element.58, bf16[1536,192]{0,1:T(8,128)(2,1)S(1)} %get-tuple-element.55, f32[640,768]{1,0:T(8,128)} %fusion.6, ...), kind=kOutput, calls=%fused_computation.9 | convolution fusion | flops 3041230848 | bytes 10616832 | tf_op jit(solution)/shard_map/dot_general | solution.py:162
  259.6 3.3 %reshape.1735 = bf16[32,20,4,384]{3,2,1,0:T(4,128)(2,1)S(1)} reshape(bf16[640,1536]{1,0:T(8,128)(2,1)} %convolution_convert_fusion) | data formatting | bytes 3932160 | tf_op jit(solution)/shard_map/reshape | solution.py:165
  264.7 8.2 %all-to-all-start.1 = ((bf16[128,20,384]{2,1,0:T(8,128)(2,1)}), bf16[128,20,384]{2,1,0:T(8,128)(2,1)}, u32[]{:S(2)}, u32[]{:S(2)}) async-start(bf16[128,20,384]{2,1,0:T(8,128)(2,1)} %bitcast.210), calls=%async_computation.1 | async-start | bytes 4718592 | tf_op jit(solution)/shard_map/all_to_all | solution.py:169
  273.7 5.4 %select_reduce_fusion = f32[512,2560]{1,0:T(8,128)} fusion(f32[512,4]{0,1:T(4,128)S(1)} %copy-done.60, s32[512,4]{0,1:T(4,128)S(1)} %get-tuple-element.71), kind=kLoop, calls=%fused_computation.1 | loop fusion | flops 14417920 | bytes 5259264 | tf_op jit(solution)/shard_map/reduce_sum | solution.py:173
  279.1 26.2 %all-to-all-done.1 = bf16[128,20,384]{2,1,0:T(8,128)(2,1)} async-done(((bf16[128,20,384]{2,1,0:T(8,128)(2,1)}), bf16[128,20,384]{2,1,0:T(8,128)(2,1)}, u32[]{:S(2)}, u32[]{:S(2)}) %all-to-all-start.1) | async-done | bytes 1966112 | tf_op jit(solution)/shard_map/all_to_all | solution.py:169
  305.3 4.0 %all_to_all.21 = bf16[2560,384]{1,0:T(8,128)(2,1)} reshape(bf16[128,20,384]{2,1,0:T(8,128)(2,1)} %all-to-all-done.1) | data formatting | bytes 3932160 | tf_op jit(solution)/shard_map/all_to_all | solution.py:169
  309.4 6.3 %fusion.5 = f32[512,384]{1,0:T(8,128)S(1)} fusion(bf16[2560,384]{1,0:T(8,128)(2,1)} %all_to_all.21, f32[512,2560]{1,0:T(8,128)} %select_reduce_fusion), kind=kOutput, calls=%fused_computation.17 | convolution fusion | flops 1011875840 | bytes 7995392 | tf_op jit(solution)/shard_map/dot_general | solution.py:176
  315.8 3.6 %add_convert_fusion = bf16[512,384]{1,0:T(8,128)(2,1)} fusion(f32[512,1536]{1,0:T(8,128)} %get-tuple-element.52, s32[]{:T(128)S(6)} %select_n.200, f32[512,384]{1,0:T(8,128)S(1)} %fusion.5, bf16[2560,384]{1,0:T(8,128)(2,1)S(1)} %copy-done.10, f32[512,2560]{1,0:T(8,128)S(1)} %bitcast.191), kind=kOutput, calls=%fused_computation.198 | convolution fusion | flops 1008533504 | bytes 9175044 | tf_op jit(solution)/shard_map/dot_general | solution.py:176
  (282 shorter events, 74.6 us)
Async XLA Ops:
  7.2 145.1 %all-reduce.3.cloned.1.call-start = ((), (), s32[]{:S(2)}) async-start(), calls=%async_computation.2 | async-start | bytes 1572864 | tf_op jit(solution)/shard_map/psum | solution.py:119
  11.3 24.2 %copy-start.47 = (bf16[512,128]{1,0:T(8,128)(2,1)}, bf16[512,128]{1,0:T(8,128)(2,1)S(1)}, u32[]{:S(2)}) copy-start(bf16[512,128]{1,0:T(8,128)(2,1)S(1)} %get-tuple-element.67) | copy-start | bytes 393220
  12.2 27.1 %collective-permute-start.7 = (bf16[528,256]{1,0:T(8,128)(2,1)}, bf16[528,256]{1,0:T(8,128)(2,1)}, u32[]{:S(2)}, u32[]{:S(2)}) collective-permute-start(bf16[528,256]{1,0:T(8,128)(2,1)} %maximum_maximum_fusion), channel_id=1, source_target_pairs={{0,32},{4,36},{8,40},{12,44},{16,48},{20,52},{24,56},{28,60},{32,6... | collective-permute-start | bytes 811016 | tf_op jit(solution)/shard_map/ppermute | solution.py:18
  17.2 24.1 %collective-permute-start.6 = (bf16[528,256]{1,0:T(8,128)(2,1)}, bf16[528,256]{1,0:T(8,128)(2,1)S(1)}, u32[]{:S(2)}, u32[]{:S(2)}) collective-permute-start(bf16[528,256]{1,0:T(8,128)(2,1)} %maximum_maximum_fusion), channel_id=1, source_target_pairs={{0,28},{4,32},{8,36},{12,40},{16,44},{20,48},{24,52},{28,56},{32,6... | collective-permute-start | bytes 811016 | tf_op jit(solution)/shard_map/ppermute | solution.py:18
  22.6 22.2 %collective-permute-start.5 = (bf16[528,256]{1,0:T(8,128)(2,1)}, bf16[528,256]{1,0:T(8,128)(2,1)S(1)}, u32[]{:S(2)}, u32[]{:S(2)}) collective-permute-start(bf16[528,256]{1,0:T(8,128)(2,1)} %maximum_maximum_fusion), channel_id=1, source_target_pairs={{0,24},{4,28},{8,32},{12,36},{16,40},{20,44},{24,48},{28,52},{32,5... | collective-permute-start | bytes 811016 | tf_op jit(solution)/shard_map/ppermute | solution.py:18
  25.8 22.5 %collective-permute-start.4 = (bf16[528,256]{1,0:T(8,128)(2,1)}, bf16[528,256]{1,0:T(8,128)(2,1)S(1)}, u32[]{:S(2)}, u32[]{:S(2)}) collective-permute-start(bf16[528,256]{1,0:T(8,128)(2,1)} %maximum_maximum_fusion), channel_id=1, source_target_pairs={{0,20},{4,24},{8,28},{12,32},{16,36},{20,40},{24,44},{28,48},{32,5... | collective-permute-start | bytes 811016 | tf_op jit(solution)/shard_map/ppermute | solution.py:18
  28.9 28.8 %collective-permute-start.3 = (bf16[528,256]{1,0:T(8,128)(2,1)}, bf16[528,256]{1,0:T(8,128)(2,1)S(1)}, u32[]{:S(2)}, u32[]{:S(2)}) collective-permute-start(bf16[528,256]{1,0:T(8,128)(2,1)} %maximum_maximum_fusion), channel_id=1, source_target_pairs={{0,16},{4,20},{8,24},{12,28},{16,32},{20,36},{24,40},{28,44},{32,4... | collective-permute-start | bytes 811016 | tf_op jit(solution)/shard_map/ppermute | solution.py:18
  39.3 21.1 %collective-permute-start.2 = (bf16[528,256]{1,0:T(8,128)(2,1)}, bf16[528,256]{1,0:T(8,128)(2,1)S(1)}, u32[]{:S(2)}, u32[]{:S(2)}) collective-permute-start(bf16[528,256]{1,0:T(8,128)(2,1)} %maximum_maximum_fusion), channel_id=1, source_target_pairs={{0,12},{4,16},{8,20},{12,24},{16,28},{20,32},{24,36},{28,40},{32,4... | collective-permute-start | bytes 811016 | tf_op jit(solution)/shard_map/ppermute | solution.py:18
  41.3 19.4 %copy-start.35 = (bf16[528,256]{1,0:T(8,128)(2,1)}, bf16[528,256]{1,0:T(8,128)(2,1)S(1)}, u32[]{:S(2)}) copy-start(bf16[528,256]{1,0:T(8,128)(2,1)S(1)} %collective-permute-done.6) | copy-start | bytes 811012
  41.3 19.2 %collective-permute-start.1 = (bf16[528,256]{1,0:T(8,128)(2,1)}, bf16[528,256]{1,0:T(8,128)(2,1)S(1)}, u32[]{:S(2)}, u32[]{:S(2)}) collective-permute-start(bf16[528,256]{1,0:T(8,128)(2,1)} %maximum_maximum_fusion), channel_id=1, source_target_pairs={{0,8},{4,12},{8,16},{12,20},{16,24},{20,28},{24,32},{28,36},{32,40... | collective-permute-start | bytes 811016 | tf_op jit(solution)/shard_map/ppermute | solution.py:18
  44.8 15.9 %copy-start.33 = (bf16[528,256]{1,0:T(8,128)(2,1)}, bf16[528,256]{1,0:T(8,128)(2,1)S(1)}, u32[]{:S(2)}) copy-start(bf16[528,256]{1,0:T(8,128)(2,1)S(1)} %collective-permute-done.5) | copy-start | bytes 811012
  44.8 15.8 %collective-permute-start = (bf16[528,256]{1,0:T(8,128)(2,1)}, bf16[528,256]{1,0:T(8,128)(2,1)S(1)}, u32[]{:S(2)}, u32[]{:S(2)}) collective-permute-start(bf16[528,256]{1,0:T(8,128)(2,1)} %maximum_maximum_fusion), channel_id=1, source_target_pairs={{0,4},{4,8},{8,12},{12,16},{16,20},{20,24},{24,28},{28,32},{32,36}... | collective-permute-start | bytes 811016 | tf_op jit(solution)/shard_map/ppermute | solution.py:18
  48.3 151.1 %collective-permute-start.9 = (bf16[1536,576]{0,1:T(8,128)(2,1)}, bf16[1536,576]{0,1:T(8,128)(2,1)}, u32[]{:S(2)}, u32[]{:S(2)}) collective-permute-start(bf16[1536,576]{0,1:T(8,128)(2,1)} %pad_maximum_fusion), channel_id=1, source_target_pairs={{0,1},{1,0},{2,3},{3,2},{4,5},{5,4},{6,7},{7,6},{8,9},{9,8},{10,11... | collective-permute-start | bytes 5308424 | tf_op jit(solution)/shard_map/ppermute | solution.py:124
  57.7 60.1 %collective-permute-start.8 = (bf16[1536,576]{0,1:T(8,128)(2,1)}, bf16[1536,576]{0,1:T(8,128)(2,1)}, u32[]{:S(2)}, u32[]{:S(2)}) collective-permute-start(bf16[1536,576]{0,1:T(8,128)(2,1)} %pad_maximum_fusion), channel_id=1, source_target_pairs={{0,2},{1,3},{2,0},{3,1},{4,6},{5,7},{6,4},{7,5},{8,10},{9,11},{10,... | collective-permute-start | bytes 5308424 | tf_op jit(solution)/shard_map/ppermute | solution.py:122
  60.4 32.7 %copy-start.39 = (bf16[528,256]{1,0:T(8,128)(2,1)}, bf16[528,256]{1,0:T(8,128)(2,1)S(1)}, u32[]{:S(2)}) copy-start(bf16[528,256]{1,0:T(8,128)(2,1)S(1)} %collective-permute-done.2) | copy-start | bytes 811012
  60.5 33.3 %copy-start.38 = (bf16[528,256]{1,0:T(8,128)(2,1)}, bf16[528,256]{1,0:T(8,128)(2,1)S(1)}, u32[]{:S(2)}) copy-start(bf16[528,256]{1,0:T(8,128)(2,1)S(1)} %collective-permute-done.1) | copy-start | bytes 811012
  60.6 35.2 %copy-start.37 = (bf16[528,256]{1,0:T(8,128)(2,1)}, bf16[528,256]{1,0:T(8,128)(2,1)S(1)}, u32[]{:S(2)}) copy-start(bf16[528,256]{1,0:T(8,128)(2,1)S(1)} %collective-permute-done) | copy-start | bytes 811012
  62.5 12.5 %copy-start.17 = (pred[256,512]{1,0:T(8,128)(4,1)}, pred[256,512]{1,0:T(8,128)(4,1)S(1)}, u32[]{:S(2)}) copy-start(pred[256,512]{1,0:T(8,128)(4,1)S(1)} %get-tuple-element.89) | copy-start | bytes 393220
  62.5 26.0 %copy-start.27 = (pred[256,512]{1,0:T(8,128)(4,1)}, pred[256,512]{1,0:T(8,128)(4,1)S(1)}, u32[]{:S(2)}) copy-start(pred[256,512]{1,0:T(8,128)(4,1)S(1)} %get-tuple-element.92) | copy-start | bytes 393220
  63.6 24.3 %copy-start.55 = (f32[256,3]{0,1:T(4,128)}, f32[256,3]{0,1:T(4,128)S(1)}, u32[]{:S(2)}) copy-start(f32[256,3]{0,1:T(4,128)S(1)} %get-tuple-element.149) | copy-start | bytes 9220
  63.6 24.9 %copy-start.13 = (f32[256,3,512]{2,0,1:T(8,128)}, f32[256,3,512]{2,0,1:T(8,128)S(1)}, u32[]{:S(2)}) copy-start(f32[256,3,512]{2,0,1:T(8,128)S(1)} %get-tuple-element.150) | copy-start | bytes 4718596
  64.7 16.5 %copy-start.25 = (pred[256,512]{1,0:T(8,128)(4,1)}, pred[256,512]{1,0:T(8,128)(4,1)S(1)}, u32[]{:S(2)}) copy-start(pred[256,512]{1,0:T(8,128)(4,1)S(1)} %get-tuple-element.87) | copy-start | bytes 393220
  64.7 18.1 %copy-start.19 = (pred[256,512]{1,0:T(8,128)(4,1)}, pred[256,512]{1,0:T(8,128)(4,1)S(1)}, u32[]{:S(2)}) copy-start(pred[256,512]{1,0:T(8,128)(4,1)S(1)} %get-tuple-element.100) | copy-start | bytes 393220
  64.7 19.9 %copy-start.21 = (pred[256,512]{1,0:T(8,128)(4,1)}, pred[256,512]{1,0:T(8,128)(4,1)S(1)}, u32[]{:S(2)}) copy-start(pred[256,512]{1,0:T(8,128)(4,1)S(1)} %get-tuple-element.102) | copy-start | bytes 393220
  64.8 21.5 %copy-start.23 = (pred[256,512]{1,0:T(8,128)(4,1)}, pred[256,512]{1,0:T(8,128)(4,1)S(1)}, u32[]{:S(2)}) copy-start(pred[256,512]{1,0:T(8,128)(4,1)S(1)} %get-tuple-element.104) | copy-start | bytes 393220
  98.6 99.6 %all-reduce.5.cloned.1.call-start = ((), (), s32[]{:S(2)}) async-start(), calls=%async_computation.3 | async-start | bytes 1572864 | tf_op jit(solution)/shard_map/psum | solution.py:119
  117.8 81.6 %collective-permute-start.10 = (bf16[1536,576]{0,1:T(8,128)(2,1)}, bf16[1536,576]{0,1:T(8,128)(2,1)}, u32[]{:S(2)}, u32[]{:S(2)}) collective-permute-start(bf16[1536,576]{0,1:T(8,128)(2,1)} %collective-permute-done.8), channel_id=1, source_target_pairs={{0,1},{1,0},{2,3},{3,2},{4,5},{5,4},{6,7},{7,6},{8,9},{9,8},{10,11... | collective-permute-start | bytes 5308424 | tf_op jit(solution)/shard_map/ppermute | solution.py:124
  126.0 26.4 %copy-start.50 = (s32[512,4]{0,1:T(4,128)S(1)}, s32[512,4]{0,1:T(4,128)}, u32[]{:S(2)}) copy-start(s32[512,4]{0,1:T(4,128)} %param.23) | copy-start | bytes 24580
  152.4 45.8 %copy-start.40 = (bf16[256,1536]{1,0:T(8,128)(2,1)S(1)}, bf16[256,1536]{1,0:T(8,128)(2,1)}, u32[]{:S(2)}) copy-start(bf16[256,1536]{1,0:T(8,128)(2,1)} %all-reduce.3.cloned.1.call-done) | copy-start | bytes 2359300
  154.5 44.9 %copy-start.12 = (bf16[512,1536]{1,0:T(8,128)(2,1)S(1)}, bf16[512,1536]{1,0:T(8,128)(2,1)}, u32[]{:S(2)}) copy-start(bf16[512,1536]{1,0:T(8,128)(2,1)} %param.13) | copy-start | bytes 4718596
  205.1 39.6 %all-to-all-start = ((bf16[32,20,1536]{2,1,0:T(8,128)(2,1)}), bf16[32,20,1536]{2,1,0:T(8,128)(2,1)}, u32[]{:S(2)}, u32[]{:S(2)}) async-start(bf16[32,20,1536]{2,1,0:T(8,128)(2,1)} %all_to_all.16), calls=%async_computation | async-start | bytes 4718592 | tf_op jit(solution)/shard_map/all_to_all | solution.py:155
  264.7 40.6 %all-to-all-start.1 = ((bf16[128,20,384]{2,1,0:T(8,128)(2,1)}), bf16[128,20,384]{2,1,0:T(8,128)(2,1)}, u32[]{:S(2)}, u32[]{:S(2)}) async-start(bf16[128,20,384]{2,1,0:T(8,128)(2,1)} %bitcast.210), calls=%async_computation.1 | async-start | bytes 4718592 | tf_op jit(solution)/shard_map/all_to_all | solution.py:169
  (55 other events, 153.0 us)
Sparse Core Ops, SparseCore 0:
  98.7 53.6 all-reduce.2
  154.9 43.2 all-reduce.4
